TPU v7x, 256 devices: a whole 4x4x8 slice. The times are simulated.
256 devices in a mesh: replica: 16 (over y_lo, x, core), fsdp: 16 (over z, y_hi).
Axes of the slice: x: 4, y: 4 (y_hi: 2, y_lo: 2; y = y_hi * 2 + y_lo), z: 8, core: 2. Of those that a mesh axis runs over, the one named last changes fastest.
Arguments:
- activations: bfloat16 [65536, 8192], P(('replica', 'fsdp')), may hold values from -6 to 6
- cotangent: bfloat16 [65536, 512], P(('replica', 'fsdp')), may hold values from -12288 to 12288
- labels: int32 [65536], P(('replica', 'fsdp')), may hold values from -1 to 128255, as said below
- local_weight: float32 [16, 8192, 512], P('replica', 'fsdp'), may hold values from -4.5 to 4.5
- first_moment: bfloat16 [16, 8192, 512], P('replica', 'fsdp'), may hold values from -1.75 to 1.75
- second_moment: bfloat16 [16, 8192, 512], P('replica', 'fsdp'), may hold values from 0.019897461 to 2
- anchor_weight: float32 [8192, 512], P('fsdp'), may hold values from -4 to 4
- outer_state: float32 [8192, 512], P('fsdp'), may hold values from -1.75 to 1.75
Outputs:
- input_grad: bfloat16 [65536, 8192], P(('replica', 'fsdp'))
- new_anchor: float32 [8192, 512], P('fsdp')
- new_state: float32 [8192, 512], P('fsdp')
- new_first: bfloat16 [16, 8192, 512], P('replica', 'fsdp')
- new_second: bfloat16 [16, 8192, 512], P('replica', 'fsdp')
Inputs may be any that keep to these rules, and one draw needn't show every extreme that they name: `labels`: each worker's tokens begin with a prompt of at least 512 tokens, labelled -1, and all later tokens carry ids of 0 to 128255; at least 512 of them do.
All inputs are finite; a program needn't handle non-finite values.
Results may differ from a plain program's by a relative error of at most 0.0059.
Values may be sent and summed in bfloat16 or wider, within the bound.
No kernel may reach another device: no remote copies, remote signals or barrier semaphores. Data moves between devices by JAX's collectives and lax.ppermute only.
A program may use at most 128 MiB of HBM per device.

v0:
```python
import jax
import jax.numpy as jnp
from jax import lax
from jax.sharding import PartitionSpec as P

D = 8192


norm_eps = 1e-05
beta_first = 0.9
beta_second = 0.95
adam_eps = 1e-08
weight_decay = 0.1
inner_rate = 0.1
outer_rate = 0.7
outer_momentum = 0.9


def contract_last(left, right):
    return lax.dot_general(
        left, right, (((1,), (1,)), ((), ())), preferred_element_type=jnp.float32
    )


def contract_first(left, right):
    return lax.dot_general(
        left, right, (((0,), (0,)), ((), ())), preferred_element_type=jnp.float32
    )


def per_device(
    activations,
    cotangent,
    labels,
    local_weight,
    first_moment,
    second_moment,
    anchor_weight,
    outer_state,
):
    width_scale = D ** (-0.5)
    weight_shard = local_weight[0]
    weight_low = weight_shard.astype(jnp.bfloat16)
    answer = (labels >= 0).astype(jnp.float32)
    values = activations.astype(jnp.float32)
    inverse = lax.rsqrt(jnp.mean(values * values, axis=1, keepdims=True) + norm_eps)
    normed = values * inverse
    normed_low = normed.astype(jnp.bfloat16)
    answers = lax.psum(jnp.sum(answer), "fsdp")
    scaled = (cotangent.astype(jnp.float32) * answer[:, None] / answers).astype(jnp.bfloat16)
    feature_grad = width_scale * contract_last(
        scaled, lax.all_gather(weight_low, "fsdp", axis=0, tiled=True)
    )
    projected = jnp.mean(feature_grad * normed, axis=1, keepdims=True)
    input_grad = (inverse * (feature_grad - normed * projected)).astype(jnp.bfloat16)
    gradient = lax.psum_scatter(
        (width_scale * contract_first(normed_low, scaled)).astype(jnp.bfloat16),
        "fsdp",
        scatter_dimension=0,
        tiled=True,
    ).astype(jnp.float32)
    first = beta_first * first_moment[0].astype(jnp.float32) + (1.0 - beta_first) * gradient
    second = (
        beta_second * second_moment[0].astype(jnp.float32)
        + (1.0 - beta_second) * gradient * gradient
    )
    stepped = weight_shard - inner_rate * (
        first / (jnp.sqrt(second) + adam_eps) + weight_decay * weight_shard
    )
    pseudo_grad = anchor_weight - stepped
    replicas = lax.axis_size("replica")
    average = lax.psum(pseudo_grad.astype(jnp.bfloat16), "replica").astype(jnp.float32) / replicas
    new_state = outer_momentum * outer_state + average
    new_anchor = anchor_weight - outer_rate * (average + outer_momentum * new_state)
    new_first = first.astype(jnp.bfloat16)[None]
    new_second = second.astype(jnp.bfloat16)[None]
    return (input_grad, new_anchor, new_state, new_first, new_second)


def solution(mesh):
    in_specs = (
        P(("replica", "fsdp"), None),
        P(("replica", "fsdp"), None),
        P(("replica", "fsdp")),
        P("replica", "fsdp", None),
        P("replica", "fsdp", None),
        P("replica", "fsdp", None),
        P("fsdp", None),
        P("fsdp", None),
    )
    out_specs = (
        P(("replica", "fsdp"), None),
        P("fsdp", None),
        P("fsdp", None),
        P("replica", "fsdp", None),
        P("replica", "fsdp", None),
    )
    return jax.shard_map(
        per_device, mesh=mesh, in_specs=in_specs, out_specs=out_specs, check_vma=False
    )
```

profile of v0, /device:TPU:1, one launch (start us, length us, event | category | flops | bytes accessed | tf_op | source)
XLA Modules:
  0.0 511.3 jit_solution(3030680337738197865)
XLA Ops:
  7.2 0.0 all-gather.2.cloned.1.call-start
  7.2 2.1 bitcast_convert_fusion
  9.3 0.0 all-gather.2.cloned.1.call-update
  9.3 0.0 reduce-scatter.2.cloned.1.call-start
  9.4 1.3 fusion.20
  10.7 39.4 %psum.14 = f32[]{:T(128)} all-reduce(f32[]{:T(128)} %fusion.20), channel_id=1, replica_groups=mesh['replica'=16,'fsdp'=16] {'fsdp'}, use_global_device_ids=true, to_apply=%region_2.0 | all-reduce | flops 1 | bytes 8 | tf_op jit(solution)/shard_map/psum | solution.py:49
  50.1 0.7 compare_convert_fusion
  50.8 3.1 fusion.7
  53.9 8.6 %multiply_convert_fusion = bf16[8192,512]{1,0:T(8,128)(2,1)} fusion(bf16[256,8192]{1,0:T(8,128)(2,1)} %param.8, f32[256]{0:T(256)S(1)} %add_rsqrt_fusion, bf16[256,512]{1,0:T(8,128)(2,1)} %param.9, f32[]{:T(128)} %psum.14, f32[256]{0:T(256)S(1)} %compare_convert_fusion), kind=kOutput, calls=%fused_computation | convolution fusion | flops 2162688000 | bytes 12847108 | tf_op jit(solution)/shard_map/dot_general | solution.py:26
  62.5 0.0 copy-start.5
  62.5 0.0 reduce-scatter.2.cloned.1.call-update
  62.5 0.0 copy-start
  62.6 0.0 copy-start.1
  62.6 0.0 copy-start.3
  62.6 0.0 copy-start.4
  62.6 0.0 all-reduce.2.cloned.1.call-start
  62.6 87.0 %all-gather.2.cloned.1.call-done = bf16[8192,512]{1,0:T(8,128)(2,1)} async-done(((bf16[512,512]{1,0:T(8,128)(2,1)}), bf16[8192,512]{1,0:T(8,128)(2,1)}) %all-gather.2.cloned.1.call-update) | async-done | bytes 8388624 | tf_op jit(solution)/shard_map/all_gather | solution.py:52
  149.6 0.0 copy-done.5
  149.6 12.5 %fusion.3 = (f32[256]{0:T(256)S(1)}, f32[256,8192]{1,0:T(8,128)}) fusion(bf16[256,8192]{1,0:T(8,128)(2,1)} %param.8, f32[256]{0:T(256)S(1)} %add_rsqrt_fusion, bf16[8192,512]{1,0:T(8,128)(2,1)} %all-gather.2.cloned.1.call-done, bf16[256,512]{1,0:T(8,128)(2,1)S(1)} %copy-done.5, f32[]{:T(128)} %psum.14, f32[256]{0:T(256)S(1)} %compare_convert_fusion), kind=kOutput, calls=%fused_computation.7 | convolution fusion | flops 2158493440 | bytes 21236740 | tf_op jit(solution)/shard_map/dot_general | solution.py:20
  162.2 210.8 %reduce-scatter.2.cloned.1.call-done = bf16[512,512]{1,0:T(8,128)(2,1)} async-done(((bf16[8192,512]{1,0:T(8,128)(2,1)}), bf16[512,512]{1,0:T(8,128)(2,1)}) %reduce-scatter.2.cloned.1.call-update) | async-done | bytes 524304 | tf_op jit(solution)/shard_map/reduce_scatter | solution.py:56
  373.0 0.0 copy-done
  373.0 0.0 copy-done.1
  373.0 0.0 copy-done.3
  373.0 0.0 copy-done.4
  373.0 3.2 fusion.18
  376.1 0.0 all-reduce.2.cloned.1.call-update
  376.2 0.0 copy-start.2
  376.2 6.9 %fusion.6 = bf16[256,8192]{1,0:T(8,128)(2,1)} fusion(f32[256,8192]{1,0:T(8,128)} %get-tuple-element.11, bf16[256,8192]{1,0:T(8,128)(2,1)} %param.8, f32[256]{0:T(256)S(1)} %broadcast_multiply_fusion, f32[256]{0:T(256)S(1)} %add_rsqrt_fusion), kind=kLoop, calls=%fused_computation.10 | loop fusion | flops 12582912 | bytes 16779264 | tf_op jit(solution)/shard_map/convert_element_type | solution.py:55
  383.1 119.0 %all-reduce.2.cloned.1.call-done = bf16[512,512]{1,0:T(8,128)(2,1)} async-done(((bf16[512,512]{1,0:T(8,128)(2,1)}), bf16[512,512]{1,0:T(8,128)(2,1)}) %all-reduce.2.cloned.1.call-update) | async-done | bytes 524304 | tf_op jit(solution)/shard_map/psum | solution.py:72
  502.1 0.0 copy-done.2
  502.1 2.7 multiply_subtract_fusion
  (2 shorter events, 0.0 us)
Async XLA Ops:
  7.2 142.5 %all-gather.2.cloned.1.call-start = ((), (), s32[]{:S(2)}) async-start(), calls=%async_computation.1 | async-start | bytes 8912896 | tf_op jit(solution)/shard_map/all_gather | solution.py:52
  9.3 363.6 %reduce-scatter.2.cloned.1.call-start = ((), (), s32[]{:S(2)}) async-start(), calls=%async_computation.2 | async-start | bytes 8912896 | tf_op jit(solution)/shard_map/reduce_scatter | solution.py:56
  62.5 87.1 %copy-start.5 = (bf16[256,512]{1,0:T(8,128)(2,1)S(1)}, bf16[256,512]{1,0:T(8,128)(2,1)}, u32[]{:S(2)}) copy-start(bf16[256,512]{1,0:T(8,128)(2,1)} %param.9) | copy-start | bytes 786436
  62.5 310.4 %copy-start = (f32[1,512,512]{2,1,0:T(8,128)S(1)}, f32[1,512,512]{2,1,0:T(8,128)}, u32[]{:S(2)}) copy-start(f32[1,512,512]{2,1,0:T(8,128)} %param.11) | copy-start | bytes 3145732
  62.6 310.4 %copy-start.1 = (f32[512,512]{1,0:T(8,128)S(1)}, f32[512,512]{1,0:T(8,128)}, u32[]{:S(2)}) copy-start(f32[512,512]{1,0:T(8,128)} %param.14) | copy-start | bytes 3145732
  62.6 310.4 %copy-start.3 = (bf16[1,512,512]{2,1,0:T(8,128)(2,1)S(1)}, bf16[1,512,512]{2,1,0:T(8,128)(2,1)}, u32[]{:S(2)}) copy-start(bf16[1,512,512]{2,1,0:T(8,128)(2,1)} %param.13) | copy-start | bytes 1572868
  62.6 310.4 %copy-start.4 = (bf16[1,512,512]{2,1,0:T(8,128)(2,1)S(1)}, bf16[1,512,512]{2,1,0:T(8,128)(2,1)}, u32[]{:S(2)}) copy-start(bf16[1,512,512]{2,1,0:T(8,128)(2,1)} %param.12) | copy-start | bytes 1572868
  62.6 439.5 %all-reduce.2.cloned.1.call-start = ((), (), s32[]{:S(2)}) async-start(), calls=%async_computation.3 | async-start | bytes 1048576 | tf_op jit(solution)/shard_map/psum | solution.py:72
  376.2 125.9 %copy-start.2 = (f32[512,512]{1,0:T(8,128)S(1)}, f32[512,512]{1,0:T(8,128)}, u32[]{:S(2)}) copy-start(f32[512,512]{1,0:T(8,128)} %param.15) | copy-start | bytes 3145732
Sparse Core Ops, SparseCore 0:
  11.1 138.4 all-gather.1
  153.7 219.1 reduce-scatter.1
  376.3 125.7 all-reduce.1
where the time goes:
time: 512 us; the launch traced here: 511 us
  waiting for transfers between devices  417 us (81%)
  blocking collectives  39.4 us (8%)
  matrix products  21.2 us (4%)
  other arithmetic  20 us (4%)
  between operations  13.8 us (3%)
    reduce_scatter x1, waiting for transfers between devices, per_device(): lax.psum_scatter((width_scale * contract_first(normed_low, scaled)).astyp...  211 us
    psum x1, waiting for transfers between devices, per_device(): lax.psum(pseudo_grad.astype(jnp.bfloat16), 'replica').astype(jnp.float32)  119 us
    all_gather x1, waiting for transfers between devices, per_device(): lax.all_gather(weight_low, 'fsdp', axis=0, tiled=True)  87 us
    psum x1, blocking collectives, per_device(): answers = lax.psum(jnp.sum(answer), 'fsdp')  39.4 us
    dot_general x1, matrix products, contract_last(): lax.dot_general(left, right, (((1,), (1,)), ((), ())), preferred_element_...  12.5 us
  transfers between devices with their start and end apart: 3, of which 3 were waited for; matrix products, arithmetic and copies ran while one was open for 6% of the time, Pallas kernels for 0%

commit v1 on v0

--- a/solution.py
+++ b/solution.py
@@ -41,24 +41,25 @@
     width_scale = D ** (-0.5)
     weight_shard = local_weight[0]
     weight_low = weight_shard.astype(jnp.bfloat16)
+    all_weight = lax.all_gather(weight_low, "fsdp", axis=0, tiled=True)
+    all_labels = lax.all_gather(labels, "fsdp", axis=0, tiled=True)
+    all_cotangent = lax.all_gather(cotangent, "fsdp", axis=0, tiled=True)
+    answers = jnp.sum((all_labels >= 0).astype(jnp.float32))
     answer = (labels >= 0).astype(jnp.float32)
+    all_answer = (all_labels >= 0).astype(jnp.float32)
+    all_scaled = (
+        all_cotangent.astype(jnp.float32) * all_answer[:, None] / answers
+    ).astype(jnp.bfloat16)
+    scaled = (cotangent.astype(jnp.float32) * answer[:, None] / answers).astype(jnp.bfloat16)
     values = activations.astype(jnp.float32)
     inverse = lax.rsqrt(jnp.mean(values * values, axis=1, keepdims=True) + norm_eps)
     normed = values * inverse
     normed_low = normed.astype(jnp.bfloat16)
-    answers = lax.psum(jnp.sum(answer), "fsdp")
-    scaled = (cotangent.astype(jnp.float32) * answer[:, None] / answers).astype(jnp.bfloat16)
-    feature_grad = width_scale * contract_last(
-        scaled, lax.all_gather(weight_low, "fsdp", axis=0, tiled=True)
-    )
+    columns = lax.all_to_all(normed_low, "fsdp", 1, 0, tiled=True)
+    gradient = width_scale * contract_first(columns, all_scaled)
+    feature_grad = width_scale * contract_last(scaled, all_weight)
     projected = jnp.mean(feature_grad * normed, axis=1, keepdims=True)
     input_grad = (inverse * (feature_grad - normed * projected)).astype(jnp.bfloat16)
-    gradient = lax.psum_scatter(
-        (width_scale * contract_first(normed_low, scaled)).astype(jnp.bfloat16),
-        "fsdp",
-        scatter_dimension=0,
-        tiled=True,
-    ).astype(jnp.float32)
     first = beta_first * first_moment[0].astype(jnp.float32) + (1.0 - beta_first) * gradient
     second = (
         beta_second * second_moment[0].astype(jnp.float32)

time: 512 us -> 447 us (0.87)
  waiting for transfers between devices: 417 us -> 359 us
  other arithmetic: 20 us -> 12.7 us
    reduce_scatter x1 -> x0, waiting for transfers between devices: 211 us -> none  [per_device(): lax.psum_scatter((width_scale * contract_first(normed_low, scaled)).astyp...]
    all_gather x1 -> x2, waiting for transfers between devices: 87 us -> 234 us  [the longest x1 137 us: per_device(): all_cotangent = lax.all_gather(cotangent, 'fsdp', axis=0, tiled=True)]
    psum x1 -> x0, blocking collectives: 39.4 us -> none  [per_device(): answers = lax.psum(jnp.sum(answer), 'fsdp')]
    all_gather x0 -> x1, blocking collectives: none -> 37.9 us  [per_device(): all_labels = lax.all_gather(labels, 'fsdp', axis=0, tiled=True)]
  transfers between devices with their start and end apart: 3 -> 4, of which waited for: 3 -> 3; matrix products, arithmetic and copies ran while one was open for 6% -> 4% of each run, Pallas kernels for 0% -> 0%
where the time goes in v1:
time: 447 us
  waiting for transfers between devices  359 us (80%)
  blocking collectives  37.9 us (8%)
  matrix products  17 us (4%)
  between operations  13.8 us (3%)
  other arithmetic  12.7 us (3%)
  starting transfers between devices  4.66 us (1%)
    all_gather x1, waiting for transfers between devices, per_device(): all_cotangent = lax.all_gather(cotangent, 'fsdp', axis=0, tiled=True)  137 us
    psum x1, waiting for transfers between devices, per_device(): lax.psum(pseudo_grad.astype(jnp.bfloat16), 'replica').astype(jnp.float32)  124 us
    all_gather x1, waiting for transfers between devices, per_device(): all_weight = lax.all_gather(weight_low, 'fsdp', axis=0, tiled=True)  97 us
    all_gather x1, blocking collectives, per_device(): all_labels = lax.all_gather(labels, 'fsdp', axis=0, tiled=True)  37.9 us
  transfers between devices with their start and end apart: 4, of which 3 were waited for; matrix products, arithmetic and copies ran while one was open for 4% of the time, Pallas kernels for 0%

profile of v1, /device:TPU:1, one launch (start us, length us, event | category | flops | bytes accessed | tf_op | source)
XLA Modules:
  0.0 447.0 jit_solution(12194430913588860542)
XLA Ops:
  7.2 0.0 all-gather.4.cloned.1.call-start
  7.2 2.1 bitcast_convert_fusion
  9.3 0.0 all-gather.4.cloned.1.call-update
  9.3 0.0 all-gather.6.cloned.1.call-start
  9.4 0.7 all-gather.6.cloned.1.call-update
  10.1 0.7 compare_convert_fusion.1
  10.8 37.9 %all-gather = s32[16,1,256]{2,1,0:T(1,128)S(1)} all-gather(s32[1,1,256]{2,1,0:T(1,128)} %bitcast.46), channel_id=1, replica_groups=mesh['replica'=16,'fsdp'=16] {'fsdp'}, dimensions={0}, use_global_device_ids=true | all-gather | bytes 17408 | tf_op jit(solution)/shard_map/all_gather | solution.py:45
  48.7 0.6 fusion.17
  49.3 3.1 fusion.7
  52.4 97.0 %all-gather.4.cloned.1.call-done = bf16[8192,512]{1,0:T(8,128)(2,1)} async-done(((bf16[512,512]{1,0:T(8,128)(2,1)}), bf16[8192,512]{1,0:T(8,128)(2,1)}) %all-gather.4.cloned.1.call-update) | async-done | bytes 8388624 | tf_op jit(solution)/shard_map/all_gather | solution.py:44
  149.4 0.0 copy-start
  149.4 8.1 %fusion.3 = (f32[256]{0:T(256)S(1)}, f32[256,8192]{1,0:T(8,128)S(1)}) fusion(bf16[256,8192]{1,0:T(8,128)(2,1)} %param.8, f32[256]{0:T(256)S(1)} %add_rsqrt_fusion, bf16[8192,512]{1,0:T(8,128)(2,1)} %all-gather.4.cloned.1.call-done, bf16[256,512]{1,0:T(8,128)(2,1)} %param.9, f32[]{:T(128)} %fusion.17, f32[256]{0:T(256)S(1)} %compare_convert_fusion.1), kind=kOutput, calls=%fused_computation.6 | convolution fusion | flops 2158493440 | bytes 21236740 | tf_op jit(solution)/shard_map/dot_general | solution.py:20
  157.6 0.0 copy-done
  157.6 3.4 fusion
  161.0 0.0 copy-start.1
  161.0 0.0 copy-start.2
  161.0 2.4 copy.17
  163.5 4.5 %all-to-all-start = ((bf16[256,16,512]{2,0,1:T(8,128)(2,1)}), bf16[256,16,512]{2,0,1:T(8,128)(2,1)}, u32[]{:S(2)}, u32[]{:S(2)}) async-start(bf16[256,16,512]{2,0,1:T(8,128)(2,1)} %bitcast.43), calls=%async_computation | async-start | bytes 8388608 | tf_op jit(solution)/shard_map/all_to_all | solution.py:58
  168.0 0.0 all-reduce.2.cloned.1.call-start
  168.1 137.3 %all-gather.6.cloned.1.call-done = bf16[4096,512]{1,0:T(8,128)(2,1)} async-done(((bf16[256,512]{1,0:T(8,128)(2,1)}), bf16[4096,512]{1,0:T(8,128)(2,1)}) %all-gather.6.cloned.1.call-update) | async-done | bytes 4194320 | tf_op jit(solution)/shard_map/all_gather | solution.py:46
  305.4 0.0 all-to-all-done
  305.4 0.0 copy-done.1
  305.4 0.0 copy-done.2
  305.4 0.0 copy-start.3
  305.4 8.8 %convert_bitcast_fusion = (bf16[1,512,512]{2,1,0:T(8,128)(2,1)}, bf16[512,512]{1,0:T(8,128)(2,1)}, bf16[1,512,512]{2,1,0:T(8,128)(2,1)}) fusion(bf16[1,512,512]{2,1,0:T(8,128)(2,1)} %param.13, f32[512,512]{1,0:T(8,128)S(1)} %copy-done.2, bf16[1,512,512]{2,1,0:T(8,128)(2,1)} %param.12, f32[1,512,512]{2,1,0:T(8,128)S(1)} %copy-done.1, ...), kind=kOutput, calls=%fused_computation.28 | convolution fusion | flops 2161115136 | bytes 13123588 | tf_op jit(solution)/shard_map/dot_general | solution.py:26
  314.2 0.0 all-reduce.2.cloned.1.call-update
  314.2 123.5 %all-reduce.2.cloned.1.call-done = bf16[512,512]{1,0:T(8,128)(2,1)} async-done(((bf16[512,512]{1,0:T(8,128)(2,1)}), bf16[512,512]{1,0:T(8,128)(2,1)}) %all-reduce.2.cloned.1.call-update) | async-done | bytes 524304 | tf_op jit(solution)/shard_map/psum | solution.py:73
  437.8 0.0 copy-done.3
  437.8 2.7 multiply_subtract_fusion
  (3 shorter events, 0.0 us)
Async XLA Ops:
  7.2 142.3 %all-gather.4.cloned.1.call-start = ((), (), s32[]{:S(2)}) async-start(), calls=%async_computation.1 | async-start | bytes 8912896 | tf_op jit(solution)/shard_map/all_gather | solution.py:44
  9.3 296.1 %all-gather.6.cloned.1.call-start = ((), (), s32[]{:S(2)}) async-start(), calls=%async_computation.2 | async-start | bytes 4456448 | tf_op jit(solution)/shard_map/all_gather | solution.py:46
  149.4 8.2 %copy-start = (bf16[256,8192]{1,0:T(8,128)(2,1)S(1)}, bf16[256,8192]{1,0:T(8,128)(2,1)}, u32[]{:S(2)}) copy-start(bf16[256,8192]{1,0:T(8,128)(2,1)} %param.8) | copy-start | bytes 12582916
  161.0 144.4 %copy-start.1 = (f32[1,512,512]{2,1,0:T(8,128)S(1)}, f32[1,512,512]{2,1,0:T(8,128)}, u32[]{:S(2)}) copy-start(f32[1,512,512]{2,1,0:T(8,128)} %param.11) | copy-start | bytes 3145732
  161.0 144.4 %copy-start.2 = (f32[512,512]{1,0:T(8,128)S(1)}, f32[512,512]{1,0:T(8,128)}, u32[]{:S(2)}) copy-start(f32[512,512]{1,0:T(8,128)} %param.14) | copy-start | bytes 3145732
  163.5 141.9 %all-to-all-start = ((bf16[256,16,512]{2,0,1:T(8,128)(2,1)}), bf16[256,16,512]{2,0,1:T(8,128)(2,1)}, u32[]{:S(2)}, u32[]{:S(2)}) async-start(bf16[256,16,512]{2,0,1:T(8,128)(2,1)} %bitcast.43), calls=%async_computation | async-start | bytes 8388608 | tf_op jit(solution)/shard_map/all_to_all | solution.py:58
  168.0 269.8 %all-reduce.2.cloned.1.call-start = ((), (), s32[]{:S(2)}) async-start(), calls=%async_computation.3 | async-start | bytes 1048576 | tf_op jit(solution)/shard_map/psum | solution.py:73
  305.4 132.4 %copy-start.3 = (f32[512,512]{1,0:T(8,128)S(1)}, f32[512,512]{1,0:T(8,128)}, u32[]{:S(2)}) copy-start(f32[512,512]{1,0:T(8,128)} %param.15) | copy-start | bytes 3145732
Sparse Core Ops, SparseCore 0:
  11.1 138.2 all-gather.3
  152.0 153.2 all-gather.5
  314.4 123.3 all-reduce.1

commit v2 on v1

--- a/solution.py
+++ b/solution.py
@@ -28,6 +28,21 @@
     )
 
 
+def gather_rows(block, axis):
+    count = lax.axis_size(axis)
+    copies = jnp.broadcast_to(block[None], (count,) + block.shape)
+    gathered = lax.all_to_all(copies, axis, 0, 0, tiled=True)
+    return gathered.reshape((count * block.shape[0],) + block.shape[1:])
+
+
+def sum_rows(block, axis):
+    count = lax.axis_size(axis)
+    pieces = block.reshape((count, block.shape[0] // count) + block.shape[1:])
+    received = lax.all_to_all(pieces, axis, 0, 0, tiled=True)
+    partial = jnp.sum(received.astype(jnp.float32), axis=0).astype(block.dtype)
+    return gather_rows(partial, axis)
+
+
 def per_device(
     activations,
     cotangent,
@@ -41,9 +56,9 @@
     width_scale = D ** (-0.5)
     weight_shard = local_weight[0]
     weight_low = weight_shard.astype(jnp.bfloat16)
-    all_weight = lax.all_gather(weight_low, "fsdp", axis=0, tiled=True)
-    all_labels = lax.all_gather(labels, "fsdp", axis=0, tiled=True)
-    all_cotangent = lax.all_gather(cotangent, "fsdp", axis=0, tiled=True)
+    all_weight = gather_rows(weight_low, "fsdp")
+    all_labels = gather_rows(labels, "fsdp")
+    all_cotangent = gather_rows(cotangent, "fsdp")
     answers = jnp.sum((all_labels >= 0).astype(jnp.float32))
     answer = (labels >= 0).astype(jnp.float32)
     all_answer = (all_labels >= 0).astype(jnp.float32)
@@ -70,7 +85,7 @@
     )
     pseudo_grad = anchor_weight - stepped
     replicas = lax.axis_size("replica")
-    average = lax.psum(pseudo_grad.astype(jnp.bfloat16), "replica").astype(jnp.float32) / replicas
+    average = sum_rows(pseudo_grad.astype(jnp.bfloat16), "replica").astype(jnp.float32) / replicas
     new_state = outer_momentum * outer_state + average
     new_anchor = anchor_weight - outer_rate * (average + outer_momentum * new_state)
     new_first = first.astype(jnp.bfloat16)[None]

time: 447 us -> 457 us (1.022)
  waiting for transfers between devices: 359 us -> 179 us
  blocking collectives: 37.9 us -> 217 us
  starting transfers between devices: 4.66 us -> 20.8 us
  between operations: 13.8 us -> 0.75 us
  local copies, waits for them, and re-layouts: 2.46 us -> 11 us
    all_gather x2 -> x0, waiting for transfers between devices: 234 us -> none  [the longest x1 137 us: per_device(): all_cotangent = lax.all_gather(cotangent, 'fsdp', axis=0, tiled=True)]
    all_to_all x0 -> x3, blocking collectives: none -> 217 us  [the longest x2 202 us: gather_rows(): gathered = lax.all_to_all(copies, axis, 0, 0, tiled=True)]
    psum x1 -> x0, waiting for transfers between devices: 124 us -> none  [per_device(): lax.psum(pseudo_grad.astype(jnp.bfloat16), 'replica').astype(jnp.float32)]
    all_to_all x1, waiting for transfers between devices: 0.01 us -> 97.6 us  [per_device(): columns = lax.all_to_all(normed_low, 'fsdp', 1, 0, tiled=True)]
    all_to_all x0 -> x2, waiting for transfers between devices: none -> 81.6 us  [gather_rows(): gathered = lax.all_to_all(copies, axis, 0, 0, tiled=True)]
    all_gather x1 -> x0, blocking collectives: 37.9 us -> none  [per_device(): all_labels = lax.all_gather(labels, 'fsdp', axis=0, tiled=True)]
    all_to_all x0 -> x2, starting transfers between devices: none -> 16.3 us  [gather_rows(): gathered = lax.all_to_all(copies, axis, 0, 0, tiled=True)]
  transfers between devices with their start and end apart: 4 -> 3, of which waited for: 3 -> 3; matrix products, arithmetic and copies ran while one was open for 4% -> 5% of each run, Pallas kernels for 0% -> 0%
where the time goes in v2:
time: 457 us
  blocking collectives  217 us (47%)
  waiting for transfers between devices  179 us (39%)
  starting transfers between devices  20.8 us (5%)
  matrix products  16.8 us (4%)
  other arithmetic  11.4 us (2%)
  local copies, waits for them, and re-layouts  11 us (2%)
    all_to_all x2, blocking collectives, gather_rows(): gathered = lax.all_to_all(copies, axis, 0, 0, tiled=True)  202 us
    all_to_all x1, waiting for transfers between devices, per_device(): columns = lax.all_to_all(normed_low, 'fsdp', 1, 0, tiled=True)  97.6 us
    all_to_all x2, waiting for transfers between devices, gather_rows(): gathered = lax.all_to_all(copies, axis, 0, 0, tiled=True)  81.6 us
    all_to_all x2, starting transfers between devices, gather_rows(): gathered = lax.all_to_all(copies, axis, 0, 0, tiled=True)  16.3 us
    all_to_all x1, blocking collectives, sum_rows(): received = lax.all_to_all(pieces, axis, 0, 0, tiled=True)  15.2 us
  transfers between devices with their start and end apart: 3, of which 3 were waited for; matrix products, arithmetic and copies ran while one was open for 5% of the time, Pallas kernels for 0%

profile of v2, /device:TPU:1, one launch (start us, length us, event | category | flops | bytes accessed | tf_op | source)
XLA Modules:
  0.0 456.8 jit_solution(13577834109296649431)
XLA Ops:
  0.6 1.3 broadcast_in_dim.14
  1.9 11.7 %all-to-all-start = ((s32[16,1,256]{2,1,0:T(1,128)}), s32[16,1,256]{2,1,0:T(1,128)S(1)}, u32[]{:S(2)}, u32[]{:S(2)}) async-start(s32[16,1,256]{2,1,0:T(1,128)} %broadcast_in_dim.14), calls=%async_computation | async-start | bytes 32768 | tf_op jit(solution)/shard_map/all_to_all | solution.py:34
  13.7 1.3 convert_bitcast_fusion.1
  15.0 7.6 %all-to-all-done = s32[16,1,256]{2,1,0:T(1,128)S(1)} async-done(((s32[16,1,256]{2,1,0:T(1,128)}), s32[16,1,256]{2,1,0:T(1,128)S(1)}, u32[]{:S(2)}, u32[]{:S(2)}) %all-to-all-start) | async-done | bytes 16416 | tf_op jit(solution)/shard_map/all_to_all | solution.py:34
  22.6 0.8 broadcast_in_dim.16
  23.4 0.0 copy-start.3
  23.4 188.2 %all_to_all.42 = bf16[16,512,512]{2,1,0:T(8,128)(2,1)} all-to-all(bf16[16,512,512]{2,1,0:T(8,128)(2,1)S(1)} %broadcast_in_dim.16), channel_id=1, replica_groups=mesh['replica'=16,'fsdp'=16] {'fsdp'}, dimensions={0} | all-to-all | bytes 16777216 | tf_op jit(solution)/shard_map/all_to_all | solution.py:34
  211.6 0.0 copy-done.3
  211.6 0.0 copy-start.4
  211.6 2.3 broadcast_in_dim.17
  214.0 4.6 all-to-all-start.3
  218.6 0.0 copy-done.4
  218.6 3.1 fusion.7
  221.7 0.6 fusion.24
  222.3 0.0 copy-start
  222.3 8.1 %fusion.3 = (f32[256]{0:T(256)S(1)}, f32[256,8192]{1,0:T(8,128)S(1)}) fusion(bf16[256,8192]{1,0:T(8,128)(2,1)} %param.8, f32[256]{0:T(256)S(1)} %add_rsqrt_fusion, bf16[8192,512]{1,0:T(8,128)(2,1)} %bitcast.60, bf16[256,512]{1,0:T(8,128)(2,1)S(1)} %copy-done.3, f32[]{:T(128)} %fusion.24, f32[256]{0:T(256)S(1)} %compare_convert_fusion.1), kind=kOutput, calls=%fused_computation.6 | convolution fusion | flops 2158493440 | bytes 21236740 | tf_op jit(solution)/shard_map/dot_general | solution.py:20
  230.4 0.0 copy-done
  230.4 4.5 fusion
  234.9 0.0 copy-start.1
  234.9 0.0 copy-start.5
  234.9 6.5 %copy.15 = bf16[256,8192]{0,1:T(8,128)(2,1)} copy(bf16[256,8192]{1,0:T(8,128)(2,1)} %get-tuple-element.7) | data formatting | bytes 8388608 | tf_op jit(solution)/shard_map/all_to_all | solution.py:73
  241.4 74.0 %all-to-all-done.3 = bf16[16,256,512]{2,1,0:T(8,128)(2,1)} async-done(((bf16[16,256,512]{2,1,0:T(8,128)(2,1)}), bf16[16,256,512]{2,1,0:T(8,128)(2,1)}, u32[]{:S(2)}, u32[]{:S(2)}) %all-to-all-start.3) | async-done | bytes 4194336 | tf_op jit(solution)/shard_map/all_to_all | solution.py:34
  315.3 4.5 all-to-all-start.2
  319.9 97.6 %all-to-all-done.2 = bf16[256,16,512]{0,2,1:T(8,128)(2,1)} async-done(((bf16[256,16,512]{0,2,1:T(8,128)(2,1)}), bf16[256,16,512]{0,2,1:T(8,128)(2,1)}, u32[]{:S(2)}, u32[]{:S(2)}) %all-to-all-start.2) | async-done | bytes 4194336 | tf_op jit(solution)/shard_map/all_to_all | solution.py:73
  417.5 0.0 copy-done.1
  417.5 0.0 copy-done.5
  417.5 0.0 copy-start.2
  417.5 8.7 %convert_bitcast_fusion = (bf16[1,512,512]{2,1,0:T(8,128)(2,1)}, bf16[512,512]{1,0:T(8,128)(2,1)S(1)}, bf16[1,512,512]{2,1,0:T(8,128)(2,1)}) fusion(bf16[1,512,512]{2,1,0:T(8,128)(2,1)S(1)} %copy-done.5, f32[512,512]{1,0:T(8,128)S(1)} %copy-done.1, bf16[1,512,512]{2,1,0:T(8,128)(2,1)} %param.12, f32[1,512,512]{2,1,0:T(8,128)} %param.11, ...), kind=kOutput, calls=%fused_computation.31 | convolution fusion | flops 2161115136 | bytes 13123588 | tf_op jit(solution)/shard_map/dot_general | solution.py:26
  426.2 15.2 %all_to_all.43 = bf16[16,32,512]{2,1,0:T(8,128)(2,1)S(1)} all-to-all(bf16[16,32,512]{2,1,0:T(8,128)(2,1)S(1)} %bitcast.61), channel_id=1, replica_groups=mesh['replica'=16,'fsdp'=16] {'replica'}, dimensions={0} | all-to-all | bytes 1048576 | tf_op jit(solution)/shard_map/all_to_all | solution.py:41
  441.4 0.1 reduce_sum.42
  441.5 13.5 %all_to_all.44 = bf16[16,32,512]{2,1,0:T(8,128)(2,1)S(1)} all-to-all(bf16[16,32,512]{2,1,0:T(8,128)(2,1)S(1)} %broadcast_in_dim.18), channel_id=1, replica_groups=mesh['replica'=16,'fsdp'=16] {'replica'}, dimensions={0} | all-to-all | bytes 1048576 | tf_op jit(solution)/shard_map/all_to_all | solution.py:34
  455.0 0.1 convert_multiply_fusion.2
  455.1 0.0 copy-done.2
  455.1 1.7 fusion.15
  (6 shorter events, 0.1 us)
Async XLA Ops:
  1.9 20.7 %all-to-all-start = ((s32[16,1,256]{2,1,0:T(1,128)}), s32[16,1,256]{2,1,0:T(1,128)S(1)}, u32[]{:S(2)}, u32[]{:S(2)}) async-start(s32[16,1,256]{2,1,0:T(1,128)} %broadcast_in_dim.14), calls=%async_computation | async-start | bytes 32768 | tf_op jit(solution)/shard_map/all_to_all | solution.py:34
  23.4 188.2 %copy-start.3 = (bf16[256,512]{1,0:T(8,128)(2,1)S(1)}, bf16[256,512]{1,0:T(8,128)(2,1)}, u32[]{:S(2)}) copy-start(bf16[256,512]{1,0:T(8,128)(2,1)} %param.9) | copy-start | bytes 786436
  211.6 6.9 %copy-start.4 = (s32[256]{0:T(256)S(1)}, s32[256]{0:T(256)}, u32[]{:S(2)}) copy-start(s32[256]{0:T(256)} %param.10) | copy-start | bytes 3076
  214.0 101.3 %all-to-all-start.3 = ((bf16[16,256,512]{2,1,0:T(8,128)(2,1)}), bf16[16,256,512]{2,1,0:T(8,128)(2,1)}, u32[]{:S(2)}, u32[]{:S(2)}) async-start(bf16[16,256,512]{2,1,0:T(8,128)(2,1)} %broadcast_in_dim.17), calls=%async_computation.3 | async-start | bytes 8388608 | tf_op jit(solution)/shard_map/all_to_all | solution.py:34
  222.3 8.1 %copy-start = (bf16[256,8192]{1,0:T(8,128)(2,1)S(1)}, bf16[256,8192]{1,0:T(8,128)(2,1)}, u32[]{:S(2)}) copy-start(bf16[256,8192]{1,0:T(8,128)(2,1)} %param.8) | copy-start | bytes 12582916
  234.9 182.6 %copy-start.1 = (f32[512,512]{1,0:T(8,128)S(1)}, f32[512,512]{1,0:T(8,128)}, u32[]{:S(2)}) copy-start(f32[512,512]{1,0:T(8,128)} %param.14) | copy-start | bytes 3145732
  234.9 182.6 %copy-start.5 = (bf16[1,512,512]{2,1,0:T(8,128)(2,1)S(1)}, bf16[1,512,512]{2,1,0:T(8,128)(2,1)}, u32[]{:S(2)}) copy-start(bf16[1,512,512]{2,1,0:T(8,128)(2,1)} %param.13) | copy-start | bytes 1572868
  315.3 102.2 %all-to-all-start.2 = ((bf16[256,16,512]{0,2,1:T(8,128)(2,1)}), bf16[256,16,512]{0,2,1:T(8,128)(2,1)}, u32[]{:S(2)}, u32[]{:S(2)}) async-start(bf16[256,16,512]{0,2,1:T(8,128)(2,1)} %bitcast.59), calls=%async_computation.2 | async-start | bytes 8388608 | tf_op jit(solution)/shard_map/all_to_all | solution.py:73
  417.5 37.6 %copy-start.2 = (f32[512,512]{1,0:T(8,128)S(1)}, f32[512,512]{1,0:T(8,128)}, u32[]{:S(2)}) copy-start(f32[512,512]{1,0:T(8,128)} %param.15) | copy-start | bytes 3145732

commit v3 on v2

--- a/solution.py
+++ b/solution.py
@@ -56,12 +56,17 @@
     width_scale = D ** (-0.5)
     weight_shard = local_weight[0]
     weight_low = weight_shard.astype(jnp.bfloat16)
-    all_weight = gather_rows(weight_low, "fsdp")
-    all_labels = gather_rows(labels, "fsdp")
-    all_cotangent = gather_rows(cotangent, "fsdp")
-    answers = jnp.sum((all_labels >= 0).astype(jnp.float32))
     answer = (labels >= 0).astype(jnp.float32)
-    all_answer = (all_labels >= 0).astype(jnp.float32)
+    rows, width = weight_low.shape
+    tokens = cotangent.shape[0]
+    flags = jnp.zeros((16, width), jnp.bfloat16).at[0, :tokens].set(answer.astype(jnp.bfloat16))
+    packed = jnp.concatenate([weight_low, cotangent, flags], axis=0)
+    gathered = lax.all_gather(packed, "fsdp", axis=0, tiled=False)
+    count = gathered.shape[0]
+    all_weight = gathered[:, :rows].reshape(count * rows, width)
+    all_cotangent = gathered[:, rows : rows + tokens].reshape(count * tokens, width)
+    all_answer = gathered[:, rows + tokens, :tokens].reshape(count * tokens).astype(jnp.float32)
+    answers = jnp.sum(all_answer)
     all_scaled = (
         all_cotangent.astype(jnp.float32) * all_answer[:, None] / answers
     ).astype(jnp.bfloat16)

time: 457 us -> 371 us (0.81)
  blocking collectives: 217 us -> 28.7 us
  waiting for transfers between devices: 179 us -> 279 us
  starting transfers between devices: 20.8 us -> 4.6 us
  between operations: 0.75 us -> 14.1 us
    all_to_all x2 -> x1, blocking collectives: 202 us -> 13.5 us  [gather_rows(): gathered = lax.all_to_all(copies, axis, 0, 0, tiled=True)]
    all_gather x0 -> x1, waiting for transfers between devices: none -> 181 us  [per_device(): gathered = lax.all_gather(packed, 'fsdp', axis=0, tiled=False)]
    all_to_all x2 -> x0, waiting for transfers between devices: 81.6 us -> none  [gather_rows(): gathered = lax.all_to_all(copies, axis, 0, 0, tiled=True)]
    all_to_all x2 -> x0, starting transfers between devices: 16.3 us -> none  [gather_rows(): gathered = lax.all_to_all(copies, axis, 0, 0, tiled=True)]
    slice x0 -> x1, local copies, waits for them, and re-layouts: none -> 7.47 us  [per_device(): all_weight = gathered[:, :rows].reshape(count * rows, width)]
  transfers between devices with their start and end apart: 3 -> 2, of which waited for: 3 -> 2; matrix products, arithmetic and copies ran while one was open for 5% -> 1% of each run, Pallas kernels for 0% -> 0%
where the time goes in v3:
time: 371 us; the launch traced here: 370 us
  waiting for transfers between devices  279 us (75%)
  blocking collectives  28.7 us (8%)
  other arithmetic  15.7 us (4%)
  matrix products  14.5 us (4%)
  between operations  14.1 us (4%)
  local copies, waits for them, and re-layouts  14 us (4%)
  starting transfers between devices  4.6 us (1%)
    all_gather x1, waiting for transfers between devices, per_device(): gathered = lax.all_gather(packed, 'fsdp', axis=0, tiled=False)  181 us
    all_to_all x1, waiting for transfers between devices, per_device(): columns = lax.all_to_all(normed_low, 'fsdp', 1, 0, tiled=True)  97.4 us
    all_to_all x1, blocking collectives, sum_rows(): received = lax.all_to_all(pieces, axis, 0, 0, tiled=True)  15.2 us
    all_to_all x1, blocking collectives, gather_rows(): gathered = lax.all_to_all(copies, axis, 0, 0, tiled=True)  13.5 us
    dot_general x1, matrix products, contract_first(): lax.dot_general(left, right, (((0,), (0,)), ((), ())), preferred_element_...  8.7 us
    slice x1, local copies, waits for them, and re-layouts, per_device(): all_weight = gathered[:, :rows].reshape(count * rows, width)  7.47 us
  transfers between devices with their start and end apart: 2, of which 2 were waited for; matrix products, arithmetic and copies ran while one was open for 1% of the time, Pallas kernels for 0%

profile of v3, /device:TPU:1, one launch (start us, length us, event | category | flops | bytes accessed | tf_op | source)
XLA Modules:
  0.0 370.3 jit_solution(8505337747548117883)
XLA Ops:
  7.2 0.0 all-gather.3.cloned.1.call-start
  7.2 0.7 compare_convert_fusion
  7.9 1.3 bitcast_convert_fusion
  9.2 1.9 fusion.21
  11.1 0.0 all-gather.3.cloned.1.call-update
  11.1 3.1 fusion.7
  14.2 181.3 %all-gather.3.cloned.1.call-done = bf16[12544,512]{1,0:T(8,128)(2,1)} async-done(((bf16[784,512]{1,0:T(8,128)(2,1)}), bf16[12544,512]{1,0:T(8,128)(2,1)}) %all-gather.3.cloned.1.call-update) | async-done | bytes 12845072 | tf_op jit(solution)/shard_map/all_gather | solution.py:64
  195.5 1.5 fusion.27
  197.0 0.0 copy-start
  197.0 0.0 copy-start.3
  197.0 7.5 %slice.29 = bf16[16,512,512]{2,1,0:T(8,128)(2,1)} slice(bf16[16,784,512]{2,1,0:T(8,128)(2,1)} %bitcast.62), slice={[0:16], [0:512], [0:512]} | slice | bytes 16777216 | tf_op jit(solution)/shard_map/slice | solution.py:66
  204.5 0.0 copy-done
  204.5 0.0 copy-done.3
  204.5 5.8 %fusion.3 = (f32[256]{0:T(256)S(1)}, f32[256,8192]{1,0:T(8,128)S(1)}) fusion(bf16[256,8192]{1,0:T(8,128)(2,1)S(1)} %copy-done, f32[256]{0:T(256)S(1)} %add_rsqrt_fusion, bf16[8192,512]{1,0:T(8,128)(2,1)} %bitcast.60, bf16[256,512]{1,0:T(8,128)(2,1)S(1)} %copy-done.3, f32[]{:T(128)} %fusion.27, f32[256]{0:T(256)S(1)} %get-tuple-element.24), kind=kOutput, calls=%fused_computation.6 | convolution fusion | flops 2158493440 | bytes 21236740 | tf_op jit(solution)/shard_map/dot_general | solution.py:20
  210.2 4.5 %fusion = (bf16[256,8192]{1,0:T(8,128)(2,1)}, bf16[256,8192]{1,0:T(8,128)(2,1)}) fusion(bf16[256,8192]{1,0:T(8,128)(2,1)S(1)} %copy-done, f32[256]{0:T(256)S(1)} %add_rsqrt_fusion, f32[256,8192]{1,0:T(8,128)S(1)} %get-tuple-element.27, f32[256]{0:T(256)S(1)} %broadcast_multiply_fusion), kind=kLoop, calls=%fused_computation.3 | loop fusion | flops 14680064 | bytes 20973568 | tf_op jit(solution)/shard_map/convert_element_type | solution.py:77
  214.7 0.0 copy-start.1
  214.7 0.0 copy-start.4
  214.7 6.5 %copy.14 = bf16[256,8192]{0,1:T(8,128)(2,1)} copy(bf16[256,8192]{1,0:T(8,128)(2,1)} %get-tuple-element.19) | data formatting | bytes 8388608 | tf_op jit(solution)/shard_map/all_to_all | solution.py:78
  221.2 4.6 %all-to-all-start = ((bf16[256,16,512]{0,2,1:T(8,128)(2,1)}), bf16[256,16,512]{0,2,1:T(8,128)(2,1)}, u32[]{:S(2)}, u32[]{:S(2)}) async-start(bf16[256,16,512]{0,2,1:T(8,128)(2,1)} %bitcast.59), calls=%async_computation | async-start | bytes 8388608 | tf_op jit(solution)/shard_map/all_to_all | solution.py:78
  225.8 0.9 slice_convert_fusion
  226.7 97.4 %all-to-all-done = bf16[256,16,512]{0,2,1:T(8,128)(2,1)} async-done(((bf16[256,16,512]{0,2,1:T(8,128)(2,1)}), bf16[256,16,512]{0,2,1:T(8,128)(2,1)}, u32[]{:S(2)}, u32[]{:S(2)}) %all-to-all-start) | async-done | bytes 4194336 | tf_op jit(solution)/shard_map/all_to_all | solution.py:78
  324.0 0.0 copy-done.1
  324.0 0.0 copy-done.4
  324.0 0.0 copy-start.2
  324.0 8.7 %convert_bitcast_fusion = (bf16[1,512,512]{2,1,0:T(8,128)(2,1)}, bf16[512,512]{1,0:T(8,128)(2,1)S(1)}, bf16[1,512,512]{2,1,0:T(8,128)(2,1)}) fusion(bf16[1,512,512]{2,1,0:T(8,128)(2,1)S(1)} %copy-done.4, f32[512,512]{1,0:T(8,128)S(1)} %copy-done.1, bf16[1,512,512]{2,1,0:T(8,128)(2,1)} %param.14, f32[1,512,512]{2,1,0:T(8,128)} %param.13, ...), kind=kOutput, calls=%fused_computation.35 | convolution fusion | flops 2161115136 | bytes 13124096 | tf_op jit(solution)/shard_map/dot_general | solution.py:26
  332.7 15.2 %all_to_all.26 = bf16[16,32,512]{2,1,0:T(8,128)(2,1)S(1)} all-to-all(bf16[16,32,512]{2,1,0:T(8,128)(2,1)S(1)} %bitcast.65), channel_id=1, replica_groups=mesh['replica'=16,'fsdp'=16] {'replica'}, dimensions={0} | all-to-all | bytes 1048576 | tf_op jit(solution)/shard_map/all_to_all | solution.py:41
  348.0 0.1 reduce_sum.42
  348.1 13.5 %all_to_all.27 = bf16[16,32,512]{2,1,0:T(8,128)(2,1)S(1)} all-to-all(bf16[16,32,512]{2,1,0:T(8,128)(2,1)S(1)} %broadcast_in_dim.6), channel_id=1, replica_groups=mesh['replica'=16,'fsdp'=16] {'replica'}, dimensions={0} | all-to-all | bytes 1048576 | tf_op jit(solution)/shard_map/all_to_all | solution.py:34
  361.6 0.1 convert_multiply_fusion.2
  361.7 0.0 copy-done.2
  361.7 1.7 fusion.16
  (5 shorter events, 0.1 us)
Async XLA Ops:
  7.2 188.3 %all-gather.3.cloned.1.call-start = ((), (), s32[]{:S(2)}) async-start(), calls=%async_computation.3 | async-start | bytes 13647872 | tf_op jit(solution)/shard_map/all_gather | solution.py:64
  197.0 7.5 %copy-start = (bf16[256,8192]{1,0:T(8,128)(2,1)S(1)}, bf16[256,8192]{1,0:T(8,128)(2,1)}, u32[]{:S(2)}) copy-start(bf16[256,8192]{1,0:T(8,128)(2,1)} %param.10) | copy-start | bytes 12582916
  197.0 7.5 %copy-start.3 = (bf16[256,512]{1,0:T(8,128)(2,1)S(1)}, bf16[256,512]{1,0:T(8,128)(2,1)}, u32[]{:S(2)}) copy-start(bf16[256,512]{1,0:T(8,128)(2,1)} %param.11) | copy-start | bytes 786436
  214.7 109.3 %copy-start.1 = (f32[512,512]{1,0:T(8,128)S(1)}, f32[512,512]{1,0:T(8,128)}, u32[]{:S(2)}) copy-start(f32[512,512]{1,0:T(8,128)} %param.16) | copy-start | bytes 3145732
  214.7 109.3 %copy-start.4 = (bf16[1,512,512]{2,1,0:T(8,128)(2,1)S(1)}, bf16[1,512,512]{2,1,0:T(8,128)(2,1)}, u32[]{:S(2)}) copy-start(bf16[1,512,512]{2,1,0:T(8,128)(2,1)} %param.15) | copy-start | bytes 1572868
  221.2 102.8 %all-to-all-start = ((bf16[256,16,512]{0,2,1:T(8,128)(2,1)}), bf16[256,16,512]{0,2,1:T(8,128)(2,1)}, u32[]{:S(2)}, u32[]{:S(2)}) async-start(bf16[256,16,512]{0,2,1:T(8,128)(2,1)} %bitcast.59), calls=%async_computation | async-start | bytes 8388608 | tf_op jit(solution)/shard_map/all_to_all | solution.py:78
  324.0 37.7 %copy-start.2 = (f32[512,512]{1,0:T(8,128)S(1)}, f32[512,512]{1,0:T(8,128)}, u32[]{:S(2)}) copy-start(f32[512,512]{1,0:T(8,128)} %param.17) | copy-start | bytes 3145732
Sparse Core Ops, SparseCore 0:
  11.2 184.2 all-gather.2

commit v4 on v3

--- a/solution.py
+++ b/solution.py
@@ -62,6 +62,12 @@
     flags = jnp.zeros((16, width), jnp.bfloat16).at[0, :tokens].set(answer.astype(jnp.bfloat16))
     packed = jnp.concatenate([weight_low, cotangent, flags], axis=0)
     gathered = lax.all_gather(packed, "fsdp", axis=0, tiled=False)
+    values = activations.astype(jnp.float32)
+    inverse = lax.rsqrt(jnp.mean(values * values, axis=1, keepdims=True) + norm_eps)
+    normed = values * inverse
+    normed_low = normed.astype(jnp.bfloat16)
+    columns = lax.all_to_all(normed_low, "fsdp", 1, 0, tiled=True)
+    gathered, columns = lax.optimization_barrier((gathered, columns))
     count = gathered.shape[0]
     all_weight = gathered[:, :rows].reshape(count * rows, width)
     all_cotangent = gathered[:, rows : rows + tokens].reshape(count * tokens, width)
@@ -71,11 +77,6 @@
         all_cotangent.astype(jnp.float32) * all_answer[:, None] / answers
     ).astype(jnp.bfloat16)
     scaled = (cotangent.astype(jnp.float32) * answer[:, None] / answers).astype(jnp.bfloat16)
-    values = activations.astype(jnp.float32)
-    inverse = lax.rsqrt(jnp.mean(values * values, axis=1, keepdims=True) + norm_eps)
-    normed = values * inverse
-    normed_low = normed.astype(jnp.bfloat16)
-    columns = lax.all_to_all(normed_low, "fsdp", 1, 0, tiled=True)
     gradient = width_scale * contract_first(columns, all_scaled)
     feature_grad = width_scale * contract_last(scaled, all_weight)
     projected = jnp.mean(feature_grad * normed, axis=1, keepdims=True)

time: 371 us -> 337 us (0.908)
  waiting for transfers between devices: 279 us -> 121 us
  blocking collectives: 28.7 us -> 137 us
  other arithmetic: 15.7 us -> 23.6 us
  starting transfers between devices: 4.6 us -> 11.5 us
    all_to_all x2 -> x1, blocking collectives: 28.7 us -> 137 us  [per_device(): columns = lax.all_to_all(normed_low, 'fsdp', 1, 0, tiled=True)]
    all_to_all x1 -> x2, waiting for transfers between devices: 97.4 us -> 2.56 us  [the longest x1 2.56 us: gather_rows(): gathered = lax.all_to_all(copies, axis, 0, 0, tiled=True)]
    all_gather x1, waiting for transfers between devices: 181 us -> 119 us  [per_device(): gathered = lax.all_gather(packed, 'fsdp', axis=0, tiled=False)]
    convert_element_type x0 -> x2, other arithmetic: none -> 9.14 us  [the longest x1 6.93 us: per_device(): (inverse * (feature_grad - normed * projected)).astype(jnp.bfloat16)]
    all_to_all x1 -> x2, starting transfers between devices: 4.57 us -> 11.4 us  [the longest x1 5.73 us: gather_rows(): gathered = lax.all_to_all(copies, axis, 0, 0, tiled=True)]
    dot_general x1, matrix products: 5.76 us -> 12.5 us  [contract_last(): lax.dot_general(left, right, (((1,), (1,)), ((), ())), preferred_element_...]
    all_to_all x1, local copies, waits for them, and re-layouts: 6.48 us -> 0.45 us  [per_device(): columns = lax.all_to_all(normed_low, 'fsdp', 1, 0, tiled=True)]
    dot_general x1, matrix products: 8.7 us -> 4.25 us  [contract_first(): lax.dot_general(left, right, (((0,), (0,)), ((), ())), preferred_element_...]
  transfers between devices with their start and end apart: 2 -> 3, of which waited for: 2 -> 2; matrix products, arithmetic and copies ran while one was open for 1% -> 8% of each run, Pallas kernels for 0% -> 0%
where the time goes in v4:
time: 337 us
  blocking collectives  137 us (41%)
  waiting for transfers between devices  121 us (36%)
  other arithmetic  23.6 us (7%)
  matrix products  16.8 us (5%)
  between operations  14.1 us (4%)
  local copies, waits for them, and re-layouts  12.1 us (4%)
  starting transfers between devices  11.5 us (3%)
    all_to_all x1, blocking collectives, per_device(): columns = lax.all_to_all(normed_low, 'fsdp', 1, 0, tiled=True)  137 us
    all_gather x1, waiting for transfers between devices, per_device(): gathered = lax.all_gather(packed, 'fsdp', axis=0, tiled=False)  119 us
    dot_general x1, matrix products, contract_last(): lax.dot_general(left, right, (((1,), (1,)), ((), ())), preferred_element_...  12.5 us
    slice x1, local copies, waits for them, and re-layouts, per_device(): all_weight = gathered[:, :rows].reshape(count * rows, width)  7.32 us
    convert_element_type x1, other arithmetic, per_device(): (inverse * (feature_grad - normed * projected)).astype(jnp.bfloat16)  6.93 us
  transfers between devices with their start and end apart: 3, of which 2 were waited for; matrix products, arithmetic and copies ran while one was open for 8% of the time, Pallas kernels for 0%

profile of v4, /device:TPU:1, one launch (start us, length us, event | category | flops | bytes accessed | tf_op | source)
XLA Modules:
  0.0 336.6 jit_solution(7755587023459017039)
XLA Ops:
  7.2 0.0 all-gather.3.cloned.1.call-start
  7.2 0.7 compare_convert_fusion
  7.9 1.3 bitcast_convert_fusion
  9.2 1.9 fusion.17
  11.1 0.0 all-gather.3.cloned.1.call-update
  11.1 3.1 fusion.7
  14.2 3.2 fusion.2
  17.5 0.4 copy.16
  17.9 137.2 %all_to_all.29 = bf16[256,16,512]{2,0,1:T(8,128)(2,1)} all-to-all(bf16[256,16,512]{2,0,1:T(8,128)(2,1)S(1)} %bitcast.57), channel_id=1, replica_groups=mesh['replica'=16,'fsdp'=16] {'fsdp'}, dimensions={1} | all-to-all | bytes 8388608 | tf_op jit(solution)/shard_map/all_to_all | solution.py:69
  155.2 118.7 %all-gather.3.cloned.1.call-done = bf16[12544,512]{1,0:T(8,128)(2,1)} async-done(((bf16[784,512]{1,0:T(8,128)(2,1)}), bf16[12544,512]{1,0:T(8,128)(2,1)}) %all-gather.3.cloned.1.call-update) | async-done | bytes 12845072 | tf_op jit(solution)/shard_map/all_gather | solution.py:64
  273.9 1.5 fusion.23
  275.4 0.8 slice_convert_fusion
  276.2 2.6 slice.27
  278.8 7.3 %slice.26 = bf16[16,512,512]{2,1,0:T(8,128)(2,1)} slice(bf16[16,784,512]{2,1,0:T(8,128)(2,1)} %bitcast.62), slice={[0:16], [0:512], [0:512]} | slice | bytes 16777216 | tf_op jit(solution)/shard_map/slice | solution.py:72
  286.2 0.0 copy-start
  286.2 0.0 copy-start.1
  286.2 0.0 copy-start.3
  286.2 0.0 copy-start.5
  286.2 0.0 copy-start.6
  286.2 2.2 fusion.9
  288.4 0.0 copy-done
  288.4 0.3 copy-done.1
  288.7 0.3 copy-done.3
  289.0 0.1 copy-done.5
  289.1 0.1 copy-done.6
  289.2 0.0 copy-start.4
  289.2 4.2 %convert_bitcast_fusion = (bf16[1,512,512]{2,1,0:T(8,128)(2,1)}, bf16[512,512]{1,0:T(8,128)(2,1)}, bf16[1,512,512]{2,1,0:T(8,128)(2,1)}) fusion(bf16[1,512,512]{2,1,0:T(8,128)(2,1)S(1)} %copy-done.5, f32[512,512]{1,0:T(8,128)S(1)} %copy-done.1, bf16[1,512,512]{2,1,0:T(8,128)(2,1)S(1)} %copy-done.6, f32[1,512,512]{2,1,0:T(8,128)S(1)} %copy-done.3, ...), kind=kOutput, calls=%fused_computation.34 | convolution fusion | flops 2152726528 | bytes 13107200 | tf_op jit(solution)/shard_map/dot_general | solution.py:26
  293.5 5.7 %all-to-all-start.1 = ((bf16[16,32,512]{2,1,0:T(8,128)(2,1)}), bf16[16,32,512]{2,1,0:T(8,128)(2,1)S(1)}, u32[]{:S(2)}, u32[]{:S(2)}) async-start(bf16[16,32,512]{2,1,0:T(8,128)(2,1)} %bitcast.9), calls=%async_computation.1 | async-start | bytes 1048576 | tf_op jit(solution)/shard_map/all_to_all | solution.py:41
  299.2 0.0 copy-done.4
  299.2 12.5 %fusion.3 = (f32[256]{0:T(256)S(1)}, f32[256,8192]{1,0:T(8,128)}) fusion(bf16[256,8192]{1,0:T(8,128)(2,1)} %param.10, f32[256]{0:T(256)S(1)} %add_rsqrt_fusion, bf16[8192,512]{1,0:T(8,128)(2,1)} %bitcast.63, bf16[256,512]{1,0:T(8,128)(2,1)S(1)} %copy-done.4, f32[]{:T(128)} %fusion.23, f32[256]{0:T(256)S(1)} %get-tuple-element.26), kind=kOutput, calls=%fused_computation.6 | convolution fusion | flops 2158493440 | bytes 21236740 | tf_op jit(solution)/shard_map/dot_general | solution.py:20
  311.7 0.0 all-to-all-done.1
  311.7 0.1 reduce_sum.42
  311.8 0.8 broadcast_in_dim.6
  312.6 5.7 %all-to-all-start.2 = ((bf16[16,32,512]{2,1,0:T(8,128)(2,1)}), bf16[16,32,512]{2,1,0:T(8,128)(2,1)S(1)}, u32[]{:S(2)}, u32[]{:S(2)}) async-start(bf16[16,32,512]{2,1,0:T(8,128)(2,1)} %broadcast_in_dim.6), calls=%async_computation.2 | async-start | bytes 1048576 | tf_op jit(solution)/shard_map/all_to_all | solution.py:34
  318.4 0.0 copy-start.2
  318.4 6.9 %fusion.6 = bf16[256,8192]{1,0:T(8,128)(2,1)} fusion(f32[256,8192]{1,0:T(8,128)} %get-tuple-element.29, bf16[256,8192]{1,0:T(8,128)(2,1)} %param.10, f32[256]{0:T(256)S(1)} %broadcast_multiply_fusion, f32[256]{0:T(256)S(1)} %add_rsqrt_fusion), kind=kLoop, calls=%fused_computation.9 | loop fusion | flops 12582912 | bytes 16779264 | tf_op jit(solution)/shard_map/convert_element_type | solution.py:83
  325.3 2.6 all-to-all-done.2
  327.9 0.1 convert_multiply_fusion.3
  328.0 0.0 copy-done.2
  328.0 1.7 fusion.12
  (3 shorter events, 0.0 us)
Async XLA Ops:
  7.2 266.7 %all-gather.3.cloned.1.call-start = ((), (), s32[]{:S(2)}) async-start(), calls=%async_computation.3 | async-start | bytes 13647872 | tf_op jit(solution)/shard_map/all_gather | solution.py:64
  286.2 2.2 copy-start
  286.2 2.5 copy-start.1
  286.2 2.8 copy-start.3
  286.2 2.9 copy-start.5
  286.2 3.1 copy-start.6
  289.2 9.9 %copy-start.4 = (bf16[256,512]{1,0:T(8,128)(2,1)S(1)}, bf16[256,512]{1,0:T(8,128)(2,1)}, u32[]{:S(2)}) copy-start(bf16[256,512]{1,0:T(8,128)(2,1)} %param.11) | copy-start | bytes 786436
  293.5 18.2 %all-to-all-start.1 = ((bf16[16,32,512]{2,1,0:T(8,128)(2,1)}), bf16[16,32,512]{2,1,0:T(8,128)(2,1)S(1)}, u32[]{:S(2)}, u32[]{:S(2)}) async-start(bf16[16,32,512]{2,1,0:T(8,128)(2,1)} %bitcast.9), calls=%async_computation.1 | async-start | bytes 1048576 | tf_op jit(solution)/shard_map/all_to_all | solution.py:41
  312.6 15.2 %all-to-all-start.2 = ((bf16[16,32,512]{2,1,0:T(8,128)(2,1)}), bf16[16,32,512]{2,1,0:T(8,128)(2,1)S(1)}, u32[]{:S(2)}, u32[]{:S(2)}) async-start(bf16[16,32,512]{2,1,0:T(8,128)(2,1)} %broadcast_in_dim.6), calls=%async_computation.2 | async-start | bytes 1048576 | tf_op jit(solution)/shard_map/all_to_all | solution.py:34
  318.4 9.6 %copy-start.2 = (f32[512,512]{1,0:T(8,128)S(1)}, f32[512,512]{1,0:T(8,128)}, u32[]{:S(2)}) copy-start(f32[512,512]{1,0:T(8,128)} %param.17) | copy-start | bytes 3145732
Sparse Core Ops, SparseCore 0:
  11.2 262.6 all-gather.2

commit v5 on v4

--- a/solution.py
+++ b/solution.py
@@ -43,6 +43,38 @@
     return gather_rows(partial, axis)
 
 
+def ring_sum_rows(partial, axis):
+    count = lax.axis_size(axis)
+    stations = count // 2
+    me = lax.axis_index(axis)
+    station = me // 2
+    side = me % 2
+    total, width = partial.shape
+    group = total // stations
+    half = width // 2
+    blocks = partial.reshape(stations, group, width)
+    ahead = [(i, ((i // 2 + 1) % stations) * 2 + i % 2) for i in range(count)]
+    behind = [(i, ((i // 2 - 1) % stations) * 2 + i % 2) for i in range(count)]
+
+    def block(index):
+        return lax.dynamic_index_in_dim(blocks, index % stations, 0, keepdims=False)
+
+    forward = block(station - 1)[:, :half]
+    backward = block(station + 1)[:, half:]
+    for step in range(stations - 1):
+        forward = lax.ppermute(forward.astype(jnp.bfloat16), axis, ahead).astype(jnp.float32)
+        backward = lax.ppermute(backward.astype(jnp.bfloat16), axis, behind).astype(jnp.float32)
+        forward = forward + block(station - step - 2)[:, :half]
+        backward = backward + block(station + step + 2)[:, half:]
+    combined = jnp.concatenate([forward, backward], axis=1)
+    rows = group // 2
+    mine = lax.dynamic_slice_in_dim(combined, side * rows, rows, 0)
+    theirs = lax.dynamic_slice_in_dim(combined, (1 - side) * rows, rows, 0)
+    partner = [(i, i ^ 1) for i in range(count)]
+    received = lax.ppermute(theirs.astype(jnp.bfloat16), axis, partner).astype(jnp.float32)
+    return mine + received
+
+
 def per_device(
     activations,
     cotangent,
@@ -60,24 +92,21 @@
     rows, width = weight_low.shape
     tokens = cotangent.shape[0]
     flags = jnp.zeros((16, width), jnp.bfloat16).at[0, :tokens].set(answer.astype(jnp.bfloat16))
-    packed = jnp.concatenate([weight_low, cotangent, flags], axis=0)
+    packed = jnp.concatenate([weight_low, flags], axis=0)
     gathered = lax.all_gather(packed, "fsdp", axis=0, tiled=False)
     values = activations.astype(jnp.float32)
     inverse = lax.rsqrt(jnp.mean(values * values, axis=1, keepdims=True) + norm_eps)
     normed = values * inverse
     normed_low = normed.astype(jnp.bfloat16)
-    columns = lax.all_to_all(normed_low, "fsdp", 1, 0, tiled=True)
-    gathered, columns = lax.optimization_barrier((gathered, columns))
+    kept = (cotangent.astype(jnp.float32) * answer[:, None]).astype(jnp.bfloat16)
+    reduced = ring_sum_rows(contract_first(normed_low, kept), "fsdp")
+    gathered, reduced = lax.optimization_barrier((gathered, reduced))
     count = gathered.shape[0]
     all_weight = gathered[:, :rows].reshape(count * rows, width)
-    all_cotangent = gathered[:, rows : rows + tokens].reshape(count * tokens, width)
-    all_answer = gathered[:, rows + tokens, :tokens].reshape(count * tokens).astype(jnp.float32)
+    all_answer = gathered[:, rows, :tokens].reshape(count * tokens).astype(jnp.float32)
     answers = jnp.sum(all_answer)
-    all_scaled = (
-        all_cotangent.astype(jnp.float32) * all_answer[:, None] / answers
-    ).astype(jnp.bfloat16)
     scaled = (cotangent.astype(jnp.float32) * answer[:, None] / answers).astype(jnp.bfloat16)
-    gradient = width_scale * contract_first(columns, all_scaled)
+    gradient = width_scale * reduced / answers
     feature_grad = width_scale * contract_last(scaled, all_weight)
     projected = jnp.mean(feature_grad * normed, axis=1, keepdims=True)
     input_grad = (inverse * (feature_grad - normed * projected)).astype(jnp.bfloat16)

time: 337 us -> 249 us (0.74)
  blocking collectives: 137 us -> 0 us
  starting transfers between devices: 11.5 us -> 61 us
  waiting for transfers between devices: 121 us -> 95.2 us
  local copies, waits for them, and re-layouts: 12.1 us -> 34 us
  other arithmetic: 23.6 us -> 28.6 us
    all_to_all x1 -> x0, blocking collectives: 137 us -> none  [per_device(): columns = lax.all_to_all(normed_low, 'fsdp', 1, 0, tiled=True)]
    all_gather x1, waiting for transfers between devices: 119 us -> 3.94 us  [per_device(): gathered = lax.all_gather(packed, 'fsdp', axis=0, tiled=False)]
    ppermute x0 -> x15, waiting for transfers between devices: none -> 88.6 us  [the longest x7 79.3 us: ring_sum_rows(): lax.ppermute(backward.astype(jnp.bfloat16), axis, behind)]
    ppermute x0 -> x15, starting transfers between devices: none -> 35.7 us  [the longest x7 27 us: ring_sum_rows(): lax.ppermute(backward.astype(jnp.bfloat16), axis, behind)]
    squeeze x0 -> x2, local copies, waits for them, and re-layouts: none -> 18.7 us  [block(): return lax.dynamic_index_in_dim(blocks, index % stations, 0, keepdims=False)]
    all_to_all x1, starting transfers between devices: 5.69 us -> 19.5 us  [sum_rows(): received = lax.all_to_all(pieces, axis, 0, 0, tiled=True)]
    unnamed x14 -> x40, local copies, waits for them, and re-layouts: 0.85 us -> 6.81 us
    add x0 -> x3, other arithmetic: none -> 3.85 us  [the longest x1 1.47 us: ring_sum_rows(): forward = forward + block(station - step - 2)[:, :half]]
  transfers between devices with their start and end apart: 3 -> 18, of which waited for: 2 -> 11; matrix products, arithmetic and copies ran while one was open for 8% -> 21% of each run, Pallas kernels for 0% -> 0%
where the time goes in v5:
time: 249 us; the launch traced here: 248 us
  waiting for transfers between devices  95.2 us (38%)
  starting transfers between devices  61 us (24%)
  local copies, waits for them, and re-layouts  34 us (14%)
  other arithmetic  28.6 us (11%)
  matrix products  15 us (6%)
  between operations  14.6 us (6%)
    ppermute x7, waiting for transfers between devices, ring_sum_rows(): lax.ppermute(backward.astype(jnp.bfloat16), axis, behind)  79.3 us
    ppermute x7, starting transfers between devices, ring_sum_rows(): lax.ppermute(backward.astype(jnp.bfloat16), axis, behind)  27 us
    all_to_all x1, starting transfers between devices, sum_rows(): received = lax.all_to_all(pieces, axis, 0, 0, tiled=True)  19.5 us
    squeeze x2, local copies, waits for them, and re-layouts, block(): return lax.dynamic_index_in_dim(blocks, index % stations, 0, keepdims=False)  18.7 us
    dot_general x1, matrix products, contract_last(): lax.dot_general(left, right, (((1,), (1,)), ((), ())), preferred_element_...  12.5 us
    ppermute x1, starting transfers between devices, ring_sum_rows(): lax.ppermute(theirs.astype(jnp.bfloat16), axis, partner).astype(jnp.float32)  8.2 us
    slice x1, local copies, waits for them, and re-layouts, per_device(): all_weight = gathered[:, :rows].reshape(count * rows, width)  7.55 us
    convert_element_type x1, other arithmetic, per_device(): (inverse * (feature_grad - normed * projected)).astype(jnp.bfloat16)  6.85 us
  transfers between devices with their start and end apart: 18, of which 11 were waited for; matrix products, arithmetic and copies ran while one was open for 21% of the time, Pallas kernels for 0%

profile of v5, /device:TPU:1, one launch (start us, length us, event | category | flops | bytes accessed | tf_op | source)
XLA Modules:
  0.0 248.4 jit_solution(4658142273218043843)
XLA Ops:
  7.2 0.0 all-gather.3.cloned.1.call-start
  7.2 0.7 compare_convert_fusion
  7.9 1.3 bitcast_convert_fusion
  9.2 0.8 fusion.38
  10.0 0.0 all-gather.3.cloned.1.call-update
  10.1 3.3 %fusion.7 = f32[256]{0:T(256)S(1)} fusion(bf16[256,8192]{1,0:T(8,128)(2,1)} %param.10), kind=kLoop, calls=%fused_computation.10 | loop fusion | flops 6291200 | bytes 4195328 | tf_op jit(solution)/shard_map/reduce_sum | solution.py:98
  13.4 0.2 copy-done.1
  13.6 2.5 %fusion.8 = f32[8192,512]{1,0:T(8,128)S(1)} fusion(bf16[256,8192]{1,0:T(8,128)(2,1)S(1)} %copy-done.1, f32[256]{0:T(256)S(1)} %add_rsqrt_fusion, bf16[256,512]{1,0:T(8,128)(2,1)S(1)} %copy-done.19, f32[256]{0:T(256)S(1)} %get-tuple-element.42), kind=kOutput, calls=%fused_computation.11 | convolution fusion | flops 2154168320 | bytes 21235712 | tf_op jit(solution)/shard_map/dot_general | solution.py:26
  16.1 5.8 %copy-done = f32[8192,512]{1,0:T(8,128)} copy-done((f32[8192,512]{1,0:T(8,128)}, f32[8192,512]{1,0:T(8,128)S(1)}, u32[]{:S(2)}) %copy-start) | copy-done | bytes 16777240
  21.9 0.3 fusion.14
  22.2 6.5 %collective-permute-start.7 = (bf16[1024,256]{1,0:T(8,128)(2,1)S(1)}, bf16[1024,256]{1,0:T(8,128)(2,1)}, u32[]{:S(2)}, u32[]{:S(2)}) collective-permute-start(bf16[1024,256]{1,0:T(8,128)(2,1)S(1)} %slice.98), channel_id=1, source_target_pairs={{0,14},{1,15},{2,0},{3,1},{4,2},{5,3},{6,4},{7,5},{8,6},{9,7},{10,... | collective-permute-start | bytes 1572872 | tf_op jit(solution)/shard_map/ppermute | solution.py:66
  28.7 0.1 collective-permute-start
  29.1 18.4 %dynamic-slice_bitcast_fusion.6 = (f32[1024,512]{1,0:T(8,128)}, f32[1024,512]{1,0:T(8,128)S(1)}, f32[1024,512]{1,0:T(8,128)}, f32[1024,512]{1,0:T(8,128)}, f32[1...) fusion(f32[8,1024,512]{2,1,0:T(8,128)} %bitcast.80, ...), kind=kLoop, calls=%fused_computation.23 | loop fusion | bytes 58720312 | tf_op jit(solution)/shard_map/jit(dynamic_index_in_dim)/squeeze | solution.py:60
  47.5 2.3 collective-permute-done.7
  49.8 1.6 fusion.24
  51.5 3.6 %collective-permute-start.8 = (bf16[1024,256]{1,0:T(8,128)(2,1)S(1)}, bf16[1024,256]{1,0:T(8,128)(2,1)S(1)}, u32[]{:S(2)}, u32[]{:S(2)}) collective-permute-start(bf16[1024,256]{1,0:T(8,128)(2,1)S(1)} %fusion.24), channel_id=1, source_target_pairs={{0,14},{1,15},{2,0},{3,1},{4,2},{5,3},{6,4},{7,5},{8,6},{9,7},{10,... | collective-permute-start | bytes 1572872 | tf_op jit(solution)/shard_map/ppermute | solution.py:66
  55.1 1.4 fusion.30
  56.4 0.1 collective-permute-start.1
  56.5 16.1 %collective-permute-done.8 = bf16[1024,256]{1,0:T(8,128)(2,1)S(1)} collective-permute-done((bf16[1024,256]{1,0:T(8,128)(2,1)S(1)}, bf16[1024,256]{1,0:T(8,128)(2,1)S(1)}, u32[]{:S(2)}, u32[]{:S(2)}) %collective-permute-start.8) | collective-permute-done | bytes 524320 | tf_op jit(solution)/shard_map/ppermute | solution.py:66
  72.6 0.2 fusion.23
  72.8 3.5 %collective-permute-start.9 = (bf16[1024,256]{1,0:T(8,128)(2,1)S(1)}, bf16[1024,256]{1,0:T(8,128)(2,1)S(1)}, u32[]{:S(2)}, u32[]{:S(2)}) collective-permute-start(bf16[1024,256]{1,0:T(8,128)(2,1)S(1)} %fusion.23), channel_id=1, source_target_pairs={{0,14},{1,15},{2,0},{3,1},{4,2},{5,3},{6,4},{7,5},{8,6},{9,7},{10,... | collective-permute-start | bytes 1572872 | tf_op jit(solution)/shard_map/ppermute | solution.py:66
  76.3 0.2 fusion.29
  76.5 0.1 collective-permute-start.2
  76.6 15.7 %collective-permute-done.9 = bf16[1024,256]{1,0:T(8,128)(2,1)S(1)} collective-permute-done((bf16[1024,256]{1,0:T(8,128)(2,1)S(1)}, bf16[1024,256]{1,0:T(8,128)(2,1)S(1)}, u32[]{:S(2)}, u32[]{:S(2)}) %collective-permute-start.9) | collective-permute-done | bytes 524320 | tf_op jit(solution)/shard_map/ppermute | solution.py:66
  92.2 0.2 fusion.22
  92.4 3.8 %collective-permute-start.10 = (bf16[1024,256]{1,0:T(8,128)(2,1)S(1)}, bf16[1024,256]{1,0:T(8,128)(2,1)S(1)}, u32[]{:S(2)}, u32[]{:S(2)}) collective-permute-start(bf16[1024,256]{1,0:T(8,128)(2,1)S(1)} %fusion.22), channel_id=1, source_target_pairs={{0,14},{1,15},{2,0},{3,1},{4,2},{5,3},{6,4},{7,5},{8,6},{9,7},{10,... | collective-permute-start | bytes 1572872 | tf_op jit(solution)/shard_map/ppermute | solution.py:66
  96.2 0.2 fusion.28
  96.4 0.1 collective-permute-start.3
  96.5 9.1 %collective-permute-done.10 = bf16[1024,256]{1,0:T(8,128)(2,1)S(1)} collective-permute-done((bf16[1024,256]{1,0:T(8,128)(2,1)S(1)}, bf16[1024,256]{1,0:T(8,128)(2,1)S(1)}, u32[]{:S(2)}, u32[]{:S(2)}) %collective-permute-start.10) | collective-permute-done | bytes 524320 | tf_op jit(solution)/shard_map/ppermute | solution.py:66
  105.6 0.2 fusion.21
  105.8 3.6 %collective-permute-start.11 = (bf16[1024,256]{1,0:T(8,128)(2,1)S(1)}, bf16[1024,256]{1,0:T(8,128)(2,1)S(1)}, u32[]{:S(2)}, u32[]{:S(2)}) collective-permute-start(bf16[1024,256]{1,0:T(8,128)(2,1)S(1)} %fusion.21), channel_id=1, source_target_pairs={{0,14},{1,15},{2,0},{3,1},{4,2},{5,3},{6,4},{7,5},{8,6},{9,7},{10,... | collective-permute-start | bytes 1572872 | tf_op jit(solution)/shard_map/ppermute | solution.py:66
  109.4 0.2 fusion.27
  109.6 0.1 collective-permute-start.4
  109.7 7.6 %collective-permute-done.11 = bf16[1024,256]{1,0:T(8,128)(2,1)S(1)} collective-permute-done((bf16[1024,256]{1,0:T(8,128)(2,1)S(1)}, bf16[1024,256]{1,0:T(8,128)(2,1)S(1)}, u32[]{:S(2)}, u32[]{:S(2)}) %collective-permute-start.11) | collective-permute-done | bytes 524320 | tf_op jit(solution)/shard_map/ppermute | solution.py:66
  117.3 0.2 fusion.20
  117.5 2.5 collective-permute-start.12
  120.0 0.2 fusion.26
  120.1 0.1 collective-permute-start.5
  120.2 8.2 %collective-permute-done.12 = bf16[1024,256]{1,0:T(8,128)(2,1)S(1)} collective-permute-done((bf16[1024,256]{1,0:T(8,128)(2,1)S(1)}, bf16[1024,256]{1,0:T(8,128)(2,1)S(1)}, u32[]{:S(2)}, u32[]{:S(2)}) %collective-permute-start.12) | collective-permute-done | bytes 524320 | tf_op jit(solution)/shard_map/ppermute | solution.py:66
  128.4 0.2 fusion.19
  128.6 3.6 %collective-permute-start.13 = (bf16[1024,256]{1,0:T(8,128)(2,1)S(1)}, bf16[1024,256]{1,0:T(8,128)(2,1)S(1)}, u32[]{:S(2)}, u32[]{:S(2)}) collective-permute-start(bf16[1024,256]{1,0:T(8,128)(2,1)S(1)} %fusion.19), channel_id=1, source_target_pairs={{0,14},{1,15},{2,0},{3,1},{4,2},{5,3},{6,4},{7,5},{8,6},{9,7},{10,... | collective-permute-start | bytes 1572872 | tf_op jit(solution)/shard_map/ppermute | solution.py:66
  132.2 1.0 fusion.25
  133.2 20.3 %collective-permute-done.13 = bf16[1024,256]{1,0:T(8,128)(2,1)S(1)} collective-permute-done((bf16[1024,256]{1,0:T(8,128)(2,1)S(1)}, bf16[1024,256]{1,0:T(8,128)(2,1)S(1)}, u32[]{:S(2)}, u32[]{:S(2)}) %collective-permute-start.13) | collective-permute-done | bytes 524320 | tf_op jit(solution)/shard_map/ppermute | solution.py:66
  153.4 0.8 copy-done.18
  154.2 1.2 slice_add_fusion
  155.4 2.6 %collective-permute-done.6 = bf16[1024,256]{1,0:T(8,128)(2,1)} collective-permute-done((bf16[1024,256]{1,0:T(8,128)(2,1)}, bf16[1024,256]{1,0:T(8,128)(2,1)}, u32[]{:S(2)}, u32[]{:S(2)}) %collective-permute-start.6) | collective-permute-done | bytes 524320 | tf_op jit(solution)/shard_map/ppermute | solution.py:65
  158.1 1.5 slice_add_fusion.7
  159.5 0.1 fusion.16
  159.6 8.2 %collective-permute-start.14 = (bf16[512,512]{1,0:T(8,128)(2,1)S(1)}, bf16[512,512]{1,0:T(8,128)(2,1)}, u32[]{:S(2)}, u32[]{:S(2)}) collective-permute-start(bf16[512,512]{1,0:T(8,128)(2,1)S(1)} %fusion.16), channel_id=1, source_target_pairs={{0,1},{1,0},{2,3},{3,2},{4,5},{5,4},{6,7},{7,6},{8,9},{9,8},{10,11... | collective-permute-start | bytes 1572872 | tf_op jit(solution)/shard_map/ppermute | solution.py:74
  167.8 6.7 %collective-permute-done.14 = bf16[512,512]{1,0:T(8,128)(2,1)} collective-permute-done((bf16[512,512]{1,0:T(8,128)(2,1)S(1)}, bf16[512,512]{1,0:T(8,128)(2,1)}, u32[]{:S(2)}, u32[]{:S(2)}) %collective-permute-start.14) | collective-permute-done | bytes 524320 | tf_op jit(solution)/shard_map/ppermute | solution.py:74
  174.5 1.2 fusion.18
  175.7 3.9 %all-gather.3.cloned.1.call-done = bf16[8448,512]{1,0:T(8,128)(2,1)} async-done(((bf16[528,512]{1,0:T(8,128)(2,1)}), bf16[8448,512]{1,0:T(8,128)(2,1)}) %all-gather.3.cloned.1.call-update) | async-done | bytes 8650768 | tf_op jit(solution)/shard_map/all_gather | solution.py:96
  179.6 1.5 convert_reduce_fusion
  181.1 7.6 %slice.89 = bf16[16,512,512]{2,1,0:T(8,128)(2,1)} slice(bf16[16,528,512]{2,1,0:T(8,128)(2,1)} %bitcast.83), slice={[0:16], [0:512], [0:512]} | slice | bytes 16777216 | tf_op jit(solution)/shard_map/slice | solution.py:105
  188.7 2.8 %fusion.40 = (bf16[1,512,512]{2,1,0:T(8,128)(2,1)}, bf16[512,512]{1,0:T(8,128)(2,1)}, bf16[1,512,512]{2,1,0:T(8,128)(2,1)}) fusion(bf16[1,512,512]{2,1,0:T(8,128)(2,1)S(1)} %copy-done.16, f32[]{:T(128)} %convert_reduce_fusion, f32[512,512]{1,0:T(8,128)S(1)} %fusion.18, f32[512,512]{1,0:T(8,128)S(1)} %copy-done.13, bf16[1,512,512]{2,1,0:T(8,128)(2,1)S(1)} %copy-done.17, ...), kind=kLoop, calls=%fused_computation.86 | loop fusion | flops 5505024 | bytes 5767172 | tf_op jit(solution)/shard_map/broadcast_in_dim | solution.py:127
  191.5 19.5 %all-to-all-start = ((bf16[16,32,512]{2,1,0:T(8,128)(2,1)}), bf16[16,32,512]{2,1,0:T(8,128)(2,1)S(1)}, u32[]{:S(2)}, u32[]{:S(2)}) async-start(bf16[16,32,512]{2,1,0:T(8,128)(2,1)} %bitcast.22), calls=%async_computation | async-start | bytes 1048576 | tf_op jit(solution)/shard_map/all_to_all | solution.py:41
  211.0 12.5 %fusion.3 = (f32[256]{0:T(256)S(1)}, f32[256,8192]{1,0:T(8,128)}) fusion(bf16[256,8192]{1,0:T(8,128)(2,1)} %param.10, f32[256]{0:T(256)S(1)} %add_rsqrt_fusion, bf16[8192,512]{1,0:T(8,128)(2,1)} %bitcast.81, bf16[256,512]{1,0:T(8,128)(2,1)S(1)} %copy-done.19, f32[]{:T(128)} %convert_reduce_fusion, f32[256]{0:T(256)S(1)} %get-tuple-element.42), kind=kOutput, calls=%fused_computation.6 | convolution fusion | flops 2158493440 | bytes 21236740 | tf_op jit(solution)/shard_map/dot_general | solution.py:20
  223.5 0.1 reduce_sum.42
  223.6 0.8 broadcast_in_dim.6
  224.4 5.7 %all-to-all-start.1 = ((bf16[16,32,512]{2,1,0:T(8,128)(2,1)}), bf16[16,32,512]{2,1,0:T(8,128)(2,1)S(1)}, u32[]{:S(2)}, u32[]{:S(2)}) async-start(bf16[16,32,512]{2,1,0:T(8,128)(2,1)} %broadcast_in_dim.6), calls=%async_computation.1 | async-start | bytes 1048576 | tf_op jit(solution)/shard_map/all_to_all | solution.py:34
  230.2 6.9 %fusion.6 = bf16[256,8192]{1,0:T(8,128)(2,1)} fusion(f32[256,8192]{1,0:T(8,128)} %get-tuple-element.45, bf16[256,8192]{1,0:T(8,128)(2,1)} %param.10, f32[256]{0:T(256)S(1)} %broadcast_multiply_fusion, f32[256]{0:T(256)S(1)} %add_rsqrt_fusion), kind=kLoop, calls=%fused_computation.9 | loop fusion | flops 12582912 | bytes 16779264 | tf_op jit(solution)/shard_map/convert_element_type | solution.py:112
  237.0 2.6 %all-to-all-done.1 = bf16[16,32,512]{2,1,0:T(8,128)(2,1)S(1)} async-done(((bf16[16,32,512]{2,1,0:T(8,128)(2,1)}), bf16[16,32,512]{2,1,0:T(8,128)(2,1)S(1)}, u32[]{:S(2)}, u32[]{:S(2)}) %all-to-all-start.1) | async-done | bytes 524320 | tf_op jit(solution)/shard_map/all_to_all | solution.py:34
  239.7 0.1 convert_multiply_fusion.2
  239.8 1.7 fusion.32
  (50 shorter events, 0.2 us)
Async XLA Ops:
  7.2 172.5 %all-gather.3.cloned.1.call-start = ((), (), s32[]{:S(2)}) async-start(), calls=%async_computation.2 | async-start | bytes 9191424 | tf_op jit(solution)/shard_map/all_gather | solution.py:96
  10.0 3.4 %copy-start.19 = (bf16[256,512]{1,0:T(8,128)(2,1)S(1)}, bf16[256,512]{1,0:T(8,128)(2,1)}, u32[]{:S(2)}) copy-start(bf16[256,512]{1,0:T(8,128)(2,1)} %param.11) | copy-start | bytes 786436
  10.1 3.5 %copy-start.1 = (bf16[256,8192]{1,0:T(8,128)(2,1)S(1)}, bf16[256,8192]{1,0:T(8,128)(2,1)}, u32[]{:S(2)}) copy-start(bf16[256,8192]{1,0:T(8,128)(2,1)} %param.10) | copy-start | bytes 12582916
  16.1 5.8 %copy-start = (f32[8192,512]{1,0:T(8,128)}, f32[8192,512]{1,0:T(8,128)S(1)}, u32[]{:S(2)}) copy-start(f32[8192,512]{1,0:T(8,128)S(1)} %fusion.8) | copy-start | bytes 50331652
  22.2 27.6 %collective-permute-start.7 = (bf16[1024,256]{1,0:T(8,128)(2,1)S(1)}, bf16[1024,256]{1,0:T(8,128)(2,1)}, u32[]{:S(2)}, u32[]{:S(2)}) collective-permute-start(bf16[1024,256]{1,0:T(8,128)(2,1)S(1)} %slice.98), channel_id=1, source_target_pairs={{0,14},{1,15},{2,0},{3,1},{4,2},{5,3},{6,4},{7,5},{8,6},{9,7},{10,... | collective-permute-start | bytes 1572872 | tf_op jit(solution)/shard_map/ppermute | solution.py:66
  28.7 26.3 %collective-permute-start = (bf16[1024,256]{1,0:T(8,128)(2,1)S(1)}, bf16[1024,256]{1,0:T(8,128)(2,1)}, u32[]{:S(2)}, u32[]{:S(2)}) collective-permute-start(bf16[1024,256]{1,0:T(8,128)(2,1)S(1)} %slice.90), channel_id=1, source_target_pairs={{0,2},{1,3},{2,4},{3,5},{4,6},{5,7},{6,8},{7,9},{8,10},{9,11},{10,... | collective-permute-start | bytes 1572872 | tf_op jit(solution)/shard_map/ppermute | solution.py:65
  47.5 7.6 %copy-start.12 = (f32[1024,512]{1,0:T(8,128)S(1)}, f32[1024,512]{1,0:T(8,128)}, u32[]{:S(2)}) copy-start(f32[1024,512]{1,0:T(8,128)} %get-tuple-element.38) | copy-start | bytes 6291460
  49.8 22.8 %copy-start.11 = (f32[1024,512]{1,0:T(8,128)S(1)}, f32[1024,512]{1,0:T(8,128)}, u32[]{:S(2)}) copy-start(f32[1024,512]{1,0:T(8,128)} %get-tuple-element.31) | copy-start | bytes 6291460
  51.5 21.1 %collective-permute-start.8 = (bf16[1024,256]{1,0:T(8,128)(2,1)S(1)}, bf16[1024,256]{1,0:T(8,128)(2,1)S(1)}, u32[]{:S(2)}, u32[]{:S(2)}) collective-permute-start(bf16[1024,256]{1,0:T(8,128)(2,1)S(1)} %fusion.24), channel_id=1, source_target_pairs={{0,14},{1,15},{2,0},{3,1},{4,2},{5,3},{6,4},{7,5},{8,6},{9,7},{10,... | collective-permute-start | bytes 1572872 | tf_op jit(solution)/shard_map/ppermute | solution.py:66
  55.1 21.2 %copy-start.10 = (f32[1024,512]{1,0:T(8,128)S(1)}, f32[1024,512]{1,0:T(8,128)}, u32[]{:S(2)}) copy-start(f32[1024,512]{1,0:T(8,128)} %get-tuple-element.37) | copy-start | bytes 6291460
  56.4 19.8 %collective-permute-start.1 = (bf16[1024,256]{1,0:T(8,128)(2,1)S(1)}, bf16[1024,256]{1,0:T(8,128)(2,1)S(1)}, u32[]{:S(2)}, u32[]{:S(2)}) collective-permute-start(bf16[1024,256]{1,0:T(8,128)(2,1)S(1)} %fusion.30), channel_id=1, source_target_pairs={{0,2},{1,3},{2,4},{3,5},{4,6},{5,7},{6,8},{7,9},{8,10},{9,11},{10,... | collective-permute-start | bytes 1572872 | tf_op jit(solution)/shard_map/ppermute | solution.py:65
  72.6 19.6 %copy-start.9 = (f32[1024,512]{1,0:T(8,128)S(1)}, f32[1024,512]{1,0:T(8,128)}, u32[]{:S(2)}) copy-start(f32[1024,512]{1,0:T(8,128)} %get-tuple-element.30) | copy-start | bytes 6291460
  72.8 19.4 %collective-permute-start.9 = (bf16[1024,256]{1,0:T(8,128)(2,1)S(1)}, bf16[1024,256]{1,0:T(8,128)(2,1)S(1)}, u32[]{:S(2)}, u32[]{:S(2)}) collective-permute-start(bf16[1024,256]{1,0:T(8,128)(2,1)S(1)} %fusion.23), channel_id=1, source_target_pairs={{0,14},{1,15},{2,0},{3,1},{4,2},{5,3},{6,4},{7,5},{8,6},{9,7},{10,... | collective-permute-start | bytes 1572872 | tf_op jit(solution)/shard_map/ppermute | solution.py:66
  76.3 19.9 %copy-start.8 = (f32[1024,512]{1,0:T(8,128)S(1)}, f32[1024,512]{1,0:T(8,128)}, u32[]{:S(2)}) copy-start(f32[1024,512]{1,0:T(8,128)} %get-tuple-element.36) | copy-start | bytes 6291460
  76.5 19.7 %collective-permute-start.2 = (bf16[1024,256]{1,0:T(8,128)(2,1)S(1)}, bf16[1024,256]{1,0:T(8,128)(2,1)S(1)}, u32[]{:S(2)}, u32[]{:S(2)}) collective-permute-start(bf16[1024,256]{1,0:T(8,128)(2,1)S(1)} %fusion.29), channel_id=1, source_target_pairs={{0,2},{1,3},{2,4},{3,5},{4,6},{5,7},{6,8},{7,9},{8,10},{9,11},{10,... | collective-permute-start | bytes 1572872 | tf_op jit(solution)/shard_map/ppermute | solution.py:65
  92.2 13.4 %copy-start.7 = (f32[1024,512]{1,0:T(8,128)S(1)}, f32[1024,512]{1,0:T(8,128)}, u32[]{:S(2)}) copy-start(f32[1024,512]{1,0:T(8,128)} %get-tuple-element.29) | copy-start | bytes 6291460
  92.4 13.2 %collective-permute-start.10 = (bf16[1024,256]{1,0:T(8,128)(2,1)S(1)}, bf16[1024,256]{1,0:T(8,128)(2,1)S(1)}, u32[]{:S(2)}, u32[]{:S(2)}) collective-permute-start(bf16[1024,256]{1,0:T(8,128)(2,1)S(1)} %fusion.22), channel_id=1, source_target_pairs={{0,14},{1,15},{2,0},{3,1},{4,2},{5,3},{6,4},{7,5},{8,6},{9,7},{10,... | collective-permute-start | bytes 1572872 | tf_op jit(solution)/shard_map/ppermute | solution.py:66
  96.2 13.2 %copy-start.6 = (f32[1024,512]{1,0:T(8,128)S(1)}, f32[1024,512]{1,0:T(8,128)}, u32[]{:S(2)}) copy-start(f32[1024,512]{1,0:T(8,128)} %get-tuple-element.35) | copy-start | bytes 6291460
  96.4 13.0 %collective-permute-start.3 = (bf16[1024,256]{1,0:T(8,128)(2,1)S(1)}, bf16[1024,256]{1,0:T(8,128)(2,1)S(1)}, u32[]{:S(2)}, u32[]{:S(2)}) collective-permute-start(bf16[1024,256]{1,0:T(8,128)(2,1)S(1)} %fusion.28), channel_id=1, source_target_pairs={{0,2},{1,3},{2,4},{3,5},{4,6},{5,7},{6,8},{7,9},{8,10},{9,11},{10,... | collective-permute-start | bytes 1572872 | tf_op jit(solution)/shard_map/ppermute | solution.py:65
  105.6 11.7 %copy-start.5 = (f32[1024,512]{1,0:T(8,128)S(1)}, f32[1024,512]{1,0:T(8,128)}, u32[]{:S(2)}) copy-start(f32[1024,512]{1,0:T(8,128)} %get-tuple-element.28) | copy-start | bytes 6291460
  105.8 11.5 %collective-permute-start.11 = (bf16[1024,256]{1,0:T(8,128)(2,1)S(1)}, bf16[1024,256]{1,0:T(8,128)(2,1)S(1)}, u32[]{:S(2)}, u32[]{:S(2)}) collective-permute-start(bf16[1024,256]{1,0:T(8,128)(2,1)S(1)} %fusion.21), channel_id=1, source_target_pairs={{0,14},{1,15},{2,0},{3,1},{4,2},{5,3},{6,4},{7,5},{8,6},{9,7},{10,... | collective-permute-start | bytes 1572872 | tf_op jit(solution)/shard_map/ppermute | solution.py:66
  109.4 10.6 %copy-start.4 = (f32[1024,512]{1,0:T(8,128)S(1)}, f32[1024,512]{1,0:T(8,128)}, u32[]{:S(2)}) copy-start(f32[1024,512]{1,0:T(8,128)} %get-tuple-element.34) | copy-start | bytes 6291460
  109.6 10.4 %collective-permute-start.4 = (bf16[1024,256]{1,0:T(8,128)(2,1)S(1)}, bf16[1024,256]{1,0:T(8,128)(2,1)S(1)}, u32[]{:S(2)}, u32[]{:S(2)}) collective-permute-start(bf16[1024,256]{1,0:T(8,128)(2,1)S(1)} %fusion.27), channel_id=1, source_target_pairs={{0,2},{1,3},{2,4},{3,5},{4,6},{5,7},{6,8},{7,9},{8,10},{9,11},{10,... | collective-permute-start | bytes 1572872 | tf_op jit(solution)/shard_map/ppermute | solution.py:65
  117.3 11.1 %copy-start.3 = (f32[1024,512]{1,0:T(8,128)S(1)}, f32[1024,512]{1,0:T(8,128)}, u32[]{:S(2)}) copy-start(f32[1024,512]{1,0:T(8,128)} %get-tuple-element.27) | copy-start | bytes 6291460
  117.5 10.9 %collective-permute-start.12 = (bf16[1024,256]{1,0:T(8,128)(2,1)S(1)}, bf16[1024,256]{1,0:T(8,128)(2,1)S(1)}, u32[]{:S(2)}, u32[]{:S(2)}) collective-permute-start(bf16[1024,256]{1,0:T(8,128)(2,1)S(1)} %fusion.20), channel_id=1, source_target_pairs={{0,14},{1,15},{2,0},{3,1},{4,2},{5,3},{6,4},{7,5},{8,6},{9,7},{10,... | collective-permute-start | bytes 1572872 | tf_op jit(solution)/shard_map/ppermute | solution.py:66
  120.0 12.2 %copy-start.2 = (f32[1024,512]{1,0:T(8,128)S(1)}, f32[1024,512]{1,0:T(8,128)}, u32[]{:S(2)}) copy-start(f32[1024,512]{1,0:T(8,128)} %get-tuple-element.33) | copy-start | bytes 6291460
  120.1 12.0 %collective-permute-start.5 = (bf16[1024,256]{1,0:T(8,128)(2,1)S(1)}, bf16[1024,256]{1,0:T(8,128)(2,1)S(1)}, u32[]{:S(2)}, u32[]{:S(2)}) collective-permute-start(bf16[1024,256]{1,0:T(8,128)(2,1)S(1)} %fusion.26), channel_id=1, source_target_pairs={{0,2},{1,3},{2,4},{3,5},{4,6},{5,7},{6,8},{7,9},{8,10},{9,11},{10,... | collective-permute-start | bytes 1572872 | tf_op jit(solution)/shard_map/ppermute | solution.py:65
  128.6 24.8 %collective-permute-start.13 = (bf16[1024,256]{1,0:T(8,128)(2,1)S(1)}, bf16[1024,256]{1,0:T(8,128)(2,1)S(1)}, u32[]{:S(2)}, u32[]{:S(2)}) collective-permute-start(bf16[1024,256]{1,0:T(8,128)(2,1)S(1)} %fusion.19), channel_id=1, source_target_pairs={{0,14},{1,15},{2,0},{3,1},{4,2},{5,3},{6,4},{7,5},{8,6},{9,7},{10,... | collective-permute-start | bytes 1572872 | tf_op jit(solution)/shard_map/ppermute | solution.py:66
  133.2 24.9 %collective-permute-start.6 = (bf16[1024,256]{1,0:T(8,128)(2,1)}, bf16[1024,256]{1,0:T(8,128)(2,1)}, u32[]{:S(2)}, u32[]{:S(2)}) collective-permute-start(bf16[1024,256]{1,0:T(8,128)(2,1)} %fusion.25), channel_id=1, source_target_pairs={{0,2},{1,3},{2,4},{3,5},{4,6},{5,7},{6,8},{7,9},{8,10},{9,11},{10,... | collective-permute-start | bytes 1572872 | tf_op jit(solution)/shard_map/ppermute | solution.py:65
  153.4 0.8 copy-start.18
  159.6 14.9 %collective-permute-start.14 = (bf16[512,512]{1,0:T(8,128)(2,1)S(1)}, bf16[512,512]{1,0:T(8,128)(2,1)}, u32[]{:S(2)}, u32[]{:S(2)}) collective-permute-start(bf16[512,512]{1,0:T(8,128)(2,1)S(1)} %fusion.16), channel_id=1, source_target_pairs={{0,1},{1,0},{2,3},{3,2},{4,5},{5,4},{6,7},{7,6},{8,9},{9,8},{10,11... | collective-permute-start | bytes 1572872 | tf_op jit(solution)/shard_map/ppermute | solution.py:74
  181.1 7.6 %copy-start.13 = (f32[512,512]{1,0:T(8,128)S(1)}, f32[512,512]{1,0:T(8,128)}, u32[]{:S(2)}) copy-start(f32[512,512]{1,0:T(8,128)} %param.16) | copy-start | bytes 3145732
  181.1 7.6 %copy-start.14 = (f32[1,512,512]{2,1,0:T(8,128)S(1)}, f32[1,512,512]{2,1,0:T(8,128)}, u32[]{:S(2)}) copy-start(f32[1,512,512]{2,1,0:T(8,128)} %param.13) | copy-start | bytes 3145732
  181.1 7.6 %copy-start.16 = (bf16[1,512,512]{2,1,0:T(8,128)(2,1)S(1)}, bf16[1,512,512]{2,1,0:T(8,128)(2,1)}, u32[]{:S(2)}) copy-start(bf16[1,512,512]{2,1,0:T(8,128)(2,1)} %param.15) | copy-start | bytes 1572868
  181.1 7.6 %copy-start.17 = (bf16[1,512,512]{2,1,0:T(8,128)(2,1)S(1)}, bf16[1,512,512]{2,1,0:T(8,128)(2,1)}, u32[]{:S(2)}) copy-start(bf16[1,512,512]{2,1,0:T(8,128)(2,1)} %param.14) | copy-start | bytes 1572868
  191.5 32.0 %all-to-all-start = ((bf16[16,32,512]{2,1,0:T(8,128)(2,1)}), bf16[16,32,512]{2,1,0:T(8,128)(2,1)S(1)}, u32[]{:S(2)}, u32[]{:S(2)}) async-start(bf16[16,32,512]{2,1,0:T(8,128)(2,1)} %bitcast.22), calls=%async_computation | async-start | bytes 1048576 | tf_op jit(solution)/shard_map/all_to_all | solution.py:41
  224.4 15.2 %all-to-all-start.1 = ((bf16[16,32,512]{2,1,0:T(8,128)(2,1)}), bf16[16,32,512]{2,1,0:T(8,128)(2,1)S(1)}, u32[]{:S(2)}, u32[]{:S(2)}) async-start(bf16[16,32,512]{2,1,0:T(8,128)(2,1)} %broadcast_in_dim.6), calls=%async_computation.1 | async-start | bytes 1048576 | tf_op jit(solution)/shard_map/all_to_all | solution.py:34
  237.0 2.8 %copy-start.15 = (f32[512,512]{1,0:T(8,128)S(1)}, f32[512,512]{1,0:T(8,128)}, u32[]{:S(2)}) copy-start(f32[512,512]{1,0:T(8,128)} %param.17) | copy-start | bytes 3145732
Sparse Core Ops, SparseCore 0:
  11.1 168.4 all-gather.2

commit v6 on v5

--- a/solution.py
+++ b/solution.py
@@ -43,29 +43,33 @@
     return gather_rows(partial, axis)
 
 
-def ring_sum_rows(partial, axis):
+def ring_sum_rows(normed_low, kept, axis):
     count = lax.axis_size(axis)
     stations = count // 2
     me = lax.axis_index(axis)
     station = me // 2
     side = me % 2
-    total, width = partial.shape
-    group = total // stations
+    features = normed_low.shape[1]
+    width = kept.shape[1]
+    group = features // stations
     half = width // 2
-    blocks = partial.reshape(stations, group, width)
     ahead = [(i, ((i // 2 + 1) % stations) * 2 + i % 2) for i in range(count)]
     behind = [(i, ((i // 2 - 1) % stations) * 2 + i % 2) for i in range(count)]
+    kept_forward = kept[:, :half]
+    kept_backward = kept[:, half:]
 
-    def block(index):
-        return lax.dynamic_index_in_dim(blocks, index % stations, 0, keepdims=False)
+    def block(index, right):
+        start = pl_multiple((index % stations) * group, group)
+        piece = lax.dynamic_slice_in_dim(normed_low, start, group, 1)
+        return contract_first(piece, right)
 
-    forward = block(station - 1)[:, :half]
-    backward = block(station + 1)[:, half:]
+    forward = block(station - 1, kept_forward)
+    backward = block(station + 1, kept_backward)
     for step in range(stations - 1):
         forward = lax.ppermute(forward.astype(jnp.bfloat16), axis, ahead).astype(jnp.float32)
         backward = lax.ppermute(backward.astype(jnp.bfloat16), axis, behind).astype(jnp.float32)
-        forward = forward + block(station - step - 2)[:, :half]
-        backward = backward + block(station + step + 2)[:, half:]
+        forward = forward + block(station - step - 2, kept_forward)
+        backward = backward + block(station + step + 2, kept_backward)
     combined = jnp.concatenate([forward, backward], axis=1)
     rows = group // 2
     mine = lax.dynamic_slice_in_dim(combined, side * rows, rows, 0)
@@ -73,6 +77,10 @@
     partner = [(i, i ^ 1) for i in range(count)]
     received = lax.ppermute(theirs.astype(jnp.bfloat16), axis, partner).astype(jnp.float32)
     return mine + received
+
+
+def pl_multiple(value, step):
+    return (value // step) * step
 
 
 def per_device(
@@ -99,7 +107,7 @@
     normed = values * inverse
     normed_low = normed.astype(jnp.bfloat16)
     kept = (cotangent.astype(jnp.float32) * answer[:, None]).astype(jnp.bfloat16)
-    reduced = ring_sum_rows(contract_first(normed_low, kept), "fsdp")
+    reduced = ring_sum_rows(normed_low, kept, "fsdp")
     gathered, reduced = lax.optimization_barrier((gathered, reduced))
     count = gathered.shape[0]
     all_weight = gathered[:, :rows].reshape(count * rows, width)

time: 249 us -> 241 us (0.968)
  local copies, waits for them, and re-layouts: 34 us -> 10.5 us
  matrix products: 15 us -> 34.6 us
  other arithmetic: 28.6 us -> 24.1 us
  starting transfers between devices: 61 us -> 57.4 us
  waiting for transfers between devices: 95.2 us -> 98.7 us
    dot_general x1 -> x16, matrix products: 2.54 us -> 22 us  [contract_first(): lax.dot_general(left, right, (((0,), (0,)), ((), ())), preferred_element_...]
    squeeze x2 -> x0, local copies, waits for them, and re-layouts: 18.7 us -> none  [block(): return lax.dynamic_index_in_dim(blocks, index % stations, 0, keepdims=False)]
    unnamed x40 -> x26, local copies, waits for them, and re-layouts: 6.81 us -> 2.12 us
    all_gather x1, waiting for transfers between devices: 3.94 us -> 7.59 us  [per_device(): gathered = lax.all_gather(packed, 'fsdp', axis=0, tiled=False)]
    convert_element_type x6 -> x5, other arithmetic: 3.06 us -> 0.57 us  [ring_sum_rows(): forward.astype(jnp.bfloat16)]
where the time goes in v6:
time: 241 us; the launch traced here: 240 us
  waiting for transfers between devices  98.7 us (41%)
  starting transfers between devices  57.4 us (24%)
  matrix products  34.6 us (14%)
  other arithmetic  24.1 us (10%)
  between operations  14.5 us (6%)
  local copies, waits for them, and re-layouts  10.5 us (4%)
    ppermute x7, waiting for transfers between devices, ring_sum_rows(): lax.ppermute(backward.astype(jnp.bfloat16), axis, behind)  77.6 us
    ppermute x7, starting transfers between devices, ring_sum_rows(): lax.ppermute(backward.astype(jnp.bfloat16), axis, behind)  27.9 us
    dot_general x16, matrix products, contract_first(): lax.dot_general(left, right, (((0,), (0,)), ((), ())), preferred_element_...  22 us
    all_to_all x1, starting transfers between devices, sum_rows(): received = lax.all_to_all(pieces, axis, 0, 0, tiled=True)  17.2 us
    dot_general x1, matrix products, contract_last(): lax.dot_general(left, right, (((1,), (1,)), ((), ())), preferred_element_...  12.6 us
    all_gather x1, waiting for transfers between devices, per_device(): gathered = lax.all_gather(packed, 'fsdp', axis=0, tiled=False)  7.59 us
    slice x1, local copies, waits for them, and re-layouts, per_device(): all_weight = gathered[:, :rows].reshape(count * rows, width)  7.52 us
    convert_element_type x1, other arithmetic, per_device(): (inverse * (feature_grad - normed * projected)).astype(jnp.bfloat16)  6.93 us
  transfers between devices with their start and end apart: 18, of which 11 were waited for; matrix products, arithmetic and copies ran while one was open for 21% of the time, Pallas kernels for 0%

profile of v6, /device:TPU:1, one launch (start us, length us, event | category | flops | bytes accessed | tf_op | source)
XLA Modules:
  0.0 239.7 jit_solution(13242813181913729152)
XLA Ops:
  7.2 0.7 compare_convert_fusion
  7.9 1.3 bitcast_convert_fusion
  9.2 0.8 fusion.21
  10.2 3.3 %fusion.7 = f32[256]{0:T(256)S(1)} fusion(bf16[256,8192]{1,0:T(8,128)(2,1)} %param.10), kind=kLoop, calls=%fused_computation.10 | loop fusion | flops 6291200 | bytes 4195328 | tf_op jit(solution)/shard_map/reduce_sum | solution.py:106
  13.5 0.1 fusion.59
  13.6 1.1 fusion.2
  14.8 2.0 copy-done
  16.8 1.1 convolution_convert_fusion
  17.9 6.4 %collective-permute-start.7 = (bf16[1024,256]{1,0:T(8,128)(2,1)}, bf16[1024,256]{1,0:T(8,128)(2,1)}, u32[]{:S(2)}, u32[]{:S(2)}) collective-permute-start(bf16[1024,256]{1,0:T(8,128)(2,1)} %convolution_convert_fusion), channel_id=1, source_target_pairs={{0,14},{1,15},{2,0},{3,1},{4,2},{5,3},{6,4},{7,5},{8,6},{9,7},{10,... | collective-permute-start | bytes 1572872 | tf_op jit(solution)/shard_map/ppermute | solution.py:70
  24.3 2.2 convolution_convert_fusion.1
  26.5 1.4 fusion.35
  27.9 1.5 fusion.33
  29.4 1.4 fusion.31
  30.9 2.4 fusion.29
  33.3 2.4 fusion.27
  35.7 5.7 %collective-permute-done.7 = bf16[1024,256]{1,0:T(8,128)(2,1)} collective-permute-done((bf16[1024,256]{1,0:T(8,128)(2,1)}, bf16[1024,256]{1,0:T(8,128)(2,1)}, u32[]{:S(2)}, u32[]{:S(2)}) %collective-permute-start.7) | collective-permute-done | bytes 524320 | tf_op jit(solution)/shard_map/ppermute | solution.py:70
  41.4 2.3 add_convert_fusion.5
  43.7 3.5 %collective-permute-start.8 = (bf16[1024,256]{1,0:T(8,128)(2,1)}, bf16[1024,256]{1,0:T(8,128)(2,1)}, u32[]{:S(2)}, u32[]{:S(2)}) collective-permute-start(bf16[1024,256]{1,0:T(8,128)(2,1)} %add_convert_fusion.5), channel_id=1, source_target_pairs={{0,14},{1,15},{2,0},{3,1},{4,2},{5,3},{6,4},{7,5},{8,6},{9,7},{10,... | collective-permute-start | bytes 1572872 | tf_op jit(solution)/shard_map/ppermute | solution.py:70
  47.2 2.4 fusion.25
  49.6 1.7 add_convert_fusion.11
  51.4 1.4 fusion.52
  52.8 14.4 %collective-permute-done.8 = bf16[1024,256]{1,0:T(8,128)(2,1)} collective-permute-done((bf16[1024,256]{1,0:T(8,128)(2,1)}, bf16[1024,256]{1,0:T(8,128)(2,1)}, u32[]{:S(2)}, u32[]{:S(2)}) %collective-permute-start.8) | collective-permute-done | bytes 524320 | tf_op jit(solution)/shard_map/ppermute | solution.py:70
  67.2 1.2 add_convert_fusion.4
  68.3 3.5 %collective-permute-start.9 = (bf16[1024,256]{1,0:T(8,128)(2,1)S(1)}, bf16[1024,256]{1,0:T(8,128)(2,1)S(1)}, u32[]{:S(2)}, u32[]{:S(2)}) collective-permute-start(bf16[1024,256]{1,0:T(8,128)(2,1)S(1)} %add_convert_fusion.4), channel_id=1, source_target_pairs={{0,14},{1,15},{2,0},{3,1},{4,2},{5,3},{6,4},{7,5},{8,6},{9,7},{10,... | collective-permute-start | bytes 1572872 | tf_op jit(solution)/shard_map/ppermute | solution.py:70
  71.8 0.1 add_convert_fusion.10
  71.9 0.4 collective-permute-start.2
  72.3 0.4 fusion.50
  72.7 8.3 %collective-permute-done.9 = bf16[1024,256]{1,0:T(8,128)(2,1)S(1)} collective-permute-done((bf16[1024,256]{1,0:T(8,128)(2,1)S(1)}, bf16[1024,256]{1,0:T(8,128)(2,1)S(1)}, u32[]{:S(2)}, u32[]{:S(2)}) %collective-permute-start.9) | collective-permute-done | bytes 524320 | tf_op jit(solution)/shard_map/ppermute | solution.py:70
  80.9 0.1 add_convert_fusion.3
  81.1 3.8 %collective-permute-start.10 = (bf16[1024,256]{1,0:T(8,128)(2,1)S(1)}, bf16[1024,256]{1,0:T(8,128)(2,1)S(1)}, u32[]{:S(2)}, u32[]{:S(2)}) collective-permute-start(bf16[1024,256]{1,0:T(8,128)(2,1)S(1)} %add_convert_fusion.3), channel_id=1, source_target_pairs={{0,14},{1,15},{2,0},{3,1},{4,2},{5,3},{6,4},{7,5},{8,6},{9,7},{10,... | collective-permute-start | bytes 1572872 | tf_op jit(solution)/shard_map/ppermute | solution.py:70
  84.8 0.1 add_convert_fusion.9
  85.1 0.4 fusion.48
  85.4 12.4 %collective-permute-done.10 = bf16[1024,256]{1,0:T(8,128)(2,1)S(1)} collective-permute-done((bf16[1024,256]{1,0:T(8,128)(2,1)S(1)}, bf16[1024,256]{1,0:T(8,128)(2,1)S(1)}, u32[]{:S(2)}, u32[]{:S(2)}) %collective-permute-start.10) | collective-permute-done | bytes 524320 | tf_op jit(solution)/shard_map/ppermute | solution.py:70
  97.9 0.1 add_convert_fusion.2
  98.0 3.6 %collective-permute-start.11 = (bf16[1024,256]{1,0:T(8,128)(2,1)S(1)}, bf16[1024,256]{1,0:T(8,128)(2,1)S(1)}, u32[]{:S(2)}, u32[]{:S(2)}) collective-permute-start(bf16[1024,256]{1,0:T(8,128)(2,1)S(1)} %add_convert_fusion.2), channel_id=1, source_target_pairs={{0,14},{1,15},{2,0},{3,1},{4,2},{5,3},{6,4},{7,5},{8,6},{9,7},{10,... | collective-permute-start | bytes 1572872 | tf_op jit(solution)/shard_map/ppermute | solution.py:70
  101.6 0.1 add_convert_fusion.8
  101.8 0.4 fusion.46
  102.2 9.1 %collective-permute-done.11 = bf16[1024,256]{1,0:T(8,128)(2,1)S(1)} collective-permute-done((bf16[1024,256]{1,0:T(8,128)(2,1)S(1)}, bf16[1024,256]{1,0:T(8,128)(2,1)S(1)}, u32[]{:S(2)}, u32[]{:S(2)}) %collective-permute-start.11) | collective-permute-done | bytes 524320 | tf_op jit(solution)/shard_map/ppermute | solution.py:70
  111.2 0.1 add_convert_fusion.1
  111.4 3.6 %collective-permute-start.12 = (bf16[1024,256]{1,0:T(8,128)(2,1)S(1)}, bf16[1024,256]{1,0:T(8,128)(2,1)S(1)}, u32[]{:S(2)}, u32[]{:S(2)}) collective-permute-start(bf16[1024,256]{1,0:T(8,128)(2,1)S(1)} %add_convert_fusion.1), channel_id=1, source_target_pairs={{0,14},{1,15},{2,0},{3,1},{4,2},{5,3},{6,4},{7,5},{8,6},{9,7},{10,... | collective-permute-start | bytes 1572872 | tf_op jit(solution)/shard_map/ppermute | solution.py:70
  115.0 0.1 add_convert_fusion.7
  115.2 0.4 fusion.44
  115.5 9.1 %collective-permute-done.12 = bf16[1024,256]{1,0:T(8,128)(2,1)S(1)} collective-permute-done((bf16[1024,256]{1,0:T(8,128)(2,1)S(1)}, bf16[1024,256]{1,0:T(8,128)(2,1)S(1)}, u32[]{:S(2)}, u32[]{:S(2)}) %collective-permute-start.12) | collective-permute-done | bytes 524320 | tf_op jit(solution)/shard_map/ppermute | solution.py:70
  124.6 0.1 add_convert_fusion
  124.7 3.6 %collective-permute-start.13 = (bf16[1024,256]{1,0:T(8,128)(2,1)S(1)}, bf16[1024,256]{1,0:T(8,128)(2,1)S(1)}, u32[]{:S(2)}, u32[]{:S(2)}) collective-permute-start(bf16[1024,256]{1,0:T(8,128)(2,1)S(1)} %add_convert_fusion), channel_id=1, source_target_pairs={{0,14},{1,15},{2,0},{3,1},{4,2},{5,3},{6,4},{7,5},{8,6},{9,7},{10,... | collective-permute-start | bytes 1572872 | tf_op jit(solution)/shard_map/ppermute | solution.py:70
  128.3 0.1 add_convert_fusion.6
  128.6 0.4 fusion.42
  128.9 18.6 %collective-permute-done.13 = bf16[1024,256]{1,0:T(8,128)(2,1)S(1)} collective-permute-done((bf16[1024,256]{1,0:T(8,128)(2,1)S(1)}, bf16[1024,256]{1,0:T(8,128)(2,1)S(1)}, u32[]{:S(2)}, u32[]{:S(2)}) %collective-permute-start.13) | collective-permute-done | bytes 524320 | tf_op jit(solution)/shard_map/ppermute | solution.py:70
  147.6 4.2 %collective-permute-done.6 = bf16[1024,256]{1,0:T(8,128)(2,1)S(1)} collective-permute-done((bf16[1024,256]{1,0:T(8,128)(2,1)S(1)}, bf16[1024,256]{1,0:T(8,128)(2,1)S(1)}, u32[]{:S(2)}, u32[]{:S(2)}) %collective-permute-start.6) | collective-permute-done | bytes 524320 | tf_op jit(solution)/shard_map/ppermute | solution.py:69
  152.0 5.8 %collective-permute-start.14 = (bf16[512,512]{1,0:T(8,128)(2,1)S(1)}, bf16[512,512]{1,0:T(8,128)(2,1)}, u32[]{:S(2)}, u32[]{:S(2)}) collective-permute-start(bf16[512,512]{1,0:T(8,128)(2,1)S(1)} %fusion.11), channel_id=1, source_target_pairs={{0,1},{1,0},{2,3},{3,2},{4,5},{5,4},{6,7},{7,6},{8,9},{9,8},{10,11... | collective-permute-start | bytes 1572872 | tf_op jit(solution)/shard_map/ppermute | solution.py:78
  157.7 6.7 %collective-permute-done.14 = bf16[512,512]{1,0:T(8,128)(2,1)} collective-permute-done((bf16[512,512]{1,0:T(8,128)(2,1)S(1)}, bf16[512,512]{1,0:T(8,128)(2,1)}, u32[]{:S(2)}, u32[]{:S(2)}) %collective-permute-start.14) | collective-permute-done | bytes 524320 | tf_op jit(solution)/shard_map/ppermute | solution.py:78
  164.4 1.2 fusion.13
  165.6 7.6 %all-gather.3.cloned.1.call-done = bf16[8448,512]{1,0:T(8,128)(2,1)} async-done(((bf16[528,512]{1,0:T(8,128)(2,1)}), bf16[8448,512]{1,0:T(8,128)(2,1)}) %all-gather.3.cloned.1.call-update) | async-done | bytes 8650768 | tf_op jit(solution)/shard_map/all_gather | solution.py:104
  173.2 1.5 convert_reduce_fusion
  174.7 7.5 %slice.31 = bf16[16,512,512]{2,1,0:T(8,128)(2,1)} slice(bf16[16,528,512]{2,1,0:T(8,128)(2,1)} %bitcast.48), slice={[0:16], [0:512], [0:512]} | slice | bytes 16777216 | tf_op jit(solution)/shard_map/slice | solution.py:113
  182.3 2.8 %fusion.23 = (bf16[1,512,512]{2,1,0:T(8,128)(2,1)}, bf16[512,512]{1,0:T(8,128)(2,1)}, bf16[1,512,512]{2,1,0:T(8,128)(2,1)}) fusion(bf16[1,512,512]{2,1,0:T(8,128)(2,1)S(1)} %copy-done.9, f32[]{:T(128)} %convert_reduce_fusion, f32[512,512]{1,0:T(8,128)S(1)} %fusion.13, f32[512,512]{1,0:T(8,128)S(1)} %copy-done.6, bf16[1,512,512]{2,1,0:T(8,128)(2,1)S(1)} %copy-done.10, ...), kind=kLoop, calls=%fused_computation.56 | loop fusion | flops 5505024 | bytes 5767172 | tf_op jit(solution)/shard_map/broadcast_in_dim | solution.py:135
  185.1 17.2 %all-to-all-start = ((bf16[16,32,512]{2,1,0:T(8,128)(2,1)}), bf16[16,32,512]{2,1,0:T(8,128)(2,1)S(1)}, u32[]{:S(2)}, u32[]{:S(2)}) async-start(bf16[16,32,512]{2,1,0:T(8,128)(2,1)} %bitcast.5), calls=%async_computation | async-start | bytes 1048576 | tf_op jit(solution)/shard_map/all_to_all | solution.py:41
  202.3 12.6 %fusion.3 = (f32[256]{0:T(256)S(1)}, f32[256,8192]{1,0:T(8,128)}) fusion(bf16[256,8192]{1,0:T(8,128)(2,1)} %param.10, f32[256]{0:T(256)S(1)} %add_rsqrt_fusion, bf16[8192,512]{1,0:T(8,128)(2,1)} %bitcast.46, bf16[256,512]{1,0:T(8,128)(2,1)S(1)} %copy-done.12, f32[]{:T(128)} %convert_reduce_fusion, f32[256]{0:T(256)S(1)} %get-tuple-element.26), kind=kOutput, calls=%fused_computation.6 | convolution fusion | flops 2158493440 | bytes 21236740 | tf_op jit(solution)/shard_map/dot_general | solution.py:20
  215.0 0.8 broadcast_in_dim.6
  215.8 5.7 %all-to-all-start.1 = ((bf16[16,32,512]{2,1,0:T(8,128)(2,1)}), bf16[16,32,512]{2,1,0:T(8,128)(2,1)S(1)}, u32[]{:S(2)}, u32[]{:S(2)}) async-start(bf16[16,32,512]{2,1,0:T(8,128)(2,1)} %broadcast_in_dim.6), calls=%async_computation.1 | async-start | bytes 1048576 | tf_op jit(solution)/shard_map/all_to_all | solution.py:34
  221.5 6.9 %fusion.6 = bf16[256,8192]{1,0:T(8,128)(2,1)} fusion(f32[256,8192]{1,0:T(8,128)} %get-tuple-element.29, bf16[256,8192]{1,0:T(8,128)(2,1)} %param.10, f32[256]{0:T(256)S(1)} %broadcast_multiply_fusion, f32[256]{0:T(256)S(1)} %add_rsqrt_fusion), kind=kLoop, calls=%fused_computation.9 | loop fusion | flops 12582912 | bytes 16779264 | tf_op jit(solution)/shard_map/convert_element_type | solution.py:120
  228.5 2.6 %all-to-all-done.1 = bf16[16,32,512]{2,1,0:T(8,128)(2,1)S(1)} async-done(((bf16[16,32,512]{2,1,0:T(8,128)(2,1)}), bf16[16,32,512]{2,1,0:T(8,128)(2,1)S(1)}, u32[]{:S(2)}, u32[]{:S(2)}) %all-to-all-start.1) | async-done | bytes 524320 | tf_op jit(solution)/shard_map/all_to_all | solution.py:34
  231.0 0.1 convert_multiply_fusion.2
  231.2 1.7 fusion.15
  (47 shorter events, 1.0 us)
Async XLA Ops:
  7.2 6.3 %copy-start.11 = (bf16[256,512]{1,0:T(8,128)(2,1)S(1)}, bf16[256,512]{1,0:T(8,128)(2,1)}, u32[]{:S(2)}) copy-start(bf16[256,512]{1,0:T(8,128)(2,1)} %param.11) | copy-start | bytes 786436
  7.2 166.0 %all-gather.3.cloned.1.call-start = ((), (), s32[]{:S(2)}) async-start(), calls=%async_computation.2 | async-start | bytes 9191424 | tf_op jit(solution)/shard_map/all_gather | solution.py:104
  10.2 3.5 %copy-start.2 = (bf16[256,8192]{1,0:T(8,128)(2,1)S(1)}, bf16[256,8192]{1,0:T(8,128)(2,1)}, u32[]{:S(2)}) copy-start(bf16[256,8192]{1,0:T(8,128)(2,1)} %param.10) | copy-start | bytes 12582916
  14.8 2.0 copy-start
  17.9 23.5 %collective-permute-start.7 = (bf16[1024,256]{1,0:T(8,128)(2,1)}, bf16[1024,256]{1,0:T(8,128)(2,1)}, u32[]{:S(2)}, u32[]{:S(2)}) collective-permute-start(bf16[1024,256]{1,0:T(8,128)(2,1)} %convolution_convert_fusion), channel_id=1, source_target_pairs={{0,14},{1,15},{2,0},{3,1},{4,2},{5,3},{6,4},{7,5},{8,6},{9,7},{10,... | collective-permute-start | bytes 1572872 | tf_op jit(solution)/shard_map/ppermute | solution.py:70
  26.5 23.1 %collective-permute-start = (bf16[1024,256]{1,0:T(8,128)(2,1)}, bf16[1024,256]{1,0:T(8,128)(2,1)}, u32[]{:S(2)}, u32[]{:S(2)}) collective-permute-start(bf16[1024,256]{1,0:T(8,128)(2,1)} %convolution_convert_fusion.1), channel_id=1, source_target_pairs={{0,2},{1,3},{2,4},{3,5},{4,6},{5,7},{6,8},{7,9},{8,10},{9,11},{10,... | collective-permute-start | bytes 1572872 | tf_op jit(solution)/shard_map/ppermute | solution.py:69
  43.7 23.4 %collective-permute-start.8 = (bf16[1024,256]{1,0:T(8,128)(2,1)}, bf16[1024,256]{1,0:T(8,128)(2,1)}, u32[]{:S(2)}, u32[]{:S(2)}) collective-permute-start(bf16[1024,256]{1,0:T(8,128)(2,1)} %add_convert_fusion.5), channel_id=1, source_target_pairs={{0,14},{1,15},{2,0},{3,1},{4,2},{5,3},{6,4},{7,5},{8,6},{9,7},{10,... | collective-permute-start | bytes 1572872 | tf_op jit(solution)/shard_map/ppermute | solution.py:70
  49.6 22.7 %copy-start.1 = (bf16[256,8192]{1,0:T(8,128)(2,1)S(1)}, bf16[256,8192]{1,0:T(8,128)(2,1)}, u32[]{:S(2)}) copy-start(bf16[256,8192]{1,0:T(8,128)(2,1)} %copy-done) | copy-start | bytes 12582916
  51.3 20.5 %collective-permute-start.1 = (bf16[1024,256]{1,0:T(8,128)(2,1)S(1)}, bf16[1024,256]{1,0:T(8,128)(2,1)S(1)}, u32[]{:S(2)}, u32[]{:S(2)}) collective-permute-start(bf16[1024,256]{1,0:T(8,128)(2,1)S(1)} %add_convert_fusion.11), channel_id=1, source_target_pairs={{0,2},{1,3},{2,4},{3,5},{4,6},{5,7},{6,8},{7,9},{8,10},{9,11},{10,... | collective-permute-start | bytes 1572872 | tf_op jit(solution)/shard_map/ppermute | solution.py:69
  68.3 12.6 %collective-permute-start.9 = (bf16[1024,256]{1,0:T(8,128)(2,1)S(1)}, bf16[1024,256]{1,0:T(8,128)(2,1)S(1)}, u32[]{:S(2)}, u32[]{:S(2)}) collective-permute-start(bf16[1024,256]{1,0:T(8,128)(2,1)S(1)} %add_convert_fusion.4), channel_id=1, source_target_pairs={{0,14},{1,15},{2,0},{3,1},{4,2},{5,3},{6,4},{7,5},{8,6},{9,7},{10,... | collective-permute-start | bytes 1572872 | tf_op jit(solution)/shard_map/ppermute | solution.py:70
  71.9 12.9 %collective-permute-start.2 = (bf16[1024,256]{1,0:T(8,128)(2,1)S(1)}, bf16[1024,256]{1,0:T(8,128)(2,1)S(1)}, u32[]{:S(2)}, u32[]{:S(2)}) collective-permute-start(bf16[1024,256]{1,0:T(8,128)(2,1)S(1)} %add_convert_fusion.10), channel_id=1, source_target_pairs={{0,2},{1,3},{2,4},{3,5},{4,6},{5,7},{6,8},{7,9},{8,10},{9,11},{10,... | collective-permute-start | bytes 1572872 | tf_op jit(solution)/shard_map/ppermute | solution.py:69
  81.1 16.8 %collective-permute-start.10 = (bf16[1024,256]{1,0:T(8,128)(2,1)S(1)}, bf16[1024,256]{1,0:T(8,128)(2,1)S(1)}, u32[]{:S(2)}, u32[]{:S(2)}) collective-permute-start(bf16[1024,256]{1,0:T(8,128)(2,1)S(1)} %add_convert_fusion.3), channel_id=1, source_target_pairs={{0,14},{1,15},{2,0},{3,1},{4,2},{5,3},{6,4},{7,5},{8,6},{9,7},{10,... | collective-permute-start | bytes 1572872 | tf_op jit(solution)/shard_map/ppermute | solution.py:70
  85.0 26.3 %copy-start.4 = (f32[1024,256]{1,0:T(8,128)S(1)}, f32[1024,256]{1,0:T(8,128)}, u32[]{:S(2)}) copy-start(f32[1024,256]{1,0:T(8,128)} %fusion.29) | copy-start | bytes 3145732
  85.0 16.6 %collective-permute-start.3 = (bf16[1024,256]{1,0:T(8,128)(2,1)S(1)}, bf16[1024,256]{1,0:T(8,128)(2,1)S(1)}, u32[]{:S(2)}, u32[]{:S(2)}) collective-permute-start(bf16[1024,256]{1,0:T(8,128)(2,1)S(1)} %add_convert_fusion.9), channel_id=1, source_target_pairs={{0,2},{1,3},{2,4},{3,5},{4,6},{5,7},{6,8},{7,9},{8,10},{9,11},{10,... | collective-permute-start | bytes 1572872 | tf_op jit(solution)/shard_map/ppermute | solution.py:69
  98.0 13.3 %collective-permute-start.11 = (bf16[1024,256]{1,0:T(8,128)(2,1)S(1)}, bf16[1024,256]{1,0:T(8,128)(2,1)S(1)}, u32[]{:S(2)}, u32[]{:S(2)}) collective-permute-start(bf16[1024,256]{1,0:T(8,128)(2,1)S(1)} %add_convert_fusion.2), channel_id=1, source_target_pairs={{0,14},{1,15},{2,0},{3,1},{4,2},{5,3},{6,4},{7,5},{8,6},{9,7},{10,... | collective-permute-start | bytes 1572872 | tf_op jit(solution)/shard_map/ppermute | solution.py:70
  101.7 22.9 %copy-start.3 = (f32[1024,256]{1,0:T(8,128)S(1)}, f32[1024,256]{1,0:T(8,128)}, u32[]{:S(2)}) copy-start(f32[1024,256]{1,0:T(8,128)} %fusion.27) | copy-start | bytes 3145732
  101.7 13.3 %collective-permute-start.4 = (bf16[1024,256]{1,0:T(8,128)(2,1)S(1)}, bf16[1024,256]{1,0:T(8,128)(2,1)S(1)}, u32[]{:S(2)}, u32[]{:S(2)}) collective-permute-start(bf16[1024,256]{1,0:T(8,128)(2,1)S(1)} %add_convert_fusion.8), channel_id=1, source_target_pairs={{0,2},{1,3},{2,4},{3,5},{4,6},{5,7},{6,8},{7,9},{8,10},{9,11},{10,... | collective-permute-start | bytes 1572872 | tf_op jit(solution)/shard_map/ppermute | solution.py:69
  111.4 13.3 %collective-permute-start.12 = (bf16[1024,256]{1,0:T(8,128)(2,1)S(1)}, bf16[1024,256]{1,0:T(8,128)(2,1)S(1)}, u32[]{:S(2)}, u32[]{:S(2)}) collective-permute-start(bf16[1024,256]{1,0:T(8,128)(2,1)S(1)} %add_convert_fusion.1), channel_id=1, source_target_pairs={{0,14},{1,15},{2,0},{3,1},{4,2},{5,3},{6,4},{7,5},{8,6},{9,7},{10,... | collective-permute-start | bytes 1572872 | tf_op jit(solution)/shard_map/ppermute | solution.py:70
  115.1 32.4 %copy-start.5 = (f32[1024,256]{1,0:T(8,128)S(1)}, f32[1024,256]{1,0:T(8,128)}, u32[]{:S(2)}) copy-start(f32[1024,256]{1,0:T(8,128)} %fusion.25) | copy-start | bytes 3145732
  115.1 13.3 %collective-permute-start.5 = (bf16[1024,256]{1,0:T(8,128)(2,1)S(1)}, bf16[1024,256]{1,0:T(8,128)(2,1)S(1)}, u32[]{:S(2)}, u32[]{:S(2)}) collective-permute-start(bf16[1024,256]{1,0:T(8,128)(2,1)S(1)} %add_convert_fusion.7), channel_id=1, source_target_pairs={{0,2},{1,3},{2,4},{3,5},{4,6},{5,7},{6,8},{7,9},{8,10},{9,11},{10,... | collective-permute-start | bytes 1572872 | tf_op jit(solution)/shard_map/ppermute | solution.py:69
  124.7 22.7 %collective-permute-start.13 = (bf16[1024,256]{1,0:T(8,128)(2,1)S(1)}, bf16[1024,256]{1,0:T(8,128)(2,1)S(1)}, u32[]{:S(2)}, u32[]{:S(2)}) collective-permute-start(bf16[1024,256]{1,0:T(8,128)(2,1)S(1)} %add_convert_fusion), channel_id=1, source_target_pairs={{0,14},{1,15},{2,0},{3,1},{4,2},{5,3},{6,4},{7,5},{8,6},{9,7},{10,... | collective-permute-start | bytes 1572872 | tf_op jit(solution)/shard_map/ppermute | solution.py:70
  128.5 23.3 %collective-permute-start.6 = (bf16[1024,256]{1,0:T(8,128)(2,1)S(1)}, bf16[1024,256]{1,0:T(8,128)(2,1)S(1)}, u32[]{:S(2)}, u32[]{:S(2)}) collective-permute-start(bf16[1024,256]{1,0:T(8,128)(2,1)S(1)} %add_convert_fusion.6), channel_id=1, source_target_pairs={{0,2},{1,3},{2,4},{3,5},{4,6},{5,7},{6,8},{7,9},{8,10},{9,11},{10,... | collective-permute-start | bytes 1572872 | tf_op jit(solution)/shard_map/ppermute | solution.py:69
  152.0 12.4 %collective-permute-start.14 = (bf16[512,512]{1,0:T(8,128)(2,1)S(1)}, bf16[512,512]{1,0:T(8,128)(2,1)}, u32[]{:S(2)}, u32[]{:S(2)}) collective-permute-start(bf16[512,512]{1,0:T(8,128)(2,1)S(1)} %fusion.11), channel_id=1, source_target_pairs={{0,1},{1,0},{2,3},{3,2},{4,5},{5,4},{6,7},{7,6},{8,9},{9,8},{10,11... | collective-permute-start | bytes 1572872 | tf_op jit(solution)/shard_map/ppermute | solution.py:78
  174.7 7.5 %copy-start.6 = (f32[512,512]{1,0:T(8,128)S(1)}, f32[512,512]{1,0:T(8,128)}, u32[]{:S(2)}) copy-start(f32[512,512]{1,0:T(8,128)} %param.16) | copy-start | bytes 3145732
  174.7 7.5 %copy-start.7 = (f32[1,512,512]{2,1,0:T(8,128)S(1)}, f32[1,512,512]{2,1,0:T(8,128)}, u32[]{:S(2)}) copy-start(f32[1,512,512]{2,1,0:T(8,128)} %param.13) | copy-start | bytes 3145732
  174.7 7.5 %copy-start.9 = (bf16[1,512,512]{2,1,0:T(8,128)(2,1)S(1)}, bf16[1,512,512]{2,1,0:T(8,128)(2,1)}, u32[]{:S(2)}) copy-start(bf16[1,512,512]{2,1,0:T(8,128)(2,1)} %param.15) | copy-start | bytes 1572868
  174.7 7.5 %copy-start.10 = (bf16[1,512,512]{2,1,0:T(8,128)(2,1)S(1)}, bf16[1,512,512]{2,1,0:T(8,128)(2,1)}, u32[]{:S(2)}) copy-start(bf16[1,512,512]{2,1,0:T(8,128)(2,1)} %param.14) | copy-start | bytes 1572868
  182.2 20.0 %copy-start.12 = (bf16[256,512]{1,0:T(8,128)(2,1)S(1)}, bf16[256,512]{1,0:T(8,128)(2,1)}, u32[]{:S(2)}) copy-start(bf16[256,512]{1,0:T(8,128)(2,1)} %param.11) | copy-start | bytes 786436
  185.1 29.8 %all-to-all-start = ((bf16[16,32,512]{2,1,0:T(8,128)(2,1)}), bf16[16,32,512]{2,1,0:T(8,128)(2,1)S(1)}, u32[]{:S(2)}, u32[]{:S(2)}) async-start(bf16[16,32,512]{2,1,0:T(8,128)(2,1)} %bitcast.5), calls=%async_computation | async-start | bytes 1048576 | tf_op jit(solution)/shard_map/all_to_all | solution.py:41
  215.8 15.2 %all-to-all-start.1 = ((bf16[16,32,512]{2,1,0:T(8,128)(2,1)}), bf16[16,32,512]{2,1,0:T(8,128)(2,1)S(1)}, u32[]{:S(2)}, u32[]{:S(2)}) async-start(bf16[16,32,512]{2,1,0:T(8,128)(2,1)} %broadcast_in_dim.6), calls=%async_computation.1 | async-start | bytes 1048576 | tf_op jit(solution)/shard_map/all_to_all | solution.py:34
  221.5 9.6 %copy-start.8 = (f32[512,512]{1,0:T(8,128)S(1)}, f32[512,512]{1,0:T(8,128)}, u32[]{:S(2)}) copy-start(f32[512,512]{1,0:T(8,128)} %param.17) | copy-start | bytes 3145732
Sparse Core Ops, SparseCore 0:
  10.6 162.5 all-gather.2

commit v7 on v6

--- a/solution.py
+++ b/solution.py
@@ -70,8 +70,13 @@
         backward = lax.ppermute(backward.astype(jnp.bfloat16), axis, behind).astype(jnp.float32)
         forward = forward + block(station - step - 2, kept_forward)
         backward = backward + block(station + step + 2, kept_backward)
-    combined = jnp.concatenate([forward, backward], axis=1)
-    rows = group // 2
+    return jnp.concatenate([forward, backward], axis=1)
+
+
+def pair_sum_rows(combined, axis):
+    count = lax.axis_size(axis)
+    side = lax.axis_index(axis) % 2
+    rows = combined.shape[0] // 2
     mine = lax.dynamic_slice_in_dim(combined, side * rows, rows, 0)
     theirs = lax.dynamic_slice_in_dim(combined, (1 - side) * rows, rows, 0)
     partner = [(i, i ^ 1) for i in range(count)]
@@ -107,8 +112,9 @@
     normed = values * inverse
     normed_low = normed.astype(jnp.bfloat16)
     kept = (cotangent.astype(jnp.float32) * answer[:, None]).astype(jnp.bfloat16)
-    reduced = ring_sum_rows(normed_low, kept, "fsdp")
-    gathered, reduced = lax.optimization_barrier((gathered, reduced))
+    combined = ring_sum_rows(normed_low, kept, "fsdp")
+    gathered, combined = lax.optimization_barrier((gathered, combined))
+    reduced = pair_sum_rows(combined, "fsdp")
     count = gathered.shape[0]
     all_weight = gathered[:, :rows].reshape(count * rows, width)
     all_answer = gathered[:, rows, :tokens].reshape(count * tokens).astype(jnp.float32)

time: 241 us -> 239 us (level)
  starting transfers between devices: 57.4 us -> 41 us
  waiting for transfers between devices: 98.7 us -> 112 us
    ppermute x7, waiting for transfers between devices: 4.22 us -> 90 us  [ring_sum_rows(): lax.ppermute(forward.astype(jnp.bfloat16), axis, ahead).astype(jnp.float32)]
    ppermute x7, waiting for transfers between devices: 77.6 us -> 1.19 us  [ring_sum_rows(): lax.ppermute(backward.astype(jnp.bfloat16), axis, behind)]
    all_to_all x1, starting transfers between devices: 17.2 us -> 7.59 us  [sum_rows(): received = lax.all_to_all(pieces, axis, 0, 0, tiled=True)]
    all_gather x1, waiting for transfers between devices: 7.59 us -> 15.7 us  [per_device(): gathered = lax.all_gather(packed, 'fsdp', axis=0, tiled=False)]
    ppermute x7, starting transfers between devices: 27.9 us -> 22.4 us  [ring_sum_rows(): lax.ppermute(backward.astype(jnp.bfloat16), axis, behind)]
    ppermute x1, waiting for transfers between devices: 6.68 us -> 2.75 us  [pair_sum_rows(): lax.ppermute(theirs.astype(jnp.bfloat16), axis, partner).astype(jnp.float32)]
    ppermute x1, starting transfers between devices: 5.77 us -> 2.23 us  [pair_sum_rows(): lax.ppermute(theirs.astype(jnp.bfloat16), axis, partner).astype(jnp.float32)]
  transfers between devices with their start and end apart: 18 -> 18, of which waited for: 11 -> 11; matrix products, arithmetic and copies ran while one was open for 21% -> 24% of each run, Pallas kernels for 0% -> 0%
where the time goes in v7:
time: 239 us; the launch traced here: 238 us
  waiting for transfers between devices  112 us (47%)
  starting transfers between devices  41 us (17%)
  matrix products  34.5 us (14%)
  other arithmetic  24.3 us (10%)
  between operations  14.5 us (6%)
  local copies, waits for them, and re-layouts  11.3 us (5%)
    ppermute x7, waiting for transfers between devices, ring_sum_rows(): lax.ppermute(forward.astype(jnp.bfloat16), axis, ahead).astype(jnp.float32)  90 us
    ppermute x7, starting transfers between devices, ring_sum_rows(): lax.ppermute(backward.astype(jnp.bfloat16), axis, behind)  22.4 us
    dot_general x16, matrix products, contract_first(): lax.dot_general(left, right, (((0,), (0,)), ((), ())), preferred_element_...  21.9 us
    all_gather x1, waiting for transfers between devices, per_device(): gathered = lax.all_gather(packed, 'fsdp', axis=0, tiled=False)  15.7 us
    dot_general x1, matrix products, contract_last(): lax.dot_general(left, right, (((1,), (1,)), ((), ())), preferred_element_...  12.6 us
    all_to_all x1, starting transfers between devices, sum_rows(): received = lax.all_to_all(pieces, axis, 0, 0, tiled=True)  7.59 us
    slice x1, local copies, waits for them, and re-layouts, per_device(): all_weight = gathered[:, :rows].reshape(count * rows, width)  7.52 us
    convert_element_type x1, other arithmetic, per_device(): (inverse * (feature_grad - normed * projected)).astype(jnp.bfloat16)  6.93 us
  transfers between devices with their start and end apart: 18, of which 11 were waited for; matrix products, arithmetic and copies ran while one was open for 24% of the time, Pallas kernels for 0%

profile of v7, /device:TPU:1, one launch (start us, length us, event | category | flops | bytes accessed | tf_op | source)
XLA Modules:
  0.0 237.9 jit_solution(3157139971473814219)
XLA Ops:
  7.2 0.7 compare_convert_fusion
  7.9 1.3 bitcast_convert_fusion
  9.2 0.8 fusion.17
  10.2 3.3 %fusion.7 = f32[256]{0:T(256)S(1)} fusion(bf16[256,8192]{1,0:T(8,128)(2,1)} %param.10), kind=kLoop, calls=%fused_computation.10 | loop fusion | flops 6291200 | bytes 4195328 | tf_op jit(solution)/shard_map/reduce_sum | solution.py:111
  13.6 1.1 fusion.2
  14.8 2.0 copy-done
  16.8 1.1 convolution_convert_fusion.1
  17.9 2.5 %collective-permute-start = (bf16[1024,256]{1,0:T(8,128)(2,1)}, bf16[1024,256]{1,0:T(8,128)(2,1)}, u32[]{:S(2)}, u32[]{:S(2)}) collective-permute-start(bf16[1024,256]{1,0:T(8,128)(2,1)} %convolution_convert_fusion.1), channel_id=1, source_target_pairs={{0,2},{1,3},{2,4},{3,5},{4,6},{5,7},{6,8},{7,9},{8,10},{9,11},{10,... | collective-permute-start | bytes 1572872 | tf_op jit(solution)/shard_map/ppermute | solution.py:69
  20.4 2.2 convolution_convert_fusion
  22.6 3.9 %collective-permute-start.7 = (bf16[1024,256]{1,0:T(8,128)(2,1)}, bf16[1024,256]{1,0:T(8,128)(2,1)}, u32[]{:S(2)}, u32[]{:S(2)}) collective-permute-start(bf16[1024,256]{1,0:T(8,128)(2,1)} %convolution_convert_fusion), channel_id=1, source_target_pairs={{0,14},{1,15},{2,0},{3,1},{4,2},{5,3},{6,4},{7,5},{8,6},{9,7},{10,... | collective-permute-start | bytes 1572872 | tf_op jit(solution)/shard_map/ppermute | solution.py:70
  26.5 1.4 fusion.48
  27.9 1.5 fusion.46
  29.4 1.4 fusion.44
  30.9 2.4 fusion.42
  33.3 2.4 fusion.40
  35.7 4.5 %collective-permute-done = bf16[1024,256]{1,0:T(8,128)(2,1)} collective-permute-done((bf16[1024,256]{1,0:T(8,128)(2,1)}, bf16[1024,256]{1,0:T(8,128)(2,1)}, u32[]{:S(2)}, u32[]{:S(2)}) %collective-permute-start) | collective-permute-done | bytes 524320 | tf_op jit(solution)/shard_map/ppermute | solution.py:69
  40.1 2.4 add_convert_fusion.11
  42.5 2.4 fusion.38
  44.9 1.2 collective-permute-done.7
  46.0 1.7 add_convert_fusion.5
  47.7 3.4 %collective-permute-start.8 = (bf16[1024,256]{1,0:T(8,128)(2,1)S(1)}, bf16[1024,256]{1,0:T(8,128)(2,1)S(1)}, u32[]{:S(2)}, u32[]{:S(2)}) collective-permute-start(bf16[1024,256]{1,0:T(8,128)(2,1)S(1)} %add_convert_fusion.5), channel_id=1, source_target_pairs={{0,14},{1,15},{2,0},{3,1},{4,2},{5,3},{6,4},{7,5},{8,6},{9,7},{10,... | collective-permute-start | bytes 1572872 | tf_op jit(solution)/shard_map/ppermute | solution.py:70
  51.1 1.4 fusion.31
  52.5 15.3 %collective-permute-done.1 = bf16[1024,256]{1,0:T(8,128)(2,1)} collective-permute-done((bf16[1024,256]{1,0:T(8,128)(2,1)}, bf16[1024,256]{1,0:T(8,128)(2,1)}, u32[]{:S(2)}, u32[]{:S(2)}) %collective-permute-start.1) | collective-permute-done | bytes 524320 | tf_op jit(solution)/shard_map/ppermute | solution.py:69
  67.8 1.2 add_convert_fusion.10
  69.1 0.1 add_convert_fusion.4
  69.2 2.7 %collective-permute-start.9 = (bf16[1024,256]{1,0:T(8,128)(2,1)S(1)}, bf16[1024,256]{1,0:T(8,128)(2,1)S(1)}, u32[]{:S(2)}, u32[]{:S(2)}) collective-permute-start(bf16[1024,256]{1,0:T(8,128)(2,1)S(1)} %add_convert_fusion.4), channel_id=1, source_target_pairs={{0,14},{1,15},{2,0},{3,1},{4,2},{5,3},{6,4},{7,5},{8,6},{9,7},{10,... | collective-permute-start | bytes 1572872 | tf_op jit(solution)/shard_map/ppermute | solution.py:70
  71.9 0.4 fusion.29
  72.3 9.3 %collective-permute-done.2 = bf16[1024,256]{1,0:T(8,128)(2,1)S(1)} collective-permute-done((bf16[1024,256]{1,0:T(8,128)(2,1)S(1)}, bf16[1024,256]{1,0:T(8,128)(2,1)S(1)}, u32[]{:S(2)}, u32[]{:S(2)}) %collective-permute-start.2) | collective-permute-done | bytes 524320 | tf_op jit(solution)/shard_map/ppermute | solution.py:69
  81.6 0.1 add_convert_fusion.9
  81.7 0.3 collective-permute-start.3
  82.0 0.1 add_convert_fusion.3
  82.2 3.4 %collective-permute-start.10 = (bf16[1024,256]{1,0:T(8,128)(2,1)S(1)}, bf16[1024,256]{1,0:T(8,128)(2,1)S(1)}, u32[]{:S(2)}, u32[]{:S(2)}) collective-permute-start(bf16[1024,256]{1,0:T(8,128)(2,1)S(1)} %add_convert_fusion.3), channel_id=1, source_target_pairs={{0,14},{1,15},{2,0},{3,1},{4,2},{5,3},{6,4},{7,5},{8,6},{9,7},{10,... | collective-permute-start | bytes 1572872 | tf_op jit(solution)/shard_map/ppermute | solution.py:70
  85.5 0.3 fusion.27
  85.9 16.8 %collective-permute-done.3 = bf16[1024,256]{1,0:T(8,128)(2,1)S(1)} collective-permute-done((bf16[1024,256]{1,0:T(8,128)(2,1)S(1)}, bf16[1024,256]{1,0:T(8,128)(2,1)S(1)}, u32[]{:S(2)}, u32[]{:S(2)}) %collective-permute-start.3) | collective-permute-done | bytes 524320 | tf_op jit(solution)/shard_map/ppermute | solution.py:69
  102.6 0.1 add_convert_fusion.8
  102.8 0.1 add_convert_fusion.2
  103.0 2.7 %collective-permute-start.11 = (bf16[1024,256]{1,0:T(8,128)(2,1)S(1)}, bf16[1024,256]{1,0:T(8,128)(2,1)S(1)}, u32[]{:S(2)}, u32[]{:S(2)}) collective-permute-start(bf16[1024,256]{1,0:T(8,128)(2,1)S(1)} %add_convert_fusion.2), channel_id=1, source_target_pairs={{0,14},{1,15},{2,0},{3,1},{4,2},{5,3},{6,4},{7,5},{8,6},{9,7},{10,... | collective-permute-start | bytes 1572872 | tf_op jit(solution)/shard_map/ppermute | solution.py:70
  105.7 0.3 fusion.25
  106.1 11.1 %collective-permute-done.4 = bf16[1024,256]{1,0:T(8,128)(2,1)S(1)} collective-permute-done((bf16[1024,256]{1,0:T(8,128)(2,1)S(1)}, bf16[1024,256]{1,0:T(8,128)(2,1)S(1)}, u32[]{:S(2)}, u32[]{:S(2)}) %collective-permute-start.4) | collective-permute-done | bytes 524320 | tf_op jit(solution)/shard_map/ppermute | solution.py:69
  117.4 0.1 add_convert_fusion.1
  117.5 3.5 %collective-permute-start.12 = (bf16[1024,256]{1,0:T(8,128)(2,1)S(1)}, bf16[1024,256]{1,0:T(8,128)(2,1)S(1)}, u32[]{:S(2)}, u32[]{:S(2)}) collective-permute-start(bf16[1024,256]{1,0:T(8,128)(2,1)S(1)} %add_convert_fusion.1), channel_id=1, source_target_pairs={{0,14},{1,15},{2,0},{3,1},{4,2},{5,3},{6,4},{7,5},{8,6},{9,7},{10,... | collective-permute-start | bytes 1572872 | tf_op jit(solution)/shard_map/ppermute | solution.py:70
  121.0 0.4 fusion.23
  121.4 10.6 %collective-permute-done.5 = bf16[1024,256]{1,0:T(8,128)(2,1)S(1)} collective-permute-done((bf16[1024,256]{1,0:T(8,128)(2,1)S(1)}, bf16[1024,256]{1,0:T(8,128)(2,1)S(1)}, u32[]{:S(2)}, u32[]{:S(2)}) %collective-permute-start.5) | collective-permute-done | bytes 524320 | tf_op jit(solution)/shard_map/ppermute | solution.py:69
  132.0 0.1 add_convert_fusion.6
  132.2 0.1 add_convert_fusion
  132.3 2.7 %collective-permute-start.13 = (bf16[1024,256]{1,0:T(8,128)(2,1)S(1)}, bf16[1024,256]{1,0:T(8,128)(2,1)S(1)}, u32[]{:S(2)}, u32[]{:S(2)}) collective-permute-start(bf16[1024,256]{1,0:T(8,128)(2,1)S(1)} %add_convert_fusion), channel_id=1, source_target_pairs={{0,14},{1,15},{2,0},{3,1},{4,2},{5,3},{6,4},{7,5},{8,6},{9,7},{10,... | collective-permute-start | bytes 1572872 | tf_op jit(solution)/shard_map/ppermute | solution.py:70
  135.1 0.3 fusion.21
  135.4 22.4 %collective-permute-done.6 = bf16[1024,256]{1,0:T(8,128)(2,1)S(1)} collective-permute-done((bf16[1024,256]{1,0:T(8,128)(2,1)S(1)}, bf16[1024,256]{1,0:T(8,128)(2,1)S(1)}, u32[]{:S(2)}, u32[]{:S(2)}) %collective-permute-start.6) | collective-permute-done | bytes 524320 | tf_op jit(solution)/shard_map/ppermute | solution.py:69
  158.0 0.3 pad_maximum_fusion
  158.4 15.7 %all-gather.3.cloned.1.call-done = bf16[8448,512]{1,0:T(8,128)(2,1)} async-done(((bf16[528,512]{1,0:T(8,128)(2,1)}), bf16[8448,512]{1,0:T(8,128)(2,1)}) %all-gather.3.cloned.1.call-update) | async-done | bytes 8650768 | tf_op jit(solution)/shard_map/all_gather | solution.py:109
  174.1 0.9 dynamic-slice_convert_fusion
  174.9 2.2 collective-permute-start.14
  177.2 7.5 %slice.31 = bf16[16,512,512]{2,1,0:T(8,128)(2,1)} slice(bf16[16,528,512]{2,1,0:T(8,128)(2,1)} %bitcast.47), slice={[0:16], [0:512], [0:512]} | slice | bytes 16777216 | tf_op jit(solution)/shard_map/slice | solution.py:119
  184.7 1.5 convert_reduce_fusion
  186.2 2.8 %collective-permute-done.14 = bf16[512,512]{1,0:T(8,128)(2,1)} collective-permute-done((bf16[512,512]{1,0:T(8,128)(2,1)}, bf16[512,512]{1,0:T(8,128)(2,1)}, u32[]{:S(2)}, u32[]{:S(2)}) %collective-permute-start.14) | collective-permute-done | bytes 524320 | tf_op jit(solution)/shard_map/ppermute | solution.py:83
  189.0 3.9 %fusion.19 = (bf16[1,512,512]{2,1,0:T(8,128)(2,1)}, bf16[512,512]{1,0:T(8,128)(2,1)}, bf16[1,512,512]{2,1,0:T(8,128)(2,1)}) fusion(bf16[1,512,512]{2,1,0:T(8,128)(2,1)S(1)} %copy-done.9, f32[]{:T(128)} %convert_reduce_fusion, bf16[512,512]{1,0:T(8,128)(2,1)} %collective-permute-done.14, f32[1024,512]{1,0:T(8,128)S(1)} %pad_maximum_fusion, s32[]{:T(128)S(6)} %select_n.227, ...), kind=kLoop, calls=%fused_computation.50 | loop fusion | flops 6029312 | bytes 6291464 | tf_op jit(solution)/shard_map/broadcast_in_dim | solution.py:141
  192.9 7.6 %all-to-all-start = ((bf16[16,32,512]{2,1,0:T(8,128)(2,1)}), bf16[16,32,512]{2,1,0:T(8,128)(2,1)S(1)}, u32[]{:S(2)}, u32[]{:S(2)}) async-start(bf16[16,32,512]{2,1,0:T(8,128)(2,1)} %bitcast.49), calls=%async_computation | async-start | bytes 1048576 | tf_op jit(solution)/shard_map/all_to_all | solution.py:41
  200.5 12.6 %fusion.3 = (f32[256]{0:T(256)S(1)}, f32[256,8192]{1,0:T(8,128)}) fusion(bf16[256,8192]{1,0:T(8,128)(2,1)} %param.10, f32[256]{0:T(256)S(1)} %add_rsqrt_fusion, bf16[8192,512]{1,0:T(8,128)(2,1)} %bitcast.46, bf16[256,512]{1,0:T(8,128)(2,1)S(1)} %copy-done.12, f32[]{:T(128)} %convert_reduce_fusion, f32[256]{0:T(256)S(1)} %get-tuple-element.26), kind=kOutput, calls=%fused_computation.6 | convolution fusion | flops 2158493440 | bytes 21236740 | tf_op jit(solution)/shard_map/dot_general | solution.py:20
  213.2 0.8 broadcast_in_dim.6
  214.0 5.7 %all-to-all-start.1 = ((bf16[16,32,512]{2,1,0:T(8,128)(2,1)}), bf16[16,32,512]{2,1,0:T(8,128)(2,1)S(1)}, u32[]{:S(2)}, u32[]{:S(2)}) async-start(bf16[16,32,512]{2,1,0:T(8,128)(2,1)} %broadcast_in_dim.6), calls=%async_computation.1 | async-start | bytes 1048576 | tf_op jit(solution)/shard_map/all_to_all | solution.py:34
  219.7 6.9 %fusion.6 = bf16[256,8192]{1,0:T(8,128)(2,1)} fusion(f32[256,8192]{1,0:T(8,128)} %get-tuple-element.29, bf16[256,8192]{1,0:T(8,128)(2,1)} %param.10, f32[256]{0:T(256)S(1)} %broadcast_multiply_fusion, f32[256]{0:T(256)S(1)} %add_rsqrt_fusion), kind=kLoop, calls=%fused_computation.9 | loop fusion | flops 12582912 | bytes 16779264 | tf_op jit(solution)/shard_map/convert_element_type | solution.py:126
  226.7 2.6 %all-to-all-done.1 = bf16[16,32,512]{2,1,0:T(8,128)(2,1)S(1)} async-done(((bf16[16,32,512]{2,1,0:T(8,128)(2,1)}), bf16[16,32,512]{2,1,0:T(8,128)(2,1)S(1)}, u32[]{:S(2)}, u32[]{:S(2)}) %all-to-all-start.1) | async-done | bytes 524320 | tf_op jit(solution)/shard_map/all_to_all | solution.py:34
  229.2 0.1 convert_multiply_fusion.2
  229.4 1.7 fusion.11
  (47 shorter events, 1.0 us)
Async XLA Ops:
  7.2 6.3 %copy-start.11 = (bf16[256,512]{1,0:T(8,128)(2,1)S(1)}, bf16[256,512]{1,0:T(8,128)(2,1)}, u32[]{:S(2)}) copy-start(bf16[256,512]{1,0:T(8,128)(2,1)} %param.11) | copy-start | bytes 786436
  7.2 166.9 %all-gather.3.cloned.1.call-start = ((), (), s32[]{:S(2)}) async-start(), calls=%async_computation.2 | async-start | bytes 9191424 | tf_op jit(solution)/shard_map/all_gather | solution.py:109
  10.2 3.5 %copy-start.2 = (bf16[256,8192]{1,0:T(8,128)(2,1)S(1)}, bf16[256,8192]{1,0:T(8,128)(2,1)}, u32[]{:S(2)}) copy-start(bf16[256,8192]{1,0:T(8,128)(2,1)} %param.10) | copy-start | bytes 12582916
  14.8 2.0 copy-start
  17.9 22.2 %collective-permute-start = (bf16[1024,256]{1,0:T(8,128)(2,1)}, bf16[1024,256]{1,0:T(8,128)(2,1)}, u32[]{:S(2)}, u32[]{:S(2)}) collective-permute-start(bf16[1024,256]{1,0:T(8,128)(2,1)} %convolution_convert_fusion.1), channel_id=1, source_target_pairs={{0,2},{1,3},{2,4},{3,5},{4,6},{5,7},{6,8},{7,9},{8,10},{9,11},{10,... | collective-permute-start | bytes 1572872 | tf_op jit(solution)/shard_map/ppermute | solution.py:69
  22.6 23.5 %collective-permute-start.7 = (bf16[1024,256]{1,0:T(8,128)(2,1)}, bf16[1024,256]{1,0:T(8,128)(2,1)}, u32[]{:S(2)}, u32[]{:S(2)}) collective-permute-start(bf16[1024,256]{1,0:T(8,128)(2,1)} %convolution_convert_fusion), channel_id=1, source_target_pairs={{0,14},{1,15},{2,0},{3,1},{4,2},{5,3},{6,4},{7,5},{8,6},{9,7},{10,... | collective-permute-start | bytes 1572872 | tf_op jit(solution)/shard_map/ppermute | solution.py:70
  42.5 25.3 %collective-permute-start.1 = (bf16[1024,256]{1,0:T(8,128)(2,1)}, bf16[1024,256]{1,0:T(8,128)(2,1)}, u32[]{:S(2)}, u32[]{:S(2)}) collective-permute-start(bf16[1024,256]{1,0:T(8,128)(2,1)} %add_convert_fusion.11), channel_id=1, source_target_pairs={{0,2},{1,3},{2,4},{3,5},{4,6},{5,7},{6,8},{7,9},{8,10},{9,11},{10,... | collective-permute-start | bytes 1572872 | tf_op jit(solution)/shard_map/ppermute | solution.py:69
  44.9 27.1 %copy-start.1 = (bf16[256,8192]{1,0:T(8,128)(2,1)S(1)}, bf16[256,8192]{1,0:T(8,128)(2,1)}, u32[]{:S(2)}) copy-start(bf16[256,8192]{1,0:T(8,128)(2,1)} %copy-done) | copy-start | bytes 12582916
  47.7 21.3 %collective-permute-start.8 = (bf16[1024,256]{1,0:T(8,128)(2,1)S(1)}, bf16[1024,256]{1,0:T(8,128)(2,1)S(1)}, u32[]{:S(2)}, u32[]{:S(2)}) collective-permute-start(bf16[1024,256]{1,0:T(8,128)(2,1)S(1)} %add_convert_fusion.5), channel_id=1, source_target_pairs={{0,14},{1,15},{2,0},{3,1},{4,2},{5,3},{6,4},{7,5},{8,6},{9,7},{10,... | collective-permute-start | bytes 1572872 | tf_op jit(solution)/shard_map/ppermute | solution.py:70
  69.0 12.6 %collective-permute-start.2 = (bf16[1024,256]{1,0:T(8,128)(2,1)S(1)}, bf16[1024,256]{1,0:T(8,128)(2,1)S(1)}, u32[]{:S(2)}, u32[]{:S(2)}) collective-permute-start(bf16[1024,256]{1,0:T(8,128)(2,1)S(1)} %add_convert_fusion.10), channel_id=1, source_target_pairs={{0,2},{1,3},{2,4},{3,5},{4,6},{5,7},{6,8},{7,9},{8,10},{9,11},{10,... | collective-permute-start | bytes 1572872 | tf_op jit(solution)/shard_map/ppermute | solution.py:69
  69.2 12.8 %collective-permute-start.9 = (bf16[1024,256]{1,0:T(8,128)(2,1)S(1)}, bf16[1024,256]{1,0:T(8,128)(2,1)S(1)}, u32[]{:S(2)}, u32[]{:S(2)}) collective-permute-start(bf16[1024,256]{1,0:T(8,128)(2,1)S(1)} %add_convert_fusion.4), channel_id=1, source_target_pairs={{0,14},{1,15},{2,0},{3,1},{4,2},{5,3},{6,4},{7,5},{8,6},{9,7},{10,... | collective-permute-start | bytes 1572872 | tf_op jit(solution)/shard_map/ppermute | solution.py:70
  81.7 20.9 %collective-permute-start.3 = (bf16[1024,256]{1,0:T(8,128)(2,1)S(1)}, bf16[1024,256]{1,0:T(8,128)(2,1)S(1)}, u32[]{:S(2)}, u32[]{:S(2)}) collective-permute-start(bf16[1024,256]{1,0:T(8,128)(2,1)S(1)} %add_convert_fusion.9), channel_id=1, source_target_pairs={{0,2},{1,3},{2,4},{3,5},{4,6},{5,7},{6,8},{7,9},{8,10},{9,11},{10,... | collective-permute-start | bytes 1572872 | tf_op jit(solution)/shard_map/ppermute | solution.py:69
  82.1 35.0 %copy-start.4 = (f32[1024,256]{1,0:T(8,128)S(1)}, f32[1024,256]{1,0:T(8,128)}, u32[]{:S(2)}) copy-start(f32[1024,256]{1,0:T(8,128)} %fusion.42) | copy-start | bytes 3145732
  82.2 20.7 %collective-permute-start.10 = (bf16[1024,256]{1,0:T(8,128)(2,1)S(1)}, bf16[1024,256]{1,0:T(8,128)(2,1)S(1)}, u32[]{:S(2)}, u32[]{:S(2)}) collective-permute-start(bf16[1024,256]{1,0:T(8,128)(2,1)S(1)} %add_convert_fusion.3), channel_id=1, source_target_pairs={{0,14},{1,15},{2,0},{3,1},{4,2},{5,3},{6,4},{7,5},{8,6},{9,7},{10,... | collective-permute-start | bytes 1572872 | tf_op jit(solution)/shard_map/ppermute | solution.py:70
  102.7 14.4 %collective-permute-start.4 = (bf16[1024,256]{1,0:T(8,128)(2,1)S(1)}, bf16[1024,256]{1,0:T(8,128)(2,1)S(1)}, u32[]{:S(2)}, u32[]{:S(2)}) collective-permute-start(bf16[1024,256]{1,0:T(8,128)(2,1)S(1)} %add_convert_fusion.8), channel_id=1, source_target_pairs={{0,2},{1,3},{2,4},{3,5},{4,6},{5,7},{6,8},{7,9},{8,10},{9,11},{10,... | collective-permute-start | bytes 1572872 | tf_op jit(solution)/shard_map/ppermute | solution.py:69
  103.0 29.0 %copy-start.3 = (f32[1024,256]{1,0:T(8,128)S(1)}, f32[1024,256]{1,0:T(8,128)}, u32[]{:S(2)}) copy-start(f32[1024,256]{1,0:T(8,128)} %fusion.40) | copy-start | bytes 3145732
  103.0 14.4 %collective-permute-start.11 = (bf16[1024,256]{1,0:T(8,128)(2,1)S(1)}, bf16[1024,256]{1,0:T(8,128)(2,1)S(1)}, u32[]{:S(2)}, u32[]{:S(2)}) collective-permute-start(bf16[1024,256]{1,0:T(8,128)(2,1)S(1)} %add_convert_fusion.2), channel_id=1, source_target_pairs={{0,14},{1,15},{2,0},{3,1},{4,2},{5,3},{6,4},{7,5},{8,6},{9,7},{10,... | collective-permute-start | bytes 1572872 | tf_op jit(solution)/shard_map/ppermute | solution.py:70
  117.3 14.7 %collective-permute-start.5 = (bf16[1024,256]{1,0:T(8,128)(2,1)S(1)}, bf16[1024,256]{1,0:T(8,128)(2,1)S(1)}, u32[]{:S(2)}, u32[]{:S(2)}) collective-permute-start(bf16[1024,256]{1,0:T(8,128)(2,1)S(1)} %add_convert_fusion.7), channel_id=1, source_target_pairs={{0,2},{1,3},{2,4},{3,5},{4,6},{5,7},{6,8},{7,9},{8,10},{9,11},{10,... | collective-permute-start | bytes 1572872 | tf_op jit(solution)/shard_map/ppermute | solution.py:69
  117.5 40.3 %copy-start.5 = (f32[1024,256]{1,0:T(8,128)S(1)}, f32[1024,256]{1,0:T(8,128)}, u32[]{:S(2)}) copy-start(f32[1024,256]{1,0:T(8,128)} %fusion.38) | copy-start | bytes 3145732
  117.5 14.7 %collective-permute-start.12 = (bf16[1024,256]{1,0:T(8,128)(2,1)S(1)}, bf16[1024,256]{1,0:T(8,128)(2,1)S(1)}, u32[]{:S(2)}, u32[]{:S(2)}) collective-permute-start(bf16[1024,256]{1,0:T(8,128)(2,1)S(1)} %add_convert_fusion.1), channel_id=1, source_target_pairs={{0,14},{1,15},{2,0},{3,1},{4,2},{5,3},{6,4},{7,5},{8,6},{9,7},{10,... | collective-permute-start | bytes 1572872 | tf_op jit(solution)/shard_map/ppermute | solution.py:70
  132.1 25.7 %collective-permute-start.6 = (bf16[1024,256]{1,0:T(8,128)(2,1)S(1)}, bf16[1024,256]{1,0:T(8,128)(2,1)S(1)}, u32[]{:S(2)}, u32[]{:S(2)}) collective-permute-start(bf16[1024,256]{1,0:T(8,128)(2,1)S(1)} %add_convert_fusion.6), channel_id=1, source_target_pairs={{0,2},{1,3},{2,4},{3,5},{4,6},{5,7},{6,8},{7,9},{8,10},{9,11},{10,... | collective-permute-start | bytes 1572872 | tf_op jit(solution)/shard_map/ppermute | solution.py:69
  132.3 25.6 %collective-permute-start.13 = (bf16[1024,256]{1,0:T(8,128)(2,1)S(1)}, bf16[1024,256]{1,0:T(8,128)(2,1)S(1)}, u32[]{:S(2)}, u32[]{:S(2)}) collective-permute-start(bf16[1024,256]{1,0:T(8,128)(2,1)S(1)} %add_convert_fusion), channel_id=1, source_target_pairs={{0,14},{1,15},{2,0},{3,1},{4,2},{5,3},{6,4},{7,5},{8,6},{9,7},{10,... | collective-permute-start | bytes 1572872 | tf_op jit(solution)/shard_map/ppermute | solution.py:70
  174.9 14.0 %collective-permute-start.14 = (bf16[512,512]{1,0:T(8,128)(2,1)}, bf16[512,512]{1,0:T(8,128)(2,1)}, u32[]{:S(2)}, u32[]{:S(2)}) collective-permute-start(bf16[512,512]{1,0:T(8,128)(2,1)} %dynamic-slice_convert_fusion), channel_id=1, source_target_pairs={{0,1},{1,0},{2,3},{3,2},{4,5},{5,4},{6,7},{7,6},{8,9},{9,8},{10,11... | collective-permute-start | bytes 1572872 | tf_op jit(solution)/shard_map/ppermute | solution.py:83
  177.1 11.8 %copy-start.6 = (f32[512,512]{1,0:T(8,128)S(1)}, f32[512,512]{1,0:T(8,128)}, u32[]{:S(2)}) copy-start(f32[512,512]{1,0:T(8,128)} %param.16) | copy-start | bytes 3145732
  177.1 11.8 %copy-start.7 = (f32[1,512,512]{2,1,0:T(8,128)S(1)}, f32[1,512,512]{2,1,0:T(8,128)}, u32[]{:S(2)}) copy-start(f32[1,512,512]{2,1,0:T(8,128)} %param.13) | copy-start | bytes 3145732
  177.2 11.8 %copy-start.9 = (bf16[1,512,512]{2,1,0:T(8,128)(2,1)S(1)}, bf16[1,512,512]{2,1,0:T(8,128)(2,1)}, u32[]{:S(2)}) copy-start(bf16[1,512,512]{2,1,0:T(8,128)(2,1)} %param.15) | copy-start | bytes 1572868
  177.2 11.8 %copy-start.10 = (bf16[1,512,512]{2,1,0:T(8,128)(2,1)S(1)}, bf16[1,512,512]{2,1,0:T(8,128)(2,1)}, u32[]{:S(2)}) copy-start(bf16[1,512,512]{2,1,0:T(8,128)(2,1)} %param.14) | copy-start | bytes 1572868
  184.7 15.8 %copy-start.12 = (bf16[256,512]{1,0:T(8,128)(2,1)S(1)}, bf16[256,512]{1,0:T(8,128)(2,1)}, u32[]{:S(2)}) copy-start(bf16[256,512]{1,0:T(8,128)(2,1)} %param.11) | copy-start | bytes 786436
  192.9 20.2 %all-to-all-start = ((bf16[16,32,512]{2,1,0:T(8,128)(2,1)}), bf16[16,32,512]{2,1,0:T(8,128)(2,1)S(1)}, u32[]{:S(2)}, u32[]{:S(2)}) async-start(bf16[16,32,512]{2,1,0:T(8,128)(2,1)} %bitcast.49), calls=%async_computation | async-start | bytes 1048576 | tf_op jit(solution)/shard_map/all_to_all | solution.py:41
  214.0 15.2 %all-to-all-start.1 = ((bf16[16,32,512]{2,1,0:T(8,128)(2,1)}), bf16[16,32,512]{2,1,0:T(8,128)(2,1)S(1)}, u32[]{:S(2)}, u32[]{:S(2)}) async-start(bf16[16,32,512]{2,1,0:T(8,128)(2,1)} %broadcast_in_dim.6), calls=%async_computation.1 | async-start | bytes 1048576 | tf_op jit(solution)/shard_map/all_to_all | solution.py:34
  219.7 9.6 %copy-start.8 = (f32[512,512]{1,0:T(8,128)S(1)}, f32[512,512]{1,0:T(8,128)}, u32[]{:S(2)}) copy-start(f32[512,512]{1,0:T(8,128)} %param.17) | copy-start | bytes 3145732
Sparse Core Ops, SparseCore 0:
  10.6 163.4 all-gather.2

commit v8 on v7

--- a/solution.py
+++ b/solution.py
@@ -1,6 +1,8 @@
 import jax
 import jax.numpy as jnp
 from jax import lax
+from jax.experimental import pallas as pl
+from jax.experimental.pallas import tpu as pltpu
 from jax.sharding import PartitionSpec as P
 
 D = 8192
@@ -41,6 +43,46 @@
     received = lax.all_to_all(pieces, axis, 0, 0, tiled=True)
     partial = jnp.sum(received.astype(jnp.float32), axis=0).astype(block.dtype)
     return gather_rows(partial, axis)
+
+
+def input_grad_kernel(scaled_ref, gathered_ref, act_ref, inv_ref, out_ref, feature_ref):
+    chunks = gathered_ref.shape[0]
+    rows = out_ref.shape[1] // chunks
+    scaled = scaled_ref[...]
+    inverse = inv_ref[...]
+    total = jnp.zeros(inverse.shape, jnp.float32)
+    for chunk in range(chunks):
+        cols = slice(chunk * rows, (chunk + 1) * rows)
+        weight = gathered_ref[chunk, :rows, :]
+        feature = D ** (-0.5) * lax.dot_general(
+            scaled, weight, (((1,), (1,)), ((), ())), preferred_element_type=jnp.float32
+        )
+        feature_ref[:, cols] = feature
+        normed = act_ref[:, cols].astype(jnp.float32) * inverse
+        total = total + jnp.sum(feature * normed, axis=1, keepdims=True)
+    projected = total / out_ref.shape[1]
+    for chunk in range(chunks):
+        cols = slice(chunk * rows, (chunk + 1) * rows)
+        normed = act_ref[:, cols].astype(jnp.float32) * inverse
+        out_ref[:, cols] = (inverse * (feature_ref[:, cols] - normed * projected)).astype(out_ref.dtype)
+
+
+def input_grad_of(scaled, gathered, activations, inverse):
+    tokens, features = activations.shape
+    vmem = pl.BlockSpec(memory_space=pltpu.VMEM)
+    return pl.pallas_call(
+        input_grad_kernel,
+        out_shape=jax.ShapeDtypeStruct((tokens, features), jnp.bfloat16),
+        in_specs=[vmem, vmem, vmem, vmem],
+        out_specs=vmem,
+        scratch_shapes=[pltpu.VMEM((tokens, features), jnp.float32)],
+        compiler_params=pltpu.CompilerParams(vmem_limit_bytes=48 * 1024 * 1024),
+        cost_estimate=pl.CostEstimate(
+            flops=2 * tokens * features * scaled.shape[1],
+            bytes_accessed=gathered.size * 2 + activations.size * 4 + scaled.size * 2,
+            transcendentals=0,
+        ),
+    )(scaled, gathered, activations, inverse)
 
 
 def ring_sum_rows(normed_low, kept, axis):
@@ -116,14 +158,11 @@
     gathered, combined = lax.optimization_barrier((gathered, combined))
     reduced = pair_sum_rows(combined, "fsdp")
     count = gathered.shape[0]
-    all_weight = gathered[:, :rows].reshape(count * rows, width)
     all_answer = gathered[:, rows, :tokens].reshape(count * tokens).astype(jnp.float32)
     answers = jnp.sum(all_answer)
     scaled = (cotangent.astype(jnp.float32) * answer[:, None] / answers).astype(jnp.bfloat16)
     gradient = width_scale * reduced / answers
-    feature_grad = width_scale * contract_last(scaled, all_weight)
-    projected = jnp.mean(feature_grad * normed, axis=1, keepdims=True)
-    input_grad = (inverse * (feature_grad - normed * projected)).astype(jnp.bfloat16)
+    input_grad = input_grad_of(scaled, gathered, activations, inverse)
     first = beta_first * first_moment[0].astype(jnp.float32) + (1.0 - beta_first) * gradient
     second = (
         beta_second * second_moment[0].astype(jnp.float32)

time: 239 us -> 240 us (level)
  blocking collectives: 0 us -> 17.3 us
  matrix products: 34.5 us -> 22 us
  Pallas kernels: 0 us -> 10.2 us
  starting transfers between devices: 41 us -> 32.2 us
  local copies, waits for them, and re-layouts: 11.3 us -> 6.13 us
  waiting for transfers between devices: 112 us -> 117 us
  other arithmetic: 24.3 us -> 19.8 us
    all_to_all x0 -> x1, blocking collectives: none -> 17.3 us  [sum_rows(): received = lax.all_to_all(pieces, axis, 0, 0, tiled=True)]
    dot_general x1 -> x0, matrix products: 12.6 us -> none  [contract_last(): lax.dot_general(left, right, (((1,), (1,)), ((), ())), preferred_element_...]
    pallas_call x0 -> x1, Pallas kernels: none -> 10.2 us  [input_grad_of(): pl.pallas_call(input_grad_kernel, out_shape=jax.ShapeDtypeStruct((tokens,...]
    all_to_all x1 -> x0, starting transfers between devices: 7.59 us -> none  [sum_rows(): received = lax.all_to_all(pieces, axis, 0, 0, tiled=True)]
    slice x1 -> x0, local copies, waits for them, and re-layouts: 7.52 us -> none  [per_device(): all_weight = gathered[:, :rows].reshape(count * rows, width)]
    ppermute x1, waiting for transfers between devices: 2.75 us -> 10.1 us  [pair_sum_rows(): lax.ppermute(theirs.astype(jnp.bfloat16), axis, partner).astype(jnp.float32)]
    convert_element_type x1, other arithmetic: 6.93 us -> 0.77 us  [per_device(): (cotangent.astype(jnp.float32) * answer[:, None] / answers).astype(jnp.bf...]
    all_to_all x1, waiting for transfers between devices: 2.56 us -> 0.01 us  [gather_rows(): gathered = lax.all_to_all(copies, axis, 0, 0, tiled=True)]
  transfers between devices with their start and end apart: 18 -> 17, of which waited for: 11 -> 10; matrix products, arithmetic and copies ran while one was open for 24% -> 13% of each run, Pallas kernels for 0% -> 4%
where the time goes in v8:
time: 240 us; the launch traced here: 239 us
  waiting for transfers between devices  117 us (49%)
  starting transfers between devices  32.2 us (13%)
  matrix products  22 us (9%)
  other arithmetic  19.8 us (8%)
  blocking collectives  17.3 us (7%)
  between operations  14.5 us (6%)
  Pallas kernels  10.2 us (4%)
  local copies, waits for them, and re-layouts  6.13 us (3%)
    ppermute x7, waiting for transfers between devices, ring_sum_rows(): lax.ppermute(forward.astype(jnp.bfloat16), axis, ahead).astype(jnp.float32)  90.1 us
    ppermute x7, starting transfers between devices, ring_sum_rows(): lax.ppermute(backward.astype(jnp.bfloat16), axis, behind)  22 us
    dot_general x16, matrix products, contract_first(): lax.dot_general(left, right, (((0,), (0,)), ((), ())), preferred_element_...  22 us
    all_to_all x1, blocking collectives, sum_rows(): received = lax.all_to_all(pieces, axis, 0, 0, tiled=True)  17.3 us
    all_gather x1, waiting for transfers between devices, per_device(): gathered = lax.all_gather(packed, 'fsdp', axis=0, tiled=False)  15.6 us
    pallas_call x1, Pallas kernels, input_grad_of(): pl.pallas_call(input_grad_kernel, out_shape=jax.ShapeDtypeStruct((tokens,...  10.2 us
    ppermute x1, waiting for transfers between devices, pair_sum_rows(): lax.ppermute(theirs.astype(jnp.bfloat16), axis, partner).astype(jnp.float32)  10.1 us
  transfers between devices with their start and end apart: 17, of which 10 were waited for; matrix products, arithmetic and copies ran while one was open for 13% of the time, Pallas kernels for 4%

profile of v8, /device:TPU:1, one launch (start us, length us, event | category | flops | bytes accessed | tf_op | source)
XLA Modules:
  0.0 239.2 jit_solution(14872954876407025894)
XLA Ops:
  7.2 0.7 compare_convert_fusion
  7.9 1.3 bitcast_convert_fusion
  9.2 0.8 fusion.11
  10.2 3.3 %fusion = f32[256]{0:T(256)S(1)} fusion(bf16[256,8192]{1,0:T(8,128)(2,1)} %act_ref.1), kind=kLoop, calls=%fused_computation.2 | loop fusion | flops 6291200 | bytes 4195328 | tf_op jit(solution)/shard_map/reduce_sum | solution.py:153
  13.6 1.1 fusion.1
  14.7 2.0 copy-done.2
  16.7 1.1 convolution_convert_fusion.1
  17.9 2.5 %collective-permute-start = (bf16[1024,256]{1,0:T(8,128)(2,1)}, bf16[1024,256]{1,0:T(8,128)(2,1)}, u32[]{:S(2)}, u32[]{:S(2)}) collective-permute-start(bf16[1024,256]{1,0:T(8,128)(2,1)} %convolution_convert_fusion.1), channel_id=1, source_target_pairs={{0,2},{1,3},{2,4},{3,5},{4,6},{5,7},{6,8},{7,9},{8,10},{9,11},{10,... | collective-permute-start | bytes 1572872 | tf_op jit(solution)/shard_map/ppermute | solution.py:111
  20.4 2.2 convolution_convert_fusion
  22.5 3.9 %collective-permute-start.7 = (bf16[1024,256]{1,0:T(8,128)(2,1)}, bf16[1024,256]{1,0:T(8,128)(2,1)}, u32[]{:S(2)}, u32[]{:S(2)}) collective-permute-start(bf16[1024,256]{1,0:T(8,128)(2,1)} %convolution_convert_fusion), channel_id=1, source_target_pairs={{0,14},{1,15},{2,0},{3,1},{4,2},{5,3},{6,4},{7,5},{8,6},{9,7},{10,... | collective-permute-start | bytes 1572872 | tf_op jit(solution)/shard_map/ppermute | solution.py:112
  26.5 1.4 fusion.42
  27.9 1.5 fusion.40
  29.4 1.4 fusion.38
  30.9 2.4 %fusion.36 = f32[1024,256]{1,0:T(8,128)} fusion(bf16[256,8192]{1,0:T(8,128)(2,1)} %copy-done.2, s32[]{:T(128)S(6)} %select_n.195, bf16[256,512]{1,0:T(8,128)(2,1)S(1)} %fusion.49), kind=kOutput, calls=%fused_computation.65 | convolution fusion | flops 134217728 | bytes 1703940 | tf_op jit(solution)/shard_map/dot_general | solution.py:28
  33.3 2.4 fusion.34
  35.7 4.4 %collective-permute-done = bf16[1024,256]{1,0:T(8,128)(2,1)} collective-permute-done((bf16[1024,256]{1,0:T(8,128)(2,1)}, bf16[1024,256]{1,0:T(8,128)(2,1)}, u32[]{:S(2)}, u32[]{:S(2)}) %collective-permute-start) | collective-permute-done | bytes 524320 | tf_op jit(solution)/shard_map/ppermute | solution.py:111
  40.1 2.4 add_convert_fusion.11
  42.5 2.4 fusion.32
  44.8 1.2 collective-permute-done.7
  46.0 1.7 add_convert_fusion.5
  47.7 3.4 %collective-permute-start.8 = (bf16[1024,256]{1,0:T(8,128)(2,1)S(1)}, bf16[1024,256]{1,0:T(8,128)(2,1)S(1)}, u32[]{:S(2)}, u32[]{:S(2)}) collective-permute-start(bf16[1024,256]{1,0:T(8,128)(2,1)S(1)} %add_convert_fusion.5), channel_id=1, source_target_pairs={{0,14},{1,15},{2,0},{3,1},{4,2},{5,3},{6,4},{7,5},{8,6},{9,7},{10,... | collective-permute-start | bytes 1572872 | tf_op jit(solution)/shard_map/ppermute | solution.py:112
  51.1 1.4 fusion.25
  52.5 15.2 %collective-permute-done.1 = bf16[1024,256]{1,0:T(8,128)(2,1)} collective-permute-done((bf16[1024,256]{1,0:T(8,128)(2,1)}, bf16[1024,256]{1,0:T(8,128)(2,1)}, u32[]{:S(2)}, u32[]{:S(2)}) %collective-permute-start.1) | collective-permute-done | bytes 524320 | tf_op jit(solution)/shard_map/ppermute | solution.py:111
  67.7 1.2 add_convert_fusion.10
  68.9 0.1 add_convert_fusion.4
  69.0 2.7 %collective-permute-start.9 = (bf16[1024,256]{1,0:T(8,128)(2,1)S(1)}, bf16[1024,256]{1,0:T(8,128)(2,1)S(1)}, u32[]{:S(2)}, u32[]{:S(2)}) collective-permute-start(bf16[1024,256]{1,0:T(8,128)(2,1)S(1)} %add_convert_fusion.4), channel_id=1, source_target_pairs={{0,14},{1,15},{2,0},{3,1},{4,2},{5,3},{6,4},{7,5},{8,6},{9,7},{10,... | collective-permute-start | bytes 1572872 | tf_op jit(solution)/shard_map/ppermute | solution.py:112
  71.8 0.4 fusion.23
  72.1 9.2 %collective-permute-done.2 = bf16[1024,256]{1,0:T(8,128)(2,1)S(1)} collective-permute-done((bf16[1024,256]{1,0:T(8,128)(2,1)S(1)}, bf16[1024,256]{1,0:T(8,128)(2,1)S(1)}, u32[]{:S(2)}, u32[]{:S(2)}) %collective-permute-start.2) | collective-permute-done | bytes 524320 | tf_op jit(solution)/shard_map/ppermute | solution.py:111
  81.3 0.1 add_convert_fusion.9
  81.5 0.3 collective-permute-start.3
  81.7 0.1 add_convert_fusion.3
  81.9 3.1 %collective-permute-start.10 = (bf16[1024,256]{1,0:T(8,128)(2,1)S(1)}, bf16[1024,256]{1,0:T(8,128)(2,1)S(1)}, u32[]{:S(2)}, u32[]{:S(2)}) collective-permute-start(bf16[1024,256]{1,0:T(8,128)(2,1)S(1)} %add_convert_fusion.3), channel_id=1, source_target_pairs={{0,14},{1,15},{2,0},{3,1},{4,2},{5,3},{6,4},{7,5},{8,6},{9,7},{10,... | collective-permute-start | bytes 1572872 | tf_op jit(solution)/shard_map/ppermute | solution.py:112
  85.0 0.4 fusion.21
  85.3 17.2 %collective-permute-done.3 = bf16[1024,256]{1,0:T(8,128)(2,1)S(1)} collective-permute-done((bf16[1024,256]{1,0:T(8,128)(2,1)S(1)}, bf16[1024,256]{1,0:T(8,128)(2,1)S(1)}, u32[]{:S(2)}, u32[]{:S(2)}) %collective-permute-start.3) | collective-permute-done | bytes 524320 | tf_op jit(solution)/shard_map/ppermute | solution.py:111
  102.5 0.1 add_convert_fusion.8
  102.7 0.1 add_convert_fusion.2
  102.8 2.7 %collective-permute-start.11 = (bf16[1024,256]{1,0:T(8,128)(2,1)S(1)}, bf16[1024,256]{1,0:T(8,128)(2,1)S(1)}, u32[]{:S(2)}, u32[]{:S(2)}) collective-permute-start(bf16[1024,256]{1,0:T(8,128)(2,1)S(1)} %add_convert_fusion.2), channel_id=1, source_target_pairs={{0,14},{1,15},{2,0},{3,1},{4,2},{5,3},{6,4},{7,5},{8,6},{9,7},{10,... | collective-permute-start | bytes 1572872 | tf_op jit(solution)/shard_map/ppermute | solution.py:112
  105.6 0.4 fusion.19
  105.9 11.1 %collective-permute-done.4 = bf16[1024,256]{1,0:T(8,128)(2,1)S(1)} collective-permute-done((bf16[1024,256]{1,0:T(8,128)(2,1)S(1)}, bf16[1024,256]{1,0:T(8,128)(2,1)S(1)}, u32[]{:S(2)}, u32[]{:S(2)}) %collective-permute-start.4) | collective-permute-done | bytes 524320 | tf_op jit(solution)/shard_map/ppermute | solution.py:111
  117.3 0.1 add_convert_fusion.1
  117.4 3.5 %collective-permute-start.12 = (bf16[1024,256]{1,0:T(8,128)(2,1)S(1)}, bf16[1024,256]{1,0:T(8,128)(2,1)S(1)}, u32[]{:S(2)}, u32[]{:S(2)}) collective-permute-start(bf16[1024,256]{1,0:T(8,128)(2,1)S(1)} %add_convert_fusion.1), channel_id=1, source_target_pairs={{0,14},{1,15},{2,0},{3,1},{4,2},{5,3},{6,4},{7,5},{8,6},{9,7},{10,... | collective-permute-start | bytes 1572872 | tf_op jit(solution)/shard_map/ppermute | solution.py:112
  120.9 0.3 fusion.17
  121.2 10.6 %collective-permute-done.5 = bf16[1024,256]{1,0:T(8,128)(2,1)S(1)} collective-permute-done((bf16[1024,256]{1,0:T(8,128)(2,1)S(1)}, bf16[1024,256]{1,0:T(8,128)(2,1)S(1)}, u32[]{:S(2)}, u32[]{:S(2)}) %collective-permute-start.5) | collective-permute-done | bytes 524320 | tf_op jit(solution)/shard_map/ppermute | solution.py:111
  132.0 0.1 add_convert_fusion
  132.2 2.7 %collective-permute-start.13 = (bf16[1024,256]{1,0:T(8,128)(2,1)S(1)}, bf16[1024,256]{1,0:T(8,128)(2,1)S(1)}, u32[]{:S(2)}, u32[]{:S(2)}) collective-permute-start(bf16[1024,256]{1,0:T(8,128)(2,1)S(1)} %add_convert_fusion), channel_id=1, source_target_pairs={{0,14},{1,15},{2,0},{3,1},{4,2},{5,3},{6,4},{7,5},{8,6},{9,7},{10,... | collective-permute-start | bytes 1572872 | tf_op jit(solution)/shard_map/ppermute | solution.py:112
  134.9 0.3 fusion.15
  135.2 22.4 %collective-permute-done.6 = bf16[1024,256]{1,0:T(8,128)(2,1)S(1)} collective-permute-done((bf16[1024,256]{1,0:T(8,128)(2,1)S(1)}, bf16[1024,256]{1,0:T(8,128)(2,1)S(1)}, u32[]{:S(2)}, u32[]{:S(2)}) %collective-permute-start.6) | collective-permute-done | bytes 524320 | tf_op jit(solution)/shard_map/ppermute | solution.py:111
  157.7 0.2 convert_add_fusion
  157.9 0.3 pad_maximum_fusion
  158.2 15.6 %all-gather.3.cloned.1.call-done = bf16[8448,512]{1,0:T(8,128)(2,1)} async-done(((bf16[528,512]{1,0:T(8,128)(2,1)}), bf16[8448,512]{1,0:T(8,128)(2,1)}) %all-gather.3.cloned.1.call-update) | async-done | bytes 8650768 | tf_op jit(solution)/shard_map/all_gather | solution.py:151
  173.8 0.9 dynamic-slice_convert_fusion
  174.7 2.3 collective-permute-start.14
  177.0 1.5 convert_reduce_fusion
  178.5 10.1 %collective-permute-done.14 = bf16[512,512]{1,0:T(8,128)(2,1)} collective-permute-done((bf16[512,512]{1,0:T(8,128)(2,1)}, bf16[512,512]{1,0:T(8,128)(2,1)}, u32[]{:S(2)}, u32[]{:S(2)}) %collective-permute-start.14) | collective-permute-done | bytes 524320 | tf_op jit(solution)/shard_map/ppermute | solution.py:125
  188.6 4.3 %fusion.13 = (bf16[1,512,512]{2,1,0:T(8,128)(2,1)}, bf16[512,512]{1,0:T(8,128)(2,1)S(1)}, bf16[1,512,512]{2,1,0:T(8,128)(2,1)}) fusion(bf16[1,512,512]{2,1,0:T(8,128)(2,1)} %param.15, f32[]{:T(128)} %convert_reduce_fusion, bf16[512,512]{1,0:T(8,128)(2,1)} %collective-permute-done.14, f32[1024,512]{1,0:T(8,128)S(1)} %pad_maximum_fusion, s32[]{:T(128)S(6)} %select_n.227, ...), kind=kLoop, calls=%fused_computation.43 | loop fusion | flops 6029312 | bytes 6291464 | tf_op jit(solution)/shard_map/broadcast_in_dim | solution.py:180
  192.9 17.3 %all_to_all.10 = bf16[16,32,512]{2,1,0:T(8,128)(2,1)S(1)} all-to-all(bf16[16,32,512]{2,1,0:T(8,128)(2,1)S(1)} %bitcast.47), channel_id=1, replica_groups=mesh['replica'=16,'fsdp'=16] {'replica'}, dimensions={0} | all-to-all | bytes 1048576 | tf_op jit(solution)/shard_map/all_to_all | solution.py:43
  210.2 0.8 broadcast_in_dim.6
  211.1 4.8 %all-to-all-start.1 = ((bf16[16,32,512]{2,1,0:T(8,128)(2,1)}), bf16[16,32,512]{2,1,0:T(8,128)(2,1)S(1)}, u32[]{:S(2)}, u32[]{:S(2)}) async-start(bf16[16,32,512]{2,1,0:T(8,128)(2,1)} %broadcast_in_dim.6), calls=%async_computation.1 | async-start | bytes 1048576 | tf_op jit(solution)/shard_map/all_to_all | solution.py:36
  215.9 0.1 copy.17.inv_ref
  216.0 0.8 divide_convert_fusion.scaled_ref
  216.8 2.2 copy-done.1
  219.0 10.2 %shard_map.119 = bf16[256,8192]{1,0:T(8,128)(2,1)} custom-call(bf16[256,512]{1,0:T(8,128)(2,1)S(1)} %divide_convert_fusion.scaled_ref, bf16[16,528,512]{2,1,0:T(8,128)(2,1)} %bitcast.46, bf16[256,8192]{1,0:T(8,128)(2,1)S(1)} %copy-done.1, f32[256,1]{1,0:T(8,128)S(1)} %copy.17.inv_ref), custom_call_target="tpu_custom_call" | custom-call | flops 2147483648 | bytes 17301504 | tf_op jit(solution)/shard_map/pallas_call | solution.py:73
  229.2 0.1 convert_multiply_fusion.2
  229.4 2.9 %fusion.5 = (f32[512,512]{1,0:T(8,128)}, f32[512,512]{1,0:T(8,128)}) fusion(f32[512,512]{1,0:T(8,128)S(1)} %copy-done.7, f32[16,32,512]{2,1,0:T(8,128)S(1)} %convert_multiply_fusion.2, f32[512,512]{1,0:T(8,128)} %param.17), kind=kLoop, calls=%fused_computation.14 | loop fusion | flops 1572864 | bytes 5242880 | tf_op jit(solution)/shard_map/sub | solution.py:178
  (39 shorter events, 1.0 us)
Async XLA Ops:
  7.2 6.3 %copy-start.8 = (bf16[256,512]{1,0:T(8,128)(2,1)S(1)}, bf16[256,512]{1,0:T(8,128)(2,1)}, u32[]{:S(2)}) copy-start(bf16[256,512]{1,0:T(8,128)(2,1)} %param.11) | copy-start | bytes 786436
  7.2 166.6 %all-gather.3.cloned.1.call-start = ((), (), s32[]{:S(2)}) async-start(), calls=%async_computation.2 | async-start | bytes 9191424 | tf_op jit(solution)/shard_map/all_gather | solution.py:151
  10.1 3.5 %copy-start = (bf16[256,8192]{1,0:T(8,128)(2,1)S(1)}, bf16[256,8192]{1,0:T(8,128)(2,1)}, u32[]{:S(2)}) copy-start(bf16[256,8192]{1,0:T(8,128)(2,1)} %act_ref.1) | copy-start | bytes 12582916
  14.7 2.0 copy-start.2
  17.9 22.2 %collective-permute-start = (bf16[1024,256]{1,0:T(8,128)(2,1)}, bf16[1024,256]{1,0:T(8,128)(2,1)}, u32[]{:S(2)}, u32[]{:S(2)}) collective-permute-start(bf16[1024,256]{1,0:T(8,128)(2,1)} %convolution_convert_fusion.1), channel_id=1, source_target_pairs={{0,2},{1,3},{2,4},{3,5},{4,6},{5,7},{6,8},{7,9},{8,10},{9,11},{10,... | collective-permute-start | bytes 1572872 | tf_op jit(solution)/shard_map/ppermute | solution.py:111
  22.5 23.4 %collective-permute-start.7 = (bf16[1024,256]{1,0:T(8,128)(2,1)}, bf16[1024,256]{1,0:T(8,128)(2,1)}, u32[]{:S(2)}, u32[]{:S(2)}) collective-permute-start(bf16[1024,256]{1,0:T(8,128)(2,1)} %convolution_convert_fusion), channel_id=1, source_target_pairs={{0,14},{1,15},{2,0},{3,1},{4,2},{5,3},{6,4},{7,5},{8,6},{9,7},{10,... | collective-permute-start | bytes 1572872 | tf_op jit(solution)/shard_map/ppermute | solution.py:112
  42.5 25.2 %collective-permute-start.1 = (bf16[1024,256]{1,0:T(8,128)(2,1)}, bf16[1024,256]{1,0:T(8,128)(2,1)}, u32[]{:S(2)}, u32[]{:S(2)}) collective-permute-start(bf16[1024,256]{1,0:T(8,128)(2,1)} %add_convert_fusion.11), channel_id=1, source_target_pairs={{0,2},{1,3},{2,4},{3,5},{4,6},{5,7},{6,8},{7,9},{8,10},{9,11},{10,... | collective-permute-start | bytes 1572872 | tf_op jit(solution)/shard_map/ppermute | solution.py:111
  44.8 26.9 %copy-start.3 = (bf16[256,8192]{1,0:T(8,128)(2,1)S(1)}, bf16[256,8192]{1,0:T(8,128)(2,1)}, u32[]{:S(2)}) copy-start(bf16[256,8192]{1,0:T(8,128)(2,1)} %copy-done.2) | copy-start | bytes 12582916
  47.7 21.2 %collective-permute-start.8 = (bf16[1024,256]{1,0:T(8,128)(2,1)S(1)}, bf16[1024,256]{1,0:T(8,128)(2,1)S(1)}, u32[]{:S(2)}, u32[]{:S(2)}) collective-permute-start(bf16[1024,256]{1,0:T(8,128)(2,1)S(1)} %add_convert_fusion.5), channel_id=1, source_target_pairs={{0,14},{1,15},{2,0},{3,1},{4,2},{5,3},{6,4},{7,5},{8,6},{9,7},{10,... | collective-permute-start | bytes 1572872 | tf_op jit(solution)/shard_map/ppermute | solution.py:112
  68.8 12.5 %collective-permute-start.2 = (bf16[1024,256]{1,0:T(8,128)(2,1)S(1)}, bf16[1024,256]{1,0:T(8,128)(2,1)S(1)}, u32[]{:S(2)}, u32[]{:S(2)}) collective-permute-start(bf16[1024,256]{1,0:T(8,128)(2,1)S(1)} %add_convert_fusion.10), channel_id=1, source_target_pairs={{0,2},{1,3},{2,4},{3,5},{4,6},{5,7},{6,8},{7,9},{8,10},{9,11},{10,... | collective-permute-start | bytes 1572872 | tf_op jit(solution)/shard_map/ppermute | solution.py:111
  69.0 12.7 %collective-permute-start.9 = (bf16[1024,256]{1,0:T(8,128)(2,1)S(1)}, bf16[1024,256]{1,0:T(8,128)(2,1)S(1)}, u32[]{:S(2)}, u32[]{:S(2)}) collective-permute-start(bf16[1024,256]{1,0:T(8,128)(2,1)S(1)} %add_convert_fusion.4), channel_id=1, source_target_pairs={{0,14},{1,15},{2,0},{3,1},{4,2},{5,3},{6,4},{7,5},{8,6},{9,7},{10,... | collective-permute-start | bytes 1572872 | tf_op jit(solution)/shard_map/ppermute | solution.py:112
  81.5 21.0 %collective-permute-start.3 = (bf16[1024,256]{1,0:T(8,128)(2,1)S(1)}, bf16[1024,256]{1,0:T(8,128)(2,1)S(1)}, u32[]{:S(2)}, u32[]{:S(2)}) collective-permute-start(bf16[1024,256]{1,0:T(8,128)(2,1)S(1)} %add_convert_fusion.9), channel_id=1, source_target_pairs={{0,2},{1,3},{2,4},{3,5},{4,6},{5,7},{6,8},{7,9},{8,10},{9,11},{10,... | collective-permute-start | bytes 1572872 | tf_op jit(solution)/shard_map/ppermute | solution.py:111
  81.9 35.2 %copy-start.5 = (f32[1024,256]{1,0:T(8,128)S(1)}, f32[1024,256]{1,0:T(8,128)}, u32[]{:S(2)}) copy-start(f32[1024,256]{1,0:T(8,128)} %fusion.36) | copy-start | bytes 3145732
  81.9 20.8 %collective-permute-start.10 = (bf16[1024,256]{1,0:T(8,128)(2,1)S(1)}, bf16[1024,256]{1,0:T(8,128)(2,1)S(1)}, u32[]{:S(2)}, u32[]{:S(2)}) collective-permute-start(bf16[1024,256]{1,0:T(8,128)(2,1)S(1)} %add_convert_fusion.3), channel_id=1, source_target_pairs={{0,14},{1,15},{2,0},{3,1},{4,2},{5,3},{6,4},{7,5},{8,6},{9,7},{10,... | collective-permute-start | bytes 1572872 | tf_op jit(solution)/shard_map/ppermute | solution.py:112
  102.6 14.4 %collective-permute-start.4 = (bf16[1024,256]{1,0:T(8,128)(2,1)S(1)}, bf16[1024,256]{1,0:T(8,128)(2,1)S(1)}, u32[]{:S(2)}, u32[]{:S(2)}) collective-permute-start(bf16[1024,256]{1,0:T(8,128)(2,1)S(1)} %add_convert_fusion.8), channel_id=1, source_target_pairs={{0,2},{1,3},{2,4},{3,5},{4,6},{5,7},{6,8},{7,9},{8,10},{9,11},{10,... | collective-permute-start | bytes 1572872 | tf_op jit(solution)/shard_map/ppermute | solution.py:111
  102.8 29.0 %copy-start.4 = (f32[1024,256]{1,0:T(8,128)S(1)}, f32[1024,256]{1,0:T(8,128)}, u32[]{:S(2)}) copy-start(f32[1024,256]{1,0:T(8,128)} %fusion.34) | copy-start | bytes 3145732
  102.8 14.4 %collective-permute-start.11 = (bf16[1024,256]{1,0:T(8,128)(2,1)S(1)}, bf16[1024,256]{1,0:T(8,128)(2,1)S(1)}, u32[]{:S(2)}, u32[]{:S(2)}) collective-permute-start(bf16[1024,256]{1,0:T(8,128)(2,1)S(1)} %add_convert_fusion.2), channel_id=1, source_target_pairs={{0,14},{1,15},{2,0},{3,1},{4,2},{5,3},{6,4},{7,5},{8,6},{9,7},{10,... | collective-permute-start | bytes 1572872 | tf_op jit(solution)/shard_map/ppermute | solution.py:112
  117.1 14.7 %collective-permute-start.5 = (bf16[1024,256]{1,0:T(8,128)(2,1)S(1)}, bf16[1024,256]{1,0:T(8,128)(2,1)S(1)}, u32[]{:S(2)}, u32[]{:S(2)}) collective-permute-start(bf16[1024,256]{1,0:T(8,128)(2,1)S(1)} %add_convert_fusion.7), channel_id=1, source_target_pairs={{0,2},{1,3},{2,4},{3,5},{4,6},{5,7},{6,8},{7,9},{8,10},{9,11},{10,... | collective-permute-start | bytes 1572872 | tf_op jit(solution)/shard_map/ppermute | solution.py:111
  117.4 40.2 %copy-start.6 = (f32[1024,256]{1,0:T(8,128)S(1)}, f32[1024,256]{1,0:T(8,128)}, u32[]{:S(2)}) copy-start(f32[1024,256]{1,0:T(8,128)} %fusion.32) | copy-start | bytes 3145732
  117.4 14.7 %collective-permute-start.12 = (bf16[1024,256]{1,0:T(8,128)(2,1)S(1)}, bf16[1024,256]{1,0:T(8,128)(2,1)S(1)}, u32[]{:S(2)}, u32[]{:S(2)}) collective-permute-start(bf16[1024,256]{1,0:T(8,128)(2,1)S(1)} %add_convert_fusion.1), channel_id=1, source_target_pairs={{0,14},{1,15},{2,0},{3,1},{4,2},{5,3},{6,4},{7,5},{8,6},{9,7},{10,... | collective-permute-start | bytes 1572872 | tf_op jit(solution)/shard_map/ppermute | solution.py:112
  131.9 25.7 %collective-permute-start.6 = (bf16[1024,256]{1,0:T(8,128)(2,1)S(1)}, bf16[1024,256]{1,0:T(8,128)(2,1)S(1)}, u32[]{:S(2)}, u32[]{:S(2)}) collective-permute-start(bf16[1024,256]{1,0:T(8,128)(2,1)S(1)} %add_convert_fusion.6), channel_id=1, source_target_pairs={{0,2},{1,3},{2,4},{3,5},{4,6},{5,7},{6,8},{7,9},{8,10},{9,11},{10,... | collective-permute-start | bytes 1572872 | tf_op jit(solution)/shard_map/ppermute | solution.py:111
  132.2 25.6 %collective-permute-start.13 = (bf16[1024,256]{1,0:T(8,128)(2,1)S(1)}, bf16[1024,256]{1,0:T(8,128)(2,1)S(1)}, u32[]{:S(2)}, u32[]{:S(2)}) collective-permute-start(bf16[1024,256]{1,0:T(8,128)(2,1)S(1)} %add_convert_fusion), channel_id=1, source_target_pairs={{0,14},{1,15},{2,0},{3,1},{4,2},{5,3},{6,4},{7,5},{8,6},{9,7},{10,... | collective-permute-start | bytes 1572872 | tf_op jit(solution)/shard_map/ppermute | solution.py:112
  157.7 30.9 %copy-start.7 = (f32[512,512]{1,0:T(8,128)S(1)}, f32[512,512]{1,0:T(8,128)}, u32[]{:S(2)}) copy-start(f32[512,512]{1,0:T(8,128)} %param.16) | copy-start | bytes 3145732
  174.7 13.9 %collective-permute-start.14 = (bf16[512,512]{1,0:T(8,128)(2,1)}, bf16[512,512]{1,0:T(8,128)(2,1)}, u32[]{:S(2)}, u32[]{:S(2)}) collective-permute-start(bf16[512,512]{1,0:T(8,128)(2,1)} %dynamic-slice_convert_fusion), channel_id=1, source_target_pairs={{0,1},{1,0},{2,3},{3,2},{4,5},{5,4},{6,7},{7,6},{8,9},{9,8},{10,11... | collective-permute-start | bytes 1572872 | tf_op jit(solution)/shard_map/ppermute | solution.py:125
  178.4 37.6 %copy-start.9 = (bf16[256,512]{1,0:T(8,128)(2,1)S(1)}, bf16[256,512]{1,0:T(8,128)(2,1)}, u32[]{:S(2)}) copy-start(bf16[256,512]{1,0:T(8,128)(2,1)} %param.11) | copy-start | bytes 786436
  211.1 18.2 %all-to-all-start.1 = ((bf16[16,32,512]{2,1,0:T(8,128)(2,1)}), bf16[16,32,512]{2,1,0:T(8,128)(2,1)S(1)}, u32[]{:S(2)}, u32[]{:S(2)}) async-start(bf16[16,32,512]{2,1,0:T(8,128)(2,1)} %broadcast_in_dim.6), calls=%async_computation.1 | async-start | bytes 1048576 | tf_op jit(solution)/shard_map/all_to_all | solution.py:36
  216.8 2.2 copy-start.1
Sparse Core Ops, SparseCore 0:
  10.6 163.1 all-gather.2

commit v9 on v8

--- a/solution.py
+++ b/solution.py
@@ -161,8 +161,9 @@
     all_answer = gathered[:, rows, :tokens].reshape(count * tokens).astype(jnp.float32)
     answers = jnp.sum(all_answer)
     scaled = (cotangent.astype(jnp.float32) * answer[:, None] / answers).astype(jnp.bfloat16)
+    input_grad = input_grad_of(scaled, gathered, activations, inverse)
+    reduced, input_grad = lax.optimization_barrier((reduced, input_grad))
     gradient = width_scale * reduced / answers
-    input_grad = input_grad_of(scaled, gathered, activations, inverse)
     first = beta_first * first_moment[0].astype(jnp.float32) + (1.0 - beta_first) * gradient
     second = (
         beta_second * second_moment[0].astype(jnp.float32)

time: 240 us -> 233 us (0.971)
  blocking collectives: 17.3 us -> 29.1 us
  waiting for transfers between devices: 117 us -> 107 us
  starting transfers between devices: 32.2 us -> 27.7 us
  other arithmetic: 19.8 us -> 17 us
    all_to_all x0 -> x1, blocking collectives: none -> 13.5 us  [gather_rows(): gathered = lax.all_to_all(copies, axis, 0, 0, tiled=True)]
    ppermute x1, waiting for transfers between devices: 10.1 us -> 0.01 us  [pair_sum_rows(): lax.ppermute(theirs.astype(jnp.bfloat16), axis, partner).astype(jnp.float32)]
    all_to_all x1 -> x0, starting transfers between devices: 4.8 us -> none  [gather_rows(): gathered = lax.all_to_all(copies, axis, 0, 0, tiled=True)]
  transfers between devices with their start and end apart: 17 -> 16, of which waited for: 10 -> 9; matrix products, arithmetic and copies ran while one was open for 13% -> 14% of each run, Pallas kernels for 4% -> 4%
where the time goes in v9:
time: 233 us; the launch traced here: 232 us
  waiting for transfers between devices  107 us (46%)
  blocking collectives  29.1 us (12%)
  starting transfers between devices  27.7 us (12%)
  matrix products  22.1 us (9%)
  other arithmetic  17 us (7%)
  between operations  14.6 us (6%)
  Pallas kernels  10.4 us (4%)
  local copies, waits for them, and re-layouts  4.55 us (2%)
    ppermute x7, waiting for transfers between devices, ring_sum_rows(): lax.ppermute(forward.astype(jnp.bfloat16), axis, ahead).astype(jnp.float32)  90 us
    dot_general x16, matrix products, contract_first(): lax.dot_general(left, right, (((0,), (0,)), ((), ())), preferred_element_...  22.1 us
    ppermute x7, starting transfers between devices, ring_sum_rows(): lax.ppermute(backward.astype(jnp.bfloat16), axis, behind)  22 us
    all_gather x1, waiting for transfers between devices, per_device(): gathered = lax.all_gather(packed, 'fsdp', axis=0, tiled=False)  15.7 us
    all_to_all x1, blocking collectives, sum_rows(): received = lax.all_to_all(pieces, axis, 0, 0, tiled=True)  15.6 us
    all_to_all x1, blocking collectives, gather_rows(): gathered = lax.all_to_all(copies, axis, 0, 0, tiled=True)  13.5 us
    pallas_call x1, Pallas kernels, input_grad_of(): pl.pallas_call(input_grad_kernel, out_shape=jax.ShapeDtypeStruct((tokens,...  10.4 us
  transfers between devices with their start and end apart: 16, of which 9 were waited for; matrix products, arithmetic and copies ran while one was open for 14% of the time, Pallas kernels for 4%

profile of v9, /device:TPU:1, one launch (start us, length us, event | category | flops | bytes accessed | tf_op | source)
XLA Modules:
  0.0 232.2 jit_solution(653975954017863508)
XLA Ops:
  7.2 0.7 compare_convert_fusion
  7.9 1.3 bitcast_convert_fusion
  9.2 0.8 fusion.11
  10.2 3.3 %fusion = f32[256]{0:T(256)S(1)} fusion(bf16[256,8192]{1,0:T(8,128)(2,1)} %act_ref.1), kind=kLoop, calls=%fused_computation.2 | loop fusion | flops 6291200 | bytes 4195328 | tf_op jit(solution)/shard_map/reduce_sum | solution.py:153
  13.4 0.1 fusion.48
  13.6 1.1 fusion.1
  14.8 2.0 copy-done.2
  16.8 1.1 convolution_convert_fusion.1
  17.9 2.5 %collective-permute-start = (bf16[1024,256]{1,0:T(8,128)(2,1)}, bf16[1024,256]{1,0:T(8,128)(2,1)}, u32[]{:S(2)}, u32[]{:S(2)}) collective-permute-start(bf16[1024,256]{1,0:T(8,128)(2,1)} %convolution_convert_fusion.1), channel_id=1, source_target_pairs={{0,2},{1,3},{2,4},{3,5},{4,6},{5,7},{6,8},{7,9},{8,10},{9,11},{10,... | collective-permute-start | bytes 1572872 | tf_op jit(solution)/shard_map/ppermute | solution.py:111
  20.4 2.2 convolution_convert_fusion
  22.5 3.9 %collective-permute-start.7 = (bf16[1024,256]{1,0:T(8,128)(2,1)}, bf16[1024,256]{1,0:T(8,128)(2,1)}, u32[]{:S(2)}, u32[]{:S(2)}) collective-permute-start(bf16[1024,256]{1,0:T(8,128)(2,1)} %convolution_convert_fusion), channel_id=1, source_target_pairs={{0,14},{1,15},{2,0},{3,1},{4,2},{5,3},{6,4},{7,5},{8,6},{9,7},{10,... | collective-permute-start | bytes 1572872 | tf_op jit(solution)/shard_map/ppermute | solution.py:112
  26.5 1.4 fusion.42
  27.9 1.5 fusion.40
  29.4 1.4 fusion.38
  30.9 2.4 %fusion.36 = f32[1024,256]{1,0:T(8,128)} fusion(bf16[256,8192]{1,0:T(8,128)(2,1)} %copy-done.2, s32[]{:T(128)S(6)} %select_n.195, bf16[256,512]{1,0:T(8,128)(2,1)S(1)} %fusion.48), kind=kOutput, calls=%fused_computation.66 | convolution fusion | flops 134217728 | bytes 1703940 | tf_op jit(solution)/shard_map/dot_general | solution.py:28
  33.3 2.4 %fusion.34 = f32[1024,256]{1,0:T(8,128)} fusion(bf16[256,8192]{1,0:T(8,128)(2,1)} %copy-done.2, s32[]{:T(128)S(6)} %select_n.198, bf16[256,512]{1,0:T(8,128)(2,1)S(1)} %fusion.48), kind=kOutput, calls=%fused_computation.64 | convolution fusion | flops 134217728 | bytes 1703940 | tf_op jit(solution)/shard_map/dot_general | solution.py:28
  35.7 4.5 %collective-permute-done = bf16[1024,256]{1,0:T(8,128)(2,1)} collective-permute-done((bf16[1024,256]{1,0:T(8,128)(2,1)}, bf16[1024,256]{1,0:T(8,128)(2,1)}, u32[]{:S(2)}, u32[]{:S(2)}) %collective-permute-start) | collective-permute-done | bytes 524320 | tf_op jit(solution)/shard_map/ppermute | solution.py:111
  40.1 2.3 %add_convert_fusion.11 = bf16[1024,256]{1,0:T(8,128)(2,1)} fusion(bf16[1024,256]{1,0:T(8,128)(2,1)} %collective-permute-done, bf16[256,8192]{1,0:T(8,128)(2,1)} %copy-done.2, s32[]{:T(128)S(6)} %select_n.183, bf16[256,512]{1,0:T(8,128)(2,1)S(1)} %fusion.48), kind=kOutput, calls=%fused_computation.40 | convolution fusion | flops 135004160 | bytes 1703940 | tf_op jit(solution)/shard_map/dot_general | solution.py:28
  42.5 2.4 %fusion.32 = f32[1024,256]{1,0:T(8,128)} fusion(bf16[256,8192]{1,0:T(8,128)(2,1)} %copy-done.2, s32[]{:T(128)S(6)} %select_n.201, bf16[256,512]{1,0:T(8,128)(2,1)S(1)} %fusion.48), kind=kOutput, calls=%fused_computation.62 | convolution fusion | flops 134217728 | bytes 1703940 | tf_op jit(solution)/shard_map/dot_general | solution.py:28
  44.8 0.1 copy.17.inv_ref
  45.0 1.0 collective-permute-done.7
  46.0 1.9 add_convert_fusion.5
  47.9 3.2 %collective-permute-start.8 = (bf16[1024,256]{1,0:T(8,128)(2,1)S(1)}, bf16[1024,256]{1,0:T(8,128)(2,1)S(1)}, u32[]{:S(2)}, u32[]{:S(2)}) collective-permute-start(bf16[1024,256]{1,0:T(8,128)(2,1)S(1)} %add_convert_fusion.5), channel_id=1, source_target_pairs={{0,14},{1,15},{2,0},{3,1},{4,2},{5,3},{6,4},{7,5},{8,6},{9,7},{10,... | collective-permute-start | bytes 1572872 | tf_op jit(solution)/shard_map/ppermute | solution.py:112
  51.1 1.4 fusion.25
  52.5 15.2 %collective-permute-done.1 = bf16[1024,256]{1,0:T(8,128)(2,1)} collective-permute-done((bf16[1024,256]{1,0:T(8,128)(2,1)}, bf16[1024,256]{1,0:T(8,128)(2,1)}, u32[]{:S(2)}, u32[]{:S(2)}) %collective-permute-start.1) | collective-permute-done | bytes 524320 | tf_op jit(solution)/shard_map/ppermute | solution.py:111
  67.7 1.2 add_convert_fusion.10
  69.0 0.1 add_convert_fusion.4
  69.1 2.7 %collective-permute-start.9 = (bf16[1024,256]{1,0:T(8,128)(2,1)S(1)}, bf16[1024,256]{1,0:T(8,128)(2,1)S(1)}, u32[]{:S(2)}, u32[]{:S(2)}) collective-permute-start(bf16[1024,256]{1,0:T(8,128)(2,1)S(1)} %add_convert_fusion.4), channel_id=1, source_target_pairs={{0,14},{1,15},{2,0},{3,1},{4,2},{5,3},{6,4},{7,5},{8,6},{9,7},{10,... | collective-permute-start | bytes 1572872 | tf_op jit(solution)/shard_map/ppermute | solution.py:112
  71.8 0.4 fusion.23
  72.2 9.3 %collective-permute-done.2 = bf16[1024,256]{1,0:T(8,128)(2,1)S(1)} collective-permute-done((bf16[1024,256]{1,0:T(8,128)(2,1)S(1)}, bf16[1024,256]{1,0:T(8,128)(2,1)S(1)}, u32[]{:S(2)}, u32[]{:S(2)}) %collective-permute-start.2) | collective-permute-done | bytes 524320 | tf_op jit(solution)/shard_map/ppermute | solution.py:111
  81.5 0.1 add_convert_fusion.9
  81.6 0.3 collective-permute-start.3
  81.9 0.1 add_convert_fusion.3
  82.0 3.2 %collective-permute-start.10 = (bf16[1024,256]{1,0:T(8,128)(2,1)S(1)}, bf16[1024,256]{1,0:T(8,128)(2,1)S(1)}, u32[]{:S(2)}, u32[]{:S(2)}) collective-permute-start(bf16[1024,256]{1,0:T(8,128)(2,1)S(1)} %add_convert_fusion.3), channel_id=1, source_target_pairs={{0,14},{1,15},{2,0},{3,1},{4,2},{5,3},{6,4},{7,5},{8,6},{9,7},{10,... | collective-permute-start | bytes 1572872 | tf_op jit(solution)/shard_map/ppermute | solution.py:112
  85.2 0.3 fusion.21
  85.5 17.0 %collective-permute-done.3 = bf16[1024,256]{1,0:T(8,128)(2,1)S(1)} collective-permute-done((bf16[1024,256]{1,0:T(8,128)(2,1)S(1)}, bf16[1024,256]{1,0:T(8,128)(2,1)S(1)}, u32[]{:S(2)}, u32[]{:S(2)}) %collective-permute-start.3) | collective-permute-done | bytes 524320 | tf_op jit(solution)/shard_map/ppermute | solution.py:111
  102.5 0.1 add_convert_fusion.8
  102.8 0.1 add_convert_fusion.2
  102.9 2.7 %collective-permute-start.11 = (bf16[1024,256]{1,0:T(8,128)(2,1)S(1)}, bf16[1024,256]{1,0:T(8,128)(2,1)S(1)}, u32[]{:S(2)}, u32[]{:S(2)}) collective-permute-start(bf16[1024,256]{1,0:T(8,128)(2,1)S(1)} %add_convert_fusion.2), channel_id=1, source_target_pairs={{0,14},{1,15},{2,0},{3,1},{4,2},{5,3},{6,4},{7,5},{8,6},{9,7},{10,... | collective-permute-start | bytes 1572872 | tf_op jit(solution)/shard_map/ppermute | solution.py:112
  105.6 0.4 fusion.19
  106.0 11.1 %collective-permute-done.4 = bf16[1024,256]{1,0:T(8,128)(2,1)S(1)} collective-permute-done((bf16[1024,256]{1,0:T(8,128)(2,1)S(1)}, bf16[1024,256]{1,0:T(8,128)(2,1)S(1)}, u32[]{:S(2)}, u32[]{:S(2)}) %collective-permute-start.4) | collective-permute-done | bytes 524320 | tf_op jit(solution)/shard_map/ppermute | solution.py:111
  117.1 0.1 add_convert_fusion.7
  117.3 0.1 add_convert_fusion.1
  117.4 3.5 %collective-permute-start.12 = (bf16[1024,256]{1,0:T(8,128)(2,1)S(1)}, bf16[1024,256]{1,0:T(8,128)(2,1)S(1)}, u32[]{:S(2)}, u32[]{:S(2)}) collective-permute-start(bf16[1024,256]{1,0:T(8,128)(2,1)S(1)} %add_convert_fusion.1), channel_id=1, source_target_pairs={{0,14},{1,15},{2,0},{3,1},{4,2},{5,3},{6,4},{7,5},{8,6},{9,7},{10,... | collective-permute-start | bytes 1572872 | tf_op jit(solution)/shard_map/ppermute | solution.py:112
  120.9 0.4 fusion.17
  121.3 10.6 %collective-permute-done.5 = bf16[1024,256]{1,0:T(8,128)(2,1)S(1)} collective-permute-done((bf16[1024,256]{1,0:T(8,128)(2,1)S(1)}, bf16[1024,256]{1,0:T(8,128)(2,1)S(1)}, u32[]{:S(2)}, u32[]{:S(2)}) %collective-permute-start.5) | collective-permute-done | bytes 524320 | tf_op jit(solution)/shard_map/ppermute | solution.py:111
  131.9 0.1 add_convert_fusion.6
  132.1 0.1 add_convert_fusion
  132.2 2.7 %collective-permute-start.13 = (bf16[1024,256]{1,0:T(8,128)(2,1)S(1)}, bf16[1024,256]{1,0:T(8,128)(2,1)S(1)}, u32[]{:S(2)}, u32[]{:S(2)}) collective-permute-start(bf16[1024,256]{1,0:T(8,128)(2,1)S(1)} %add_convert_fusion), channel_id=1, source_target_pairs={{0,14},{1,15},{2,0},{3,1},{4,2},{5,3},{6,4},{7,5},{8,6},{9,7},{10,... | collective-permute-start | bytes 1572872 | tf_op jit(solution)/shard_map/ppermute | solution.py:112
  134.9 0.3 fusion.15
  135.3 22.4 %collective-permute-done.6 = bf16[1024,256]{1,0:T(8,128)(2,1)S(1)} collective-permute-done((bf16[1024,256]{1,0:T(8,128)(2,1)S(1)}, bf16[1024,256]{1,0:T(8,128)(2,1)S(1)}, u32[]{:S(2)}, u32[]{:S(2)}) %collective-permute-start.6) | collective-permute-done | bytes 524320 | tf_op jit(solution)/shard_map/ppermute | solution.py:111
  157.9 0.3 pad_maximum_fusion
  158.2 15.7 %all-gather.3.cloned.1.call-done = bf16[8448,512]{1,0:T(8,128)(2,1)} async-done(((bf16[528,512]{1,0:T(8,128)(2,1)}), bf16[8448,512]{1,0:T(8,128)(2,1)}) %all-gather.3.cloned.1.call-update) | async-done | bytes 8650768 | tf_op jit(solution)/shard_map/all_gather | solution.py:151
  174.0 2.6 %collective-permute-start.14 = (bf16[512,512]{1,0:T(8,128)(2,1)S(1)}, bf16[512,512]{1,0:T(8,128)(2,1)S(1)}, u32[]{:S(2)}, u32[]{:S(2)}) collective-permute-start(bf16[512,512]{1,0:T(8,128)(2,1)S(1)} %dynamic-slice_convert_fusion), channel_id=1, source_target_pairs={{0,1},{1,0},{2,3},{3,2},{4,5},{5,4},{6,7},{7,6},{8,9},{9,8},{10,11... | collective-permute-start | bytes 1572872 | tf_op jit(solution)/shard_map/ppermute | solution.py:125
  176.5 1.5 convert_reduce_fusion
  178.0 0.8 divide_convert_fusion.scaled_ref
  178.8 2.2 copy-done.1
  181.0 10.4 %shard_map.119 = bf16[256,8192]{1,0:T(8,128)(2,1)} custom-call(bf16[256,512]{1,0:T(8,128)(2,1)S(1)} %divide_convert_fusion.scaled_ref, bf16[16,528,512]{2,1,0:T(8,128)(2,1)} %bitcast.46, bf16[256,8192]{1,0:T(8,128)(2,1)S(1)} %copy-done.1, f32[256,1]{1,0:T(8,128)S(1)} %copy.17.inv_ref), custom_call_target="tpu_custom_call" | custom-call | flops 2147483648 | bytes 17301504 | tf_op jit(solution)/shard_map/pallas_call | solution.py:73
  191.4 0.2 convert_add_fusion
  191.6 2.6 %fusion.13 = (bf16[1,512,512]{2,1,0:T(8,128)(2,1)}, bf16[512,512]{1,0:T(8,128)(2,1)S(1)}, bf16[1,512,512]{2,1,0:T(8,128)(2,1)}) fusion(bf16[1,512,512]{2,1,0:T(8,128)(2,1)S(1)} %copy-done.12, f32[]{:T(128)} %convert_reduce_fusion, f32[512,512]{1,0:T(8,128)S(1)} %convert_add_fusion, f32[512,512]{1,0:T(8,128)S(1)} %copy-done.7, ...), kind=kLoop, calls=%fused_computation.44 | loop fusion | flops 5505024 | bytes 5767172 | tf_op jit(solution)/shard_map/broadcast_in_dim | solution.py:181
  194.3 15.6 %all_to_all.10 = bf16[16,32,512]{2,1,0:T(8,128)(2,1)S(1)} all-to-all(bf16[16,32,512]{2,1,0:T(8,128)(2,1)S(1)} %bitcast.47), channel_id=1, replica_groups=mesh['replica'=16,'fsdp'=16] {'replica'}, dimensions={0} | all-to-all | bytes 1048576 | tf_op jit(solution)/shard_map/all_to_all | solution.py:43
  210.0 13.5 %all_to_all.11 = bf16[16,32,512]{2,1,0:T(8,128)(2,1)S(1)} all-to-all(bf16[16,32,512]{2,1,0:T(8,128)(2,1)S(1)} %broadcast_in_dim.6), channel_id=1, replica_groups=mesh['replica'=16,'fsdp'=16] {'replica'}, dimensions={0} | all-to-all | bytes 1048576 | tf_op jit(solution)/shard_map/all_to_all | solution.py:36
  223.5 0.1 convert_multiply_fusion.2
  223.6 1.7 fusion.5
  (47 shorter events, 0.9 us)
Async XLA Ops:
  7.2 6.3 %copy-start.10 = (bf16[256,512]{1,0:T(8,128)(2,1)S(1)}, bf16[256,512]{1,0:T(8,128)(2,1)}, u32[]{:S(2)}) copy-start(bf16[256,512]{1,0:T(8,128)(2,1)} %param.11) | copy-start | bytes 786436
  7.2 166.7 %all-gather.3.cloned.1.call-start = ((), (), s32[]{:S(2)}) async-start(), calls=%async_computation.2 | async-start | bytes 9191424 | tf_op jit(solution)/shard_map/all_gather | solution.py:151
  10.2 3.5 %copy-start = (bf16[256,8192]{1,0:T(8,128)(2,1)S(1)}, bf16[256,8192]{1,0:T(8,128)(2,1)}, u32[]{:S(2)}) copy-start(bf16[256,8192]{1,0:T(8,128)(2,1)} %act_ref.1) | copy-start | bytes 12582916
  14.7 2.0 copy-start.2
  17.9 22.2 %collective-permute-start = (bf16[1024,256]{1,0:T(8,128)(2,1)}, bf16[1024,256]{1,0:T(8,128)(2,1)}, u32[]{:S(2)}, u32[]{:S(2)}) collective-permute-start(bf16[1024,256]{1,0:T(8,128)(2,1)} %convolution_convert_fusion.1), channel_id=1, source_target_pairs={{0,2},{1,3},{2,4},{3,5},{4,6},{5,7},{6,8},{7,9},{8,10},{9,11},{10,... | collective-permute-start | bytes 1572872 | tf_op jit(solution)/shard_map/ppermute | solution.py:111
  22.5 23.5 %collective-permute-start.7 = (bf16[1024,256]{1,0:T(8,128)(2,1)}, bf16[1024,256]{1,0:T(8,128)(2,1)}, u32[]{:S(2)}, u32[]{:S(2)}) collective-permute-start(bf16[1024,256]{1,0:T(8,128)(2,1)} %convolution_convert_fusion), channel_id=1, source_target_pairs={{0,14},{1,15},{2,0},{3,1},{4,2},{5,3},{6,4},{7,5},{8,6},{9,7},{10,... | collective-permute-start | bytes 1572872 | tf_op jit(solution)/shard_map/ppermute | solution.py:112
  42.5 25.3 %collective-permute-start.1 = (bf16[1024,256]{1,0:T(8,128)(2,1)}, bf16[1024,256]{1,0:T(8,128)(2,1)}, u32[]{:S(2)}, u32[]{:S(2)}) collective-permute-start(bf16[1024,256]{1,0:T(8,128)(2,1)} %add_convert_fusion.11), channel_id=1, source_target_pairs={{0,2},{1,3},{2,4},{3,5},{4,6},{5,7},{6,8},{7,9},{8,10},{9,11},{10,... | collective-permute-start | bytes 1572872 | tf_op jit(solution)/shard_map/ppermute | solution.py:111
  45.0 26.8 %copy-start.3 = (bf16[256,8192]{1,0:T(8,128)(2,1)S(1)}, bf16[256,8192]{1,0:T(8,128)(2,1)}, u32[]{:S(2)}) copy-start(bf16[256,8192]{1,0:T(8,128)(2,1)} %copy-done.2) | copy-start | bytes 12582916
  47.9 21.1 %collective-permute-start.8 = (bf16[1024,256]{1,0:T(8,128)(2,1)S(1)}, bf16[1024,256]{1,0:T(8,128)(2,1)S(1)}, u32[]{:S(2)}, u32[]{:S(2)}) collective-permute-start(bf16[1024,256]{1,0:T(8,128)(2,1)S(1)} %add_convert_fusion.5), channel_id=1, source_target_pairs={{0,14},{1,15},{2,0},{3,1},{4,2},{5,3},{6,4},{7,5},{8,6},{9,7},{10,... | collective-permute-start | bytes 1572872 | tf_op jit(solution)/shard_map/ppermute | solution.py:112
  68.9 12.6 %collective-permute-start.2 = (bf16[1024,256]{1,0:T(8,128)(2,1)S(1)}, bf16[1024,256]{1,0:T(8,128)(2,1)S(1)}, u32[]{:S(2)}, u32[]{:S(2)}) collective-permute-start(bf16[1024,256]{1,0:T(8,128)(2,1)S(1)} %add_convert_fusion.10), channel_id=1, source_target_pairs={{0,2},{1,3},{2,4},{3,5},{4,6},{5,7},{6,8},{7,9},{8,10},{9,11},{10,... | collective-permute-start | bytes 1572872 | tf_op jit(solution)/shard_map/ppermute | solution.py:111
  69.1 12.7 %collective-permute-start.9 = (bf16[1024,256]{1,0:T(8,128)(2,1)S(1)}, bf16[1024,256]{1,0:T(8,128)(2,1)S(1)}, u32[]{:S(2)}, u32[]{:S(2)}) collective-permute-start(bf16[1024,256]{1,0:T(8,128)(2,1)S(1)} %add_convert_fusion.4), channel_id=1, source_target_pairs={{0,14},{1,15},{2,0},{3,1},{4,2},{5,3},{6,4},{7,5},{8,6},{9,7},{10,... | collective-permute-start | bytes 1572872 | tf_op jit(solution)/shard_map/ppermute | solution.py:112
  81.6 21.0 %collective-permute-start.3 = (bf16[1024,256]{1,0:T(8,128)(2,1)S(1)}, bf16[1024,256]{1,0:T(8,128)(2,1)S(1)}, u32[]{:S(2)}, u32[]{:S(2)}) collective-permute-start(bf16[1024,256]{1,0:T(8,128)(2,1)S(1)} %add_convert_fusion.9), channel_id=1, source_target_pairs={{0,2},{1,3},{2,4},{3,5},{4,6},{5,7},{6,8},{7,9},{8,10},{9,11},{10,... | collective-permute-start | bytes 1572872 | tf_op jit(solution)/shard_map/ppermute | solution.py:111
  82.0 35.1 %copy-start.5 = (f32[1024,256]{1,0:T(8,128)S(1)}, f32[1024,256]{1,0:T(8,128)}, u32[]{:S(2)}) copy-start(f32[1024,256]{1,0:T(8,128)} %fusion.36) | copy-start | bytes 3145732
  82.0 20.8 %collective-permute-start.10 = (bf16[1024,256]{1,0:T(8,128)(2,1)S(1)}, bf16[1024,256]{1,0:T(8,128)(2,1)S(1)}, u32[]{:S(2)}, u32[]{:S(2)}) collective-permute-start(bf16[1024,256]{1,0:T(8,128)(2,1)S(1)} %add_convert_fusion.3), channel_id=1, source_target_pairs={{0,14},{1,15},{2,0},{3,1},{4,2},{5,3},{6,4},{7,5},{8,6},{9,7},{10,... | collective-permute-start | bytes 1572872 | tf_op jit(solution)/shard_map/ppermute | solution.py:112
  102.7 14.4 %collective-permute-start.4 = (bf16[1024,256]{1,0:T(8,128)(2,1)S(1)}, bf16[1024,256]{1,0:T(8,128)(2,1)S(1)}, u32[]{:S(2)}, u32[]{:S(2)}) collective-permute-start(bf16[1024,256]{1,0:T(8,128)(2,1)S(1)} %add_convert_fusion.8), channel_id=1, source_target_pairs={{0,2},{1,3},{2,4},{3,5},{4,6},{5,7},{6,8},{7,9},{8,10},{9,11},{10,... | collective-permute-start | bytes 1572872 | tf_op jit(solution)/shard_map/ppermute | solution.py:111
  102.9 29.0 %copy-start.4 = (f32[1024,256]{1,0:T(8,128)S(1)}, f32[1024,256]{1,0:T(8,128)}, u32[]{:S(2)}) copy-start(f32[1024,256]{1,0:T(8,128)} %fusion.34) | copy-start | bytes 3145732
  102.9 14.4 %collective-permute-start.11 = (bf16[1024,256]{1,0:T(8,128)(2,1)S(1)}, bf16[1024,256]{1,0:T(8,128)(2,1)S(1)}, u32[]{:S(2)}, u32[]{:S(2)}) collective-permute-start(bf16[1024,256]{1,0:T(8,128)(2,1)S(1)} %add_convert_fusion.2), channel_id=1, source_target_pairs={{0,14},{1,15},{2,0},{3,1},{4,2},{5,3},{6,4},{7,5},{8,6},{9,7},{10,... | collective-permute-start | bytes 1572872 | tf_op jit(solution)/shard_map/ppermute | solution.py:112
  117.2 14.7 %collective-permute-start.5 = (bf16[1024,256]{1,0:T(8,128)(2,1)S(1)}, bf16[1024,256]{1,0:T(8,128)(2,1)S(1)}, u32[]{:S(2)}, u32[]{:S(2)}) collective-permute-start(bf16[1024,256]{1,0:T(8,128)(2,1)S(1)} %add_convert_fusion.7), channel_id=1, source_target_pairs={{0,2},{1,3},{2,4},{3,5},{4,6},{5,7},{6,8},{7,9},{8,10},{9,11},{10,... | collective-permute-start | bytes 1572872 | tf_op jit(solution)/shard_map/ppermute | solution.py:111
  117.4 40.2 %copy-start.6 = (f32[1024,256]{1,0:T(8,128)S(1)}, f32[1024,256]{1,0:T(8,128)}, u32[]{:S(2)}) copy-start(f32[1024,256]{1,0:T(8,128)} %fusion.32) | copy-start | bytes 3145732
  117.4 14.7 %collective-permute-start.12 = (bf16[1024,256]{1,0:T(8,128)(2,1)S(1)}, bf16[1024,256]{1,0:T(8,128)(2,1)S(1)}, u32[]{:S(2)}, u32[]{:S(2)}) collective-permute-start(bf16[1024,256]{1,0:T(8,128)(2,1)S(1)} %add_convert_fusion.1), channel_id=1, source_target_pairs={{0,14},{1,15},{2,0},{3,1},{4,2},{5,3},{6,4},{7,5},{8,6},{9,7},{10,... | collective-permute-start | bytes 1572872 | tf_op jit(solution)/shard_map/ppermute | solution.py:112
  132.0 25.7 %collective-permute-start.6 = (bf16[1024,256]{1,0:T(8,128)(2,1)S(1)}, bf16[1024,256]{1,0:T(8,128)(2,1)S(1)}, u32[]{:S(2)}, u32[]{:S(2)}) collective-permute-start(bf16[1024,256]{1,0:T(8,128)(2,1)S(1)} %add_convert_fusion.6), channel_id=1, source_target_pairs={{0,2},{1,3},{2,4},{3,5},{4,6},{5,7},{6,8},{7,9},{8,10},{9,11},{10,... | collective-permute-start | bytes 1572872 | tf_op jit(solution)/shard_map/ppermute | solution.py:111
  132.2 25.6 %collective-permute-start.13 = (bf16[1024,256]{1,0:T(8,128)(2,1)S(1)}, bf16[1024,256]{1,0:T(8,128)(2,1)S(1)}, u32[]{:S(2)}, u32[]{:S(2)}) collective-permute-start(bf16[1024,256]{1,0:T(8,128)(2,1)S(1)} %add_convert_fusion), channel_id=1, source_target_pairs={{0,14},{1,15},{2,0},{3,1},{4,2},{5,3},{6,4},{7,5},{8,6},{9,7},{10,... | collective-permute-start | bytes 1572872 | tf_op jit(solution)/shard_map/ppermute | solution.py:112
  157.8 20.3 %copy-start.11 = (bf16[256,512]{1,0:T(8,128)(2,1)S(1)}, bf16[256,512]{1,0:T(8,128)(2,1)}, u32[]{:S(2)}) copy-start(bf16[256,512]{1,0:T(8,128)(2,1)} %param.11) | copy-start | bytes 786436
  174.0 17.5 %collective-permute-start.14 = (bf16[512,512]{1,0:T(8,128)(2,1)S(1)}, bf16[512,512]{1,0:T(8,128)(2,1)S(1)}, u32[]{:S(2)}, u32[]{:S(2)}) collective-permute-start(bf16[512,512]{1,0:T(8,128)(2,1)S(1)} %dynamic-slice_convert_fusion), channel_id=1, source_target_pairs={{0,1},{1,0},{2,3},{3,2},{4,5},{5,4},{6,7},{7,6},{8,9},{9,8},{10,11... | collective-permute-start | bytes 1572872 | tf_op jit(solution)/shard_map/ppermute | solution.py:125
  178.8 2.2 copy-start.1
  181.0 10.6 %copy-start.7 = (f32[512,512]{1,0:T(8,128)S(1)}, f32[512,512]{1,0:T(8,128)}, u32[]{:S(2)}) copy-start(f32[512,512]{1,0:T(8,128)} %param.16) | copy-start | bytes 3145732
  181.0 10.6 %copy-start.8 = (f32[1,512,512]{2,1,0:T(8,128)S(1)}, f32[1,512,512]{2,1,0:T(8,128)}, u32[]{:S(2)}) copy-start(f32[1,512,512]{2,1,0:T(8,128)} %param.13) | copy-start | bytes 3145732
  181.0 10.6 %copy-start.12 = (bf16[1,512,512]{2,1,0:T(8,128)(2,1)S(1)}, bf16[1,512,512]{2,1,0:T(8,128)(2,1)}, u32[]{:S(2)}) copy-start(bf16[1,512,512]{2,1,0:T(8,128)(2,1)} %param.15) | copy-start | bytes 1572868
  181.0 10.6 %copy-start.13 = (bf16[1,512,512]{2,1,0:T(8,128)(2,1)S(1)}, bf16[1,512,512]{2,1,0:T(8,128)(2,1)}, u32[]{:S(2)}) copy-start(bf16[1,512,512]{2,1,0:T(8,128)(2,1)} %param.14) | copy-start | bytes 1572868
  191.6 32.0 %copy-start.9 = (f32[512,512]{1,0:T(8,128)S(1)}, f32[512,512]{1,0:T(8,128)}, u32[]{:S(2)}) copy-start(f32[512,512]{1,0:T(8,128)} %param.17) | copy-start | bytes 3145732
Sparse Core Ops, SparseCore 0:
  10.6 163.2 all-gather.2

commit v10 on v9

--- a/solution.py
+++ b/solution.py
@@ -155,8 +155,8 @@
     normed_low = normed.astype(jnp.bfloat16)
     kept = (cotangent.astype(jnp.float32) * answer[:, None]).astype(jnp.bfloat16)
     combined = ring_sum_rows(normed_low, kept, "fsdp")
-    gathered, combined = lax.optimization_barrier((gathered, combined))
     reduced = pair_sum_rows(combined, "fsdp")
+    gathered, reduced = lax.optimization_barrier((gathered, reduced))
     count = gathered.shape[0]
     all_answer = gathered[:, rows, :tokens].reshape(count * tokens).astype(jnp.float32)
     answers = jnp.sum(all_answer)

time: 233 us -> 242 us (1.039)
  blocking collectives: 29.1 us -> 40.7 us
  waiting for transfers between devices: 107 us -> 95.6 us
  starting transfers between devices: 27.7 us -> 34.8 us
    ppermute x7, waiting for transfers between devices: 90 us -> 4.32 us  [ring_sum_rows(): lax.ppermute(forward.astype(jnp.bfloat16), axis, ahead).astype(jnp.float32)]
    ppermute x7, waiting for transfers between devices: 0.99 us -> 77.4 us  [ring_sum_rows(): lax.ppermute(backward.astype(jnp.bfloat16), axis, behind)]
    all_to_all x1, blocking collectives: 15.6 us -> 27.3 us  [sum_rows(): received = lax.all_to_all(pieces, axis, 0, 0, tiled=True)]
    all_gather x1, waiting for transfers between devices: 15.7 us -> 7.37 us  [per_device(): gathered = lax.all_gather(packed, 'fsdp', axis=0, tiled=False)]
    ppermute x1, waiting for transfers between devices: 0.01 us -> 6.53 us  [pair_sum_rows(): lax.ppermute(theirs.astype(jnp.bfloat16), axis, partner).astype(jnp.float32)]
    ppermute x7, starting transfers between devices: 22 us -> 27.9 us  [ring_sum_rows(): lax.ppermute(backward.astype(jnp.bfloat16), axis, behind)]
    ppermute x1, starting transfers between devices: 2.6 us -> 6.02 us  [pair_sum_rows(): lax.ppermute(theirs.astype(jnp.bfloat16), axis, partner).astype(jnp.float32)]
  transfers between devices with their start and end apart: 16 -> 16, of which waited for: 9 -> 10; matrix products, arithmetic and copies ran while one was open for 14% -> 13% of each run, Pallas kernels for 4% -> 0%
where the time goes in v10:
time: 242 us; the launch traced here: 241 us
  waiting for transfers between devices  95.6 us (40%)
  blocking collectives  40.7 us (17%)
  starting transfers between devices  34.8 us (14%)
  matrix products  22 us (9%)
  other arithmetic  18.6 us (8%)
  between operations  14.5 us (6%)
  Pallas kernels  10.4 us (4%)
  local copies, waits for them, and re-layouts  4.48 us (2%)
    ppermute x7, waiting for transfers between devices, ring_sum_rows(): lax.ppermute(backward.astype(jnp.bfloat16), axis, behind)  77.4 us
    ppermute x7, starting transfers between devices, ring_sum_rows(): lax.ppermute(backward.astype(jnp.bfloat16), axis, behind)  27.9 us
    all_to_all x1, blocking collectives, sum_rows(): received = lax.all_to_all(pieces, axis, 0, 0, tiled=True)  27.3 us
    dot_general x16, matrix products, contract_first(): lax.dot_general(left, right, (((0,), (0,)), ((), ())), preferred_element_...  22 us
    all_to_all x1, blocking collectives, gather_rows(): gathered = lax.all_to_all(copies, axis, 0, 0, tiled=True)  13.5 us
    pallas_call x1, Pallas kernels, input_grad_of(): pl.pallas_call(input_grad_kernel, out_shape=jax.ShapeDtypeStruct((tokens,...  10.4 us
    all_gather x1, waiting for transfers between devices, per_device(): gathered = lax.all_gather(packed, 'fsdp', axis=0, tiled=False)  7.37 us
    ppermute x1, waiting for transfers between devices, pair_sum_rows(): lax.ppermute(theirs.astype(jnp.bfloat16), axis, partner).astype(jnp.float32)  6.53 us
  transfers between devices with their start and end apart: 16, of which 10 were waited for; matrix products, arithmetic and copies ran while one was open for 13% of the time, Pallas kernels for 0%

profile of v10, /device:TPU:1, one launch (start us, length us, event | category | flops | bytes accessed | tf_op | source)
XLA Modules:
  0.0 241.2 jit_solution(936444125485365388)
XLA Ops:
  7.2 0.7 compare_convert_fusion
  7.9 1.3 bitcast_convert_fusion
  9.2 0.8 fusion.15
  10.2 3.3 %fusion = f32[256]{0:T(256)S(1)} fusion(bf16[256,8192]{1,0:T(8,128)(2,1)} %act_ref.1), kind=kLoop, calls=%fused_computation.2 | loop fusion | flops 6291200 | bytes 4195328 | tf_op jit(solution)/shard_map/reduce_sum | solution.py:153
  13.4 0.1 fusion.52
  13.6 1.1 fusion.1
  14.8 2.0 copy-done.2
  16.8 1.1 convolution_convert_fusion
  17.9 6.4 %collective-permute-start.7 = (bf16[1024,256]{1,0:T(8,128)(2,1)}, bf16[1024,256]{1,0:T(8,128)(2,1)}, u32[]{:S(2)}, u32[]{:S(2)}) collective-permute-start(bf16[1024,256]{1,0:T(8,128)(2,1)} %convolution_convert_fusion), channel_id=1, source_target_pairs={{0,14},{1,15},{2,0},{3,1},{4,2},{5,3},{6,4},{7,5},{8,6},{9,7},{10,... | collective-permute-start | bytes 1572872 | tf_op jit(solution)/shard_map/ppermute | solution.py:112
  24.3 2.2 convolution_convert_fusion.1
  26.5 1.4 fusion.29
  27.9 1.5 fusion.27
  29.4 1.4 fusion.25
  30.9 2.4 fusion.23
  33.3 2.4 fusion.21
  35.7 5.7 %collective-permute-done.7 = bf16[1024,256]{1,0:T(8,128)(2,1)} collective-permute-done((bf16[1024,256]{1,0:T(8,128)(2,1)}, bf16[1024,256]{1,0:T(8,128)(2,1)}, u32[]{:S(2)}, u32[]{:S(2)}) %collective-permute-start.7) | collective-permute-done | bytes 524320 | tf_op jit(solution)/shard_map/ppermute | solution.py:112
  41.4 2.3 add_convert_fusion.5
  43.7 3.4 %collective-permute-start.8 = (bf16[1024,256]{1,0:T(8,128)(2,1)}, bf16[1024,256]{1,0:T(8,128)(2,1)}, u32[]{:S(2)}, u32[]{:S(2)}) collective-permute-start(bf16[1024,256]{1,0:T(8,128)(2,1)} %add_convert_fusion.5), channel_id=1, source_target_pairs={{0,14},{1,15},{2,0},{3,1},{4,2},{5,3},{6,4},{7,5},{8,6},{9,7},{10,... | collective-permute-start | bytes 1572872 | tf_op jit(solution)/shard_map/ppermute | solution.py:112
  47.2 2.4 fusion.19
  49.6 1.7 add_convert_fusion.11
  51.4 1.4 fusion.46
  52.8 14.4 %collective-permute-done.8 = bf16[1024,256]{1,0:T(8,128)(2,1)} collective-permute-done((bf16[1024,256]{1,0:T(8,128)(2,1)}, bf16[1024,256]{1,0:T(8,128)(2,1)}, u32[]{:S(2)}, u32[]{:S(2)}) %collective-permute-start.8) | collective-permute-done | bytes 524320 | tf_op jit(solution)/shard_map/ppermute | solution.py:112
  67.1 1.2 add_convert_fusion.4
  68.3 3.5 %collective-permute-start.9 = (bf16[1024,256]{1,0:T(8,128)(2,1)S(1)}, bf16[1024,256]{1,0:T(8,128)(2,1)S(1)}, u32[]{:S(2)}, u32[]{:S(2)}) collective-permute-start(bf16[1024,256]{1,0:T(8,128)(2,1)S(1)} %add_convert_fusion.4), channel_id=1, source_target_pairs={{0,14},{1,15},{2,0},{3,1},{4,2},{5,3},{6,4},{7,5},{8,6},{9,7},{10,... | collective-permute-start | bytes 1572872 | tf_op jit(solution)/shard_map/ppermute | solution.py:112
  71.8 0.1 add_convert_fusion.10
  71.9 0.4 collective-permute-start.2
  72.3 0.4 fusion.44
  72.6 8.2 %collective-permute-done.9 = bf16[1024,256]{1,0:T(8,128)(2,1)S(1)} collective-permute-done((bf16[1024,256]{1,0:T(8,128)(2,1)S(1)}, bf16[1024,256]{1,0:T(8,128)(2,1)S(1)}, u32[]{:S(2)}, u32[]{:S(2)}) %collective-permute-start.9) | collective-permute-done | bytes 524320 | tf_op jit(solution)/shard_map/ppermute | solution.py:112
  80.8 0.1 add_convert_fusion.3
  80.9 3.8 %collective-permute-start.10 = (bf16[1024,256]{1,0:T(8,128)(2,1)S(1)}, bf16[1024,256]{1,0:T(8,128)(2,1)S(1)}, u32[]{:S(2)}, u32[]{:S(2)}) collective-permute-start(bf16[1024,256]{1,0:T(8,128)(2,1)S(1)} %add_convert_fusion.3), channel_id=1, source_target_pairs={{0,14},{1,15},{2,0},{3,1},{4,2},{5,3},{6,4},{7,5},{8,6},{9,7},{10,... | collective-permute-start | bytes 1572872 | tf_op jit(solution)/shard_map/ppermute | solution.py:112
  84.7 0.1 add_convert_fusion.9
  84.8 0.1 collective-permute-start.3
  85.0 0.4 fusion.42
  85.3 12.5 %collective-permute-done.10 = bf16[1024,256]{1,0:T(8,128)(2,1)S(1)} collective-permute-done((bf16[1024,256]{1,0:T(8,128)(2,1)S(1)}, bf16[1024,256]{1,0:T(8,128)(2,1)S(1)}, u32[]{:S(2)}, u32[]{:S(2)}) %collective-permute-start.10) | collective-permute-done | bytes 524320 | tf_op jit(solution)/shard_map/ppermute | solution.py:112
  97.8 0.1 add_convert_fusion.2
  97.9 3.6 %collective-permute-start.11 = (bf16[1024,256]{1,0:T(8,128)(2,1)S(1)}, bf16[1024,256]{1,0:T(8,128)(2,1)S(1)}, u32[]{:S(2)}, u32[]{:S(2)}) collective-permute-start(bf16[1024,256]{1,0:T(8,128)(2,1)S(1)} %add_convert_fusion.2), channel_id=1, source_target_pairs={{0,14},{1,15},{2,0},{3,1},{4,2},{5,3},{6,4},{7,5},{8,6},{9,7},{10,... | collective-permute-start | bytes 1572872 | tf_op jit(solution)/shard_map/ppermute | solution.py:112
  101.5 0.1 add_convert_fusion.8
  101.8 0.4 fusion.40
  102.1 9.1 %collective-permute-done.11 = bf16[1024,256]{1,0:T(8,128)(2,1)S(1)} collective-permute-done((bf16[1024,256]{1,0:T(8,128)(2,1)S(1)}, bf16[1024,256]{1,0:T(8,128)(2,1)S(1)}, u32[]{:S(2)}, u32[]{:S(2)}) %collective-permute-start.11) | collective-permute-done | bytes 524320 | tf_op jit(solution)/shard_map/ppermute | solution.py:112
  111.2 0.1 add_convert_fusion.1
  111.3 3.6 %collective-permute-start.12 = (bf16[1024,256]{1,0:T(8,128)(2,1)S(1)}, bf16[1024,256]{1,0:T(8,128)(2,1)S(1)}, u32[]{:S(2)}, u32[]{:S(2)}) collective-permute-start(bf16[1024,256]{1,0:T(8,128)(2,1)S(1)} %add_convert_fusion.1), channel_id=1, source_target_pairs={{0,14},{1,15},{2,0},{3,1},{4,2},{5,3},{6,4},{7,5},{8,6},{9,7},{10,... | collective-permute-start | bytes 1572872 | tf_op jit(solution)/shard_map/ppermute | solution.py:112
  114.9 0.1 add_convert_fusion.7
  115.1 0.4 fusion.38
  115.5 9.1 %collective-permute-done.12 = bf16[1024,256]{1,0:T(8,128)(2,1)S(1)} collective-permute-done((bf16[1024,256]{1,0:T(8,128)(2,1)S(1)}, bf16[1024,256]{1,0:T(8,128)(2,1)S(1)}, u32[]{:S(2)}, u32[]{:S(2)}) %collective-permute-start.12) | collective-permute-done | bytes 524320 | tf_op jit(solution)/shard_map/ppermute | solution.py:112
  124.6 0.1 add_convert_fusion
  124.7 3.6 %collective-permute-start.13 = (bf16[1024,256]{1,0:T(8,128)(2,1)S(1)}, bf16[1024,256]{1,0:T(8,128)(2,1)S(1)}, u32[]{:S(2)}, u32[]{:S(2)}) collective-permute-start(bf16[1024,256]{1,0:T(8,128)(2,1)S(1)} %add_convert_fusion), channel_id=1, source_target_pairs={{0,14},{1,15},{2,0},{3,1},{4,2},{5,3},{6,4},{7,5},{8,6},{9,7},{10,... | collective-permute-start | bytes 1572872 | tf_op jit(solution)/shard_map/ppermute | solution.py:112
  128.3 0.1 add_convert_fusion.6
  128.5 0.4 fusion.36
  128.9 18.5 %collective-permute-done.13 = bf16[1024,256]{1,0:T(8,128)(2,1)S(1)} collective-permute-done((bf16[1024,256]{1,0:T(8,128)(2,1)S(1)}, bf16[1024,256]{1,0:T(8,128)(2,1)S(1)}, u32[]{:S(2)}, u32[]{:S(2)}) %collective-permute-start.13) | collective-permute-done | bytes 524320 | tf_op jit(solution)/shard_map/ppermute | solution.py:112
  147.4 4.3 %collective-permute-done.6 = bf16[1024,256]{1,0:T(8,128)(2,1)S(1)} collective-permute-done((bf16[1024,256]{1,0:T(8,128)(2,1)S(1)}, bf16[1024,256]{1,0:T(8,128)(2,1)S(1)}, u32[]{:S(2)}, u32[]{:S(2)}) %collective-permute-start.6) | collective-permute-done | bytes 524320 | tf_op jit(solution)/shard_map/ppermute | solution.py:111
  151.9 6.0 %collective-permute-start.14 = (bf16[512,512]{1,0:T(8,128)(2,1)S(1)}, bf16[512,512]{1,0:T(8,128)(2,1)}, u32[]{:S(2)}, u32[]{:S(2)}) collective-permute-start(bf16[512,512]{1,0:T(8,128)(2,1)S(1)} %fusion.5), channel_id=1, source_target_pairs={{0,1},{1,0},{2,3},{3,2},{4,5},{5,4},{6,7},{7,6},{8,9},{9,8},{10,11... | collective-permute-start | bytes 1572872 | tf_op jit(solution)/shard_map/ppermute | solution.py:125
  157.9 0.1 copy.17.inv_ref
  158.1 6.5 %collective-permute-done.14 = bf16[512,512]{1,0:T(8,128)(2,1)} collective-permute-done((bf16[512,512]{1,0:T(8,128)(2,1)S(1)}, bf16[512,512]{1,0:T(8,128)(2,1)}, u32[]{:S(2)}, u32[]{:S(2)}) %collective-permute-start.14) | collective-permute-done | bytes 524320 | tf_op jit(solution)/shard_map/ppermute | solution.py:125
  164.6 1.2 fusion.7
  165.8 7.4 %all-gather.3.cloned.1.call-done = bf16[8448,512]{1,0:T(8,128)(2,1)} async-done(((bf16[528,512]{1,0:T(8,128)(2,1)}), bf16[8448,512]{1,0:T(8,128)(2,1)}) %all-gather.3.cloned.1.call-update) | async-done | bytes 8650768 | tf_op jit(solution)/shard_map/all_gather | solution.py:151
  173.2 1.5 convert_reduce_fusion
  174.7 1.7 divide_convert_fusion.scaled_ref
  176.4 2.2 copy-done.1
  178.6 10.4 %shard_map.119 = bf16[256,8192]{1,0:T(8,128)(2,1)} custom-call(bf16[256,512]{1,0:T(8,128)(2,1)S(1)} %divide_convert_fusion.scaled_ref, bf16[16,528,512]{2,1,0:T(8,128)(2,1)} %bitcast.46, bf16[256,8192]{1,0:T(8,128)(2,1)S(1)} %copy-done.1, f32[256,1]{1,0:T(8,128)S(1)} %copy.17.inv_ref), custom_call_target="tpu_custom_call" | custom-call | flops 2147483648 | bytes 17301504 | tf_op jit(solution)/shard_map/pallas_call | solution.py:73
  189.0 2.5 %fusion.17 = (bf16[1,512,512]{2,1,0:T(8,128)(2,1)}, bf16[512,512]{1,0:T(8,128)(2,1)S(1)}, bf16[1,512,512]{2,1,0:T(8,128)(2,1)}) fusion(bf16[1,512,512]{2,1,0:T(8,128)(2,1)S(1)} %copy-done.11, f32[]{:T(128)} %convert_reduce_fusion, f32[512,512]{1,0:T(8,128)S(1)} %fusion.7, f32[512,512]{1,0:T(8,128)S(1)} %copy-done.7, bf16[1,512,512]{2,1,0:T(8,128)(2,1)S(1)} %copy-done.12, ...), kind=kLoop, calls=%fused_computation.49 | loop fusion | flops 5505024 | bytes 5767172 | tf_op jit(solution)/shard_map/broadcast_in_dim | solution.py:181
  191.6 27.3 %all_to_all.10 = bf16[16,32,512]{2,1,0:T(8,128)(2,1)S(1)} all-to-all(bf16[16,32,512]{2,1,0:T(8,128)(2,1)S(1)} %bitcast.47), channel_id=1, replica_groups=mesh['replica'=16,'fsdp'=16] {'replica'}, dimensions={0} | all-to-all | bytes 1048576 | tf_op jit(solution)/shard_map/all_to_all | solution.py:43
  219.0 13.5 %all_to_all.11 = bf16[16,32,512]{2,1,0:T(8,128)(2,1)S(1)} all-to-all(bf16[16,32,512]{2,1,0:T(8,128)(2,1)S(1)} %broadcast_in_dim.6), channel_id=1, replica_groups=mesh['replica'=16,'fsdp'=16] {'replica'}, dimensions={0} | all-to-all | bytes 1048576 | tf_op jit(solution)/shard_map/all_to_all | solution.py:36
  232.4 0.1 convert_multiply_fusion.2
  232.6 1.7 fusion.9
  (44 shorter events, 0.9 us)
Async XLA Ops:
  7.2 6.3 %copy-start.10 = (bf16[256,512]{1,0:T(8,128)(2,1)S(1)}, bf16[256,512]{1,0:T(8,128)(2,1)}, u32[]{:S(2)}) copy-start(bf16[256,512]{1,0:T(8,128)(2,1)} %param.11) | copy-start | bytes 786436
  7.2 166.0 %all-gather.3.cloned.1.call-start = ((), (), s32[]{:S(2)}) async-start(), calls=%async_computation.2 | async-start | bytes 9191424 | tf_op jit(solution)/shard_map/all_gather | solution.py:151
  10.2 3.5 %copy-start = (bf16[256,8192]{1,0:T(8,128)(2,1)S(1)}, bf16[256,8192]{1,0:T(8,128)(2,1)}, u32[]{:S(2)}) copy-start(bf16[256,8192]{1,0:T(8,128)(2,1)} %act_ref.1) | copy-start | bytes 12582916
  14.7 2.0 copy-start.2
  17.9 23.5 %collective-permute-start.7 = (bf16[1024,256]{1,0:T(8,128)(2,1)}, bf16[1024,256]{1,0:T(8,128)(2,1)}, u32[]{:S(2)}, u32[]{:S(2)}) collective-permute-start(bf16[1024,256]{1,0:T(8,128)(2,1)} %convolution_convert_fusion), channel_id=1, source_target_pairs={{0,14},{1,15},{2,0},{3,1},{4,2},{5,3},{6,4},{7,5},{8,6},{9,7},{10,... | collective-permute-start | bytes 1572872 | tf_op jit(solution)/shard_map/ppermute | solution.py:112
  26.5 23.1 %collective-permute-start = (bf16[1024,256]{1,0:T(8,128)(2,1)}, bf16[1024,256]{1,0:T(8,128)(2,1)}, u32[]{:S(2)}, u32[]{:S(2)}) collective-permute-start(bf16[1024,256]{1,0:T(8,128)(2,1)} %convolution_convert_fusion.1), channel_id=1, source_target_pairs={{0,2},{1,3},{2,4},{3,5},{4,6},{5,7},{6,8},{7,9},{8,10},{9,11},{10,... | collective-permute-start | bytes 1572872 | tf_op jit(solution)/shard_map/ppermute | solution.py:111
  43.7 23.4 %collective-permute-start.8 = (bf16[1024,256]{1,0:T(8,128)(2,1)}, bf16[1024,256]{1,0:T(8,128)(2,1)}, u32[]{:S(2)}, u32[]{:S(2)}) collective-permute-start(bf16[1024,256]{1,0:T(8,128)(2,1)} %add_convert_fusion.5), channel_id=1, source_target_pairs={{0,14},{1,15},{2,0},{3,1},{4,2},{5,3},{6,4},{7,5},{8,6},{9,7},{10,... | collective-permute-start | bytes 1572872 | tf_op jit(solution)/shard_map/ppermute | solution.py:112
  49.5 22.7 %copy-start.3 = (bf16[256,8192]{1,0:T(8,128)(2,1)S(1)}, bf16[256,8192]{1,0:T(8,128)(2,1)}, u32[]{:S(2)}) copy-start(bf16[256,8192]{1,0:T(8,128)(2,1)} %copy-done.2) | copy-start | bytes 12582916
  51.3 20.5 %collective-permute-start.1 = (bf16[1024,256]{1,0:T(8,128)(2,1)S(1)}, bf16[1024,256]{1,0:T(8,128)(2,1)S(1)}, u32[]{:S(2)}, u32[]{:S(2)}) collective-permute-start(bf16[1024,256]{1,0:T(8,128)(2,1)S(1)} %add_convert_fusion.11), channel_id=1, source_target_pairs={{0,2},{1,3},{2,4},{3,5},{4,6},{5,7},{6,8},{7,9},{8,10},{9,11},{10,... | collective-permute-start | bytes 1572872 | tf_op jit(solution)/shard_map/ppermute | solution.py:111
  68.3 12.5 %collective-permute-start.9 = (bf16[1024,256]{1,0:T(8,128)(2,1)S(1)}, bf16[1024,256]{1,0:T(8,128)(2,1)S(1)}, u32[]{:S(2)}, u32[]{:S(2)}) collective-permute-start(bf16[1024,256]{1,0:T(8,128)(2,1)S(1)} %add_convert_fusion.4), channel_id=1, source_target_pairs={{0,14},{1,15},{2,0},{3,1},{4,2},{5,3},{6,4},{7,5},{8,6},{9,7},{10,... | collective-permute-start | bytes 1572872 | tf_op jit(solution)/shard_map/ppermute | solution.py:112
  71.9 12.8 %collective-permute-start.2 = (bf16[1024,256]{1,0:T(8,128)(2,1)S(1)}, bf16[1024,256]{1,0:T(8,128)(2,1)S(1)}, u32[]{:S(2)}, u32[]{:S(2)}) collective-permute-start(bf16[1024,256]{1,0:T(8,128)(2,1)S(1)} %add_convert_fusion.10), channel_id=1, source_target_pairs={{0,2},{1,3},{2,4},{3,5},{4,6},{5,7},{6,8},{7,9},{8,10},{9,11},{10,... | collective-permute-start | bytes 1572872 | tf_op jit(solution)/shard_map/ppermute | solution.py:111
  80.9 16.9 %collective-permute-start.10 = (bf16[1024,256]{1,0:T(8,128)(2,1)S(1)}, bf16[1024,256]{1,0:T(8,128)(2,1)S(1)}, u32[]{:S(2)}, u32[]{:S(2)}) collective-permute-start(bf16[1024,256]{1,0:T(8,128)(2,1)S(1)} %add_convert_fusion.3), channel_id=1, source_target_pairs={{0,14},{1,15},{2,0},{3,1},{4,2},{5,3},{6,4},{7,5},{8,6},{9,7},{10,... | collective-permute-start | bytes 1572872 | tf_op jit(solution)/shard_map/ppermute | solution.py:112
  84.8 26.4 %copy-start.5 = (f32[1024,256]{1,0:T(8,128)S(1)}, f32[1024,256]{1,0:T(8,128)}, u32[]{:S(2)}) copy-start(f32[1024,256]{1,0:T(8,128)} %fusion.23) | copy-start | bytes 3145732
  84.8 16.7 %collective-permute-start.3 = (bf16[1024,256]{1,0:T(8,128)(2,1)S(1)}, bf16[1024,256]{1,0:T(8,128)(2,1)S(1)}, u32[]{:S(2)}, u32[]{:S(2)}) collective-permute-start(bf16[1024,256]{1,0:T(8,128)(2,1)S(1)} %add_convert_fusion.9), channel_id=1, source_target_pairs={{0,2},{1,3},{2,4},{3,5},{4,6},{5,7},{6,8},{7,9},{8,10},{9,11},{10,... | collective-permute-start | bytes 1572872 | tf_op jit(solution)/shard_map/ppermute | solution.py:111
  97.9 13.3 %collective-permute-start.11 = (bf16[1024,256]{1,0:T(8,128)(2,1)S(1)}, bf16[1024,256]{1,0:T(8,128)(2,1)S(1)}, u32[]{:S(2)}, u32[]{:S(2)}) collective-permute-start(bf16[1024,256]{1,0:T(8,128)(2,1)S(1)} %add_convert_fusion.2), channel_id=1, source_target_pairs={{0,14},{1,15},{2,0},{3,1},{4,2},{5,3},{6,4},{7,5},{8,6},{9,7},{10,... | collective-permute-start | bytes 1572872 | tf_op jit(solution)/shard_map/ppermute | solution.py:112
  101.7 22.9 %copy-start.4 = (f32[1024,256]{1,0:T(8,128)S(1)}, f32[1024,256]{1,0:T(8,128)}, u32[]{:S(2)}) copy-start(f32[1024,256]{1,0:T(8,128)} %fusion.21) | copy-start | bytes 3145732
  101.7 13.3 %collective-permute-start.4 = (bf16[1024,256]{1,0:T(8,128)(2,1)S(1)}, bf16[1024,256]{1,0:T(8,128)(2,1)S(1)}, u32[]{:S(2)}, u32[]{:S(2)}) collective-permute-start(bf16[1024,256]{1,0:T(8,128)(2,1)S(1)} %add_convert_fusion.8), channel_id=1, source_target_pairs={{0,2},{1,3},{2,4},{3,5},{4,6},{5,7},{6,8},{7,9},{8,10},{9,11},{10,... | collective-permute-start | bytes 1572872 | tf_op jit(solution)/shard_map/ppermute | solution.py:111
  111.3 13.3 %collective-permute-start.12 = (bf16[1024,256]{1,0:T(8,128)(2,1)S(1)}, bf16[1024,256]{1,0:T(8,128)(2,1)S(1)}, u32[]{:S(2)}, u32[]{:S(2)}) collective-permute-start(bf16[1024,256]{1,0:T(8,128)(2,1)S(1)} %add_convert_fusion.1), channel_id=1, source_target_pairs={{0,14},{1,15},{2,0},{3,1},{4,2},{5,3},{6,4},{7,5},{8,6},{9,7},{10,... | collective-permute-start | bytes 1572872 | tf_op jit(solution)/shard_map/ppermute | solution.py:112
  115.0 32.3 %copy-start.6 = (f32[1024,256]{1,0:T(8,128)S(1)}, f32[1024,256]{1,0:T(8,128)}, u32[]{:S(2)}) copy-start(f32[1024,256]{1,0:T(8,128)} %fusion.19) | copy-start | bytes 3145732
  115.1 13.3 %collective-permute-start.5 = (bf16[1024,256]{1,0:T(8,128)(2,1)S(1)}, bf16[1024,256]{1,0:T(8,128)(2,1)S(1)}, u32[]{:S(2)}, u32[]{:S(2)}) collective-permute-start(bf16[1024,256]{1,0:T(8,128)(2,1)S(1)} %add_convert_fusion.7), channel_id=1, source_target_pairs={{0,2},{1,3},{2,4},{3,5},{4,6},{5,7},{6,8},{7,9},{8,10},{9,11},{10,... | collective-permute-start | bytes 1572872 | tf_op jit(solution)/shard_map/ppermute | solution.py:111
  124.7 22.6 %collective-permute-start.13 = (bf16[1024,256]{1,0:T(8,128)(2,1)S(1)}, bf16[1024,256]{1,0:T(8,128)(2,1)S(1)}, u32[]{:S(2)}, u32[]{:S(2)}) collective-permute-start(bf16[1024,256]{1,0:T(8,128)(2,1)S(1)} %add_convert_fusion), channel_id=1, source_target_pairs={{0,14},{1,15},{2,0},{3,1},{4,2},{5,3},{6,4},{7,5},{8,6},{9,7},{10,... | collective-permute-start | bytes 1572872 | tf_op jit(solution)/shard_map/ppermute | solution.py:112
  128.4 23.3 %collective-permute-start.6 = (bf16[1024,256]{1,0:T(8,128)(2,1)S(1)}, bf16[1024,256]{1,0:T(8,128)(2,1)S(1)}, u32[]{:S(2)}, u32[]{:S(2)}) collective-permute-start(bf16[1024,256]{1,0:T(8,128)(2,1)S(1)} %add_convert_fusion.6), channel_id=1, source_target_pairs={{0,2},{1,3},{2,4},{3,5},{4,6},{5,7},{6,8},{7,9},{8,10},{9,11},{10,... | collective-permute-start | bytes 1572872 | tf_op jit(solution)/shard_map/ppermute | solution.py:111
  151.9 12.7 %collective-permute-start.14 = (bf16[512,512]{1,0:T(8,128)(2,1)S(1)}, bf16[512,512]{1,0:T(8,128)(2,1)}, u32[]{:S(2)}, u32[]{:S(2)}) collective-permute-start(bf16[512,512]{1,0:T(8,128)(2,1)S(1)} %fusion.5), channel_id=1, source_target_pairs={{0,1},{1,0},{2,3},{3,2},{4,5},{5,4},{6,7},{7,6},{8,9},{9,8},{10,11... | collective-permute-start | bytes 1572872 | tf_op jit(solution)/shard_map/ppermute | solution.py:125
  176.4 2.2 copy-start.1
  178.6 10.4 %copy-start.7 = (f32[512,512]{1,0:T(8,128)S(1)}, f32[512,512]{1,0:T(8,128)}, u32[]{:S(2)}) copy-start(f32[512,512]{1,0:T(8,128)} %param.16) | copy-start | bytes 3145732
  178.6 10.4 %copy-start.8 = (f32[1,512,512]{2,1,0:T(8,128)S(1)}, f32[1,512,512]{2,1,0:T(8,128)}, u32[]{:S(2)}) copy-start(f32[1,512,512]{2,1,0:T(8,128)} %param.13) | copy-start | bytes 3145732
  178.6 10.4 %copy-start.11 = (bf16[1,512,512]{2,1,0:T(8,128)(2,1)S(1)}, bf16[1,512,512]{2,1,0:T(8,128)(2,1)}, u32[]{:S(2)}) copy-start(bf16[1,512,512]{2,1,0:T(8,128)(2,1)} %param.15) | copy-start | bytes 1572868
  178.6 10.4 %copy-start.12 = (bf16[1,512,512]{2,1,0:T(8,128)(2,1)S(1)}, bf16[1,512,512]{2,1,0:T(8,128)(2,1)}, u32[]{:S(2)}) copy-start(bf16[1,512,512]{2,1,0:T(8,128)(2,1)} %param.14) | copy-start | bytes 1572868
  191.6 41.0 %copy-start.9 = (f32[512,512]{1,0:T(8,128)S(1)}, f32[512,512]{1,0:T(8,128)}, u32[]{:S(2)}) copy-start(f32[512,512]{1,0:T(8,128)} %param.17) | copy-start | bytes 3145732
Sparse Core Ops, SparseCore 0:
  10.6 162.5 all-gather.2

commit v11 on v10

--- a/solution.py
+++ b/solution.py
@@ -146,20 +146,17 @@
     answer = (labels >= 0).astype(jnp.float32)
     rows, width = weight_low.shape
     tokens = cotangent.shape[0]
-    flags = jnp.zeros((16, width), jnp.bfloat16).at[0, :tokens].set(answer.astype(jnp.bfloat16))
-    packed = jnp.concatenate([weight_low, flags], axis=0)
-    gathered = lax.all_gather(packed, "fsdp", axis=0, tiled=False)
+    gathered = lax.all_gather(weight_low, "fsdp", axis=0, tiled=False)
+    all_labels = gather_rows(labels, "fsdp")
     values = activations.astype(jnp.float32)
     inverse = lax.rsqrt(jnp.mean(values * values, axis=1, keepdims=True) + norm_eps)
     normed = values * inverse
     normed_low = normed.astype(jnp.bfloat16)
     kept = (cotangent.astype(jnp.float32) * answer[:, None]).astype(jnp.bfloat16)
     combined = ring_sum_rows(normed_low, kept, "fsdp")
+    gathered, combined, all_labels = lax.optimization_barrier((gathered, combined, all_labels))
     reduced = pair_sum_rows(combined, "fsdp")
-    gathered, reduced = lax.optimization_barrier((gathered, reduced))
-    count = gathered.shape[0]
-    all_answer = gathered[:, rows, :tokens].reshape(count * tokens).astype(jnp.float32)
-    answers = jnp.sum(all_answer)
+    answers = jnp.sum((all_labels >= 0).astype(jnp.float32))
     scaled = (cotangent.astype(jnp.float32) * answer[:, None] / answers).astype(jnp.bfloat16)
     input_grad = input_grad_of(scaled, gathered, activations, inverse)
     reduced, input_grad = lax.optimization_barrier((reduced, input_grad))

time: 242 us -> 231 us (0.955)
  blocking collectives: 40.7 us -> 28.9 us
  other arithmetic: 18.6 us -> 15.4 us
    ppermute x7, waiting for transfers between devices: 77.4 us -> 1.63 us  [ring_sum_rows(): lax.ppermute(backward.astype(jnp.bfloat16), axis, behind)]
    ppermute x7, waiting for transfers between devices: 4.32 us -> 79.1 us  [ring_sum_rows(): lax.ppermute(forward.astype(jnp.bfloat16), axis, ahead).astype(jnp.float32)]
    all_to_all x1, blocking collectives: 27.3 us -> 15.5 us  [sum_rows(): received = lax.all_to_all(pieces, axis, 0, 0, tiled=True)]
    all_gather x1, waiting for transfers between devices: 7.37 us -> 16.7 us  [per_device(): gathered = lax.all_gather(weight_low, 'fsdp', axis=0, tiled=False)]
    all_to_all x0 -> x1, starting transfers between devices: none -> 8.02 us  [gather_rows(): gathered = lax.all_to_all(copies, axis, 0, 0, tiled=True)]
    ppermute x7, starting transfers between devices: 27.9 us -> 20 us  [ring_sum_rows(): lax.ppermute(backward.astype(jnp.bfloat16), axis, behind)]
    ppermute x1, waiting for transfers between devices: 6.53 us -> 0.01 us  [pair_sum_rows(): lax.ppermute(theirs.astype(jnp.bfloat16), axis, partner).astype(jnp.float32)]
    ppermute x1, starting transfers between devices: 6.02 us -> 2.18 us  [pair_sum_rows(): lax.ppermute(theirs.astype(jnp.bfloat16), axis, partner).astype(jnp.float32)]
  transfers between devices with their start and end apart: 16 -> 17, of which waited for: 10 -> 8; matrix products, arithmetic and copies ran while one was open for 13% -> 14% of each run, Pallas kernels for 0% -> 5%
where the time goes in v11:
time: 231 us; the launch traced here: 230 us
  waiting for transfers between devices  97.5 us (42%)
  starting transfers between devices  34.5 us (15%)
  blocking collectives  28.9 us (13%)
  matrix products  21.9 us (9%)
  other arithmetic  15.4 us (7%)
  between operations  14.8 us (6%)
  Pallas kernels  10.5 us (5%)
  local copies, waits for them, and re-layouts  6.36 us (3%)
    ppermute x7, waiting for transfers between devices, ring_sum_rows(): lax.ppermute(forward.astype(jnp.bfloat16), axis, ahead).astype(jnp.float32)  79.1 us
    dot_general x16, matrix products, contract_first(): lax.dot_general(left, right, (((0,), (0,)), ((), ())), preferred_element_...  21.9 us
    ppermute x7, starting transfers between devices, ring_sum_rows(): lax.ppermute(backward.astype(jnp.bfloat16), axis, behind)  20 us
    all_gather x1, waiting for transfers between devices, per_device(): gathered = lax.all_gather(weight_low, 'fsdp', axis=0, tiled=False)  16.7 us
    all_to_all x1, blocking collectives, sum_rows(): received = lax.all_to_all(pieces, axis, 0, 0, tiled=True)  15.5 us
    all_to_all x1, blocking collectives, gather_rows(): gathered = lax.all_to_all(copies, axis, 0, 0, tiled=True)  13.5 us
    pallas_call x1, Pallas kernels, input_grad_of(): pl.pallas_call(input_grad_kernel, out_shape=jax.ShapeDtypeStruct((tokens,...  10.5 us
    all_to_all x1, starting transfers between devices, gather_rows(): gathered = lax.all_to_all(copies, axis, 0, 0, tiled=True)  8.02 us
  transfers between devices with their start and end apart: 17, of which 8 were waited for; matrix products, arithmetic and copies ran while one was open for 14% of the time, Pallas kernels for 5%

profile of v11, /device:TPU:1, one launch (start us, length us, event | category | flops | bytes accessed | tf_op | source)
XLA Modules:
  0.0 229.9 jit_solution(13838190782459506424)
XLA Ops:
  7.2 2.1 convert_element_type.139
  9.4 3.3 %fusion = f32[256]{0:T(256)S(1)} fusion(bf16[256,8192]{1,0:T(8,128)(2,1)} %act_ref.1), kind=kLoop, calls=%fused_computation.2 | loop fusion | flops 6291200 | bytes 4195328 | tf_op jit(solution)/shard_map/reduce_sum | solution.py:152
  12.7 0.6 copy-done.14
  13.5 1.1 fusion.1
  14.6 2.0 copy-done.2
  16.6 1.1 convolution_convert_fusion.1
  17.8 2.5 %collective-permute-start = (bf16[1024,256]{1,0:T(8,128)(2,1)}, bf16[1024,256]{1,0:T(8,128)(2,1)}, u32[]{:S(2)}, u32[]{:S(2)}) collective-permute-start(bf16[1024,256]{1,0:T(8,128)(2,1)} %convolution_convert_fusion.1), channel_id=1, source_target_pairs={{0,2},{1,3},{2,4},{3,5},{4,6},{5,7},{6,8},{7,9},{8,10},{9,11},{10,... | collective-permute-start | bytes 1572872 | tf_op jit(solution)/shard_map/ppermute | solution.py:111
  20.2 2.2 convolution_convert_fusion
  22.4 3.9 %collective-permute-start.7 = (bf16[1024,256]{1,0:T(8,128)(2,1)}, bf16[1024,256]{1,0:T(8,128)(2,1)}, u32[]{:S(2)}, u32[]{:S(2)}) collective-permute-start(bf16[1024,256]{1,0:T(8,128)(2,1)} %convolution_convert_fusion), channel_id=1, source_target_pairs={{0,14},{1,15},{2,0},{3,1},{4,2},{5,3},{6,4},{7,5},{8,6},{9,7},{10,... | collective-permute-start | bytes 1572872 | tf_op jit(solution)/shard_map/ppermute | solution.py:112
  26.3 0.6 broadcast_in_dim.8
  27.0 8.0 %all-to-all-start = ((s32[16,1,256]{2,1,0:T(1,128)}), s32[16,1,256]{2,1,0:T(1,128)S(1)}, u32[]{:S(2)}, u32[]{:S(2)}) async-start(s32[16,1,256]{2,1,0:T(1,128)} %broadcast_in_dim.8), calls=%async_computation | async-start | bytes 32768 | tf_op jit(solution)/shard_map/all_to_all | solution.py:36
  35.1 1.4 fusion.40
  36.5 1.4 fusion.38
  37.9 1.4 fusion.36
  39.4 2.4 %fusion.34 = f32[1024,256]{1,0:T(8,128)} fusion(bf16[256,8192]{1,0:T(8,128)(2,1)} %copy-done.2, s32[]{:T(128)S(6)} %select_n.195, bf16[256,512]{1,0:T(8,128)(2,1)S(1)} %fusion.46), kind=kOutput, calls=%fused_computation.62 | convolution fusion | flops 134217728 | bytes 1703940 | tf_op jit(solution)/shard_map/dot_general | solution.py:28
  41.8 2.4 %fusion.32 = f32[1024,256]{1,0:T(8,128)} fusion(bf16[256,8192]{1,0:T(8,128)(2,1)} %copy-done.2, s32[]{:T(128)S(6)} %select_n.198, bf16[256,512]{1,0:T(8,128)(2,1)S(1)} %fusion.46), kind=kOutput, calls=%fused_computation.60 | convolution fusion | flops 134217728 | bytes 1703940 | tf_op jit(solution)/shard_map/dot_general | solution.py:28
  44.2 2.4 %add_convert_fusion.11 = bf16[1024,256]{1,0:T(8,128)(2,1)} fusion(bf16[1024,256]{1,0:T(8,128)(2,1)} %collective-permute-done, bf16[256,8192]{1,0:T(8,128)(2,1)} %copy-done.2, s32[]{:T(128)S(6)} %select_n.183, bf16[256,512]{1,0:T(8,128)(2,1)S(1)} %fusion.46), kind=kOutput, calls=%fused_computation.37 | convolution fusion | flops 135004160 | bytes 1703940 | tf_op jit(solution)/shard_map/dot_general | solution.py:28
  46.6 1.3 collective-permute-start.1
  47.9 2.4 %fusion.30 = f32[1024,256]{1,0:T(8,128)} fusion(bf16[256,8192]{1,0:T(8,128)(2,1)} %copy-done.2, s32[]{:T(128)S(6)} %select_n.201, bf16[256,512]{1,0:T(8,128)(2,1)S(1)} %fusion.46), kind=kOutput, calls=%fused_computation.58 | convolution fusion | flops 134217728 | bytes 1703940 | tf_op jit(solution)/shard_map/dot_general | solution.py:28
  50.2 0.8 copy.20.inv_ref
  51.1 1.7 add_convert_fusion.5
  52.8 1.5 collective-permute-start.8
  54.3 1.4 fusion.23
  55.7 14.4 %collective-permute-done.1 = bf16[1024,256]{1,0:T(8,128)(2,1)} collective-permute-done((bf16[1024,256]{1,0:T(8,128)(2,1)}, bf16[1024,256]{1,0:T(8,128)(2,1)}, u32[]{:S(2)}, u32[]{:S(2)}) %collective-permute-start.1) | collective-permute-done | bytes 524320 | tf_op jit(solution)/shard_map/ppermute | solution.py:111
  70.2 1.2 add_convert_fusion.10
  71.4 0.1 add_convert_fusion.4
  71.6 2.7 %collective-permute-start.9 = (bf16[1024,256]{1,0:T(8,128)(2,1)S(1)}, bf16[1024,256]{1,0:T(8,128)(2,1)S(1)}, u32[]{:S(2)}, u32[]{:S(2)}) collective-permute-start(bf16[1024,256]{1,0:T(8,128)(2,1)S(1)} %add_convert_fusion.4), channel_id=1, source_target_pairs={{0,14},{1,15},{2,0},{3,1},{4,2},{5,3},{6,4},{7,5},{8,6},{9,7},{10,... | collective-permute-start | bytes 1572872 | tf_op jit(solution)/shard_map/ppermute | solution.py:112
  74.3 0.3 fusion.21
  74.6 12.4 %collective-permute-done.2 = bf16[1024,256]{1,0:T(8,128)(2,1)S(1)} collective-permute-done((bf16[1024,256]{1,0:T(8,128)(2,1)S(1)}, bf16[1024,256]{1,0:T(8,128)(2,1)S(1)}, u32[]{:S(2)}, u32[]{:S(2)}) %collective-permute-start.2) | collective-permute-done | bytes 524320 | tf_op jit(solution)/shard_map/ppermute | solution.py:111
  87.0 0.1 add_convert_fusion.9
  87.1 0.3 collective-permute-start.3
  87.4 1.6 collective-permute-done.9
  89.0 0.1 add_convert_fusion.3
  89.1 3.6 %collective-permute-start.10 = (bf16[1024,256]{1,0:T(8,128)(2,1)S(1)}, bf16[1024,256]{1,0:T(8,128)(2,1)S(1)}, u32[]{:S(2)}, u32[]{:S(2)}) collective-permute-start(bf16[1024,256]{1,0:T(8,128)(2,1)S(1)} %add_convert_fusion.3), channel_id=1, source_target_pairs={{0,14},{1,15},{2,0},{3,1},{4,2},{5,3},{6,4},{7,5},{8,6},{9,7},{10,... | collective-permute-start | bytes 1572872 | tf_op jit(solution)/shard_map/ppermute | solution.py:112
  92.7 0.4 fusion.19
  93.1 10.1 %collective-permute-done.3 = bf16[1024,256]{1,0:T(8,128)(2,1)S(1)} collective-permute-done((bf16[1024,256]{1,0:T(8,128)(2,1)S(1)}, bf16[1024,256]{1,0:T(8,128)(2,1)S(1)}, u32[]{:S(2)}, u32[]{:S(2)}) %collective-permute-start.3) | collective-permute-done | bytes 524320 | tf_op jit(solution)/shard_map/ppermute | solution.py:111
  103.2 0.1 add_convert_fusion.8
  103.4 0.1 add_convert_fusion.2
  103.6 2.7 %collective-permute-start.11 = (bf16[1024,256]{1,0:T(8,128)(2,1)S(1)}, bf16[1024,256]{1,0:T(8,128)(2,1)S(1)}, u32[]{:S(2)}, u32[]{:S(2)}) collective-permute-start(bf16[1024,256]{1,0:T(8,128)(2,1)S(1)} %add_convert_fusion.2), channel_id=1, source_target_pairs={{0,14},{1,15},{2,0},{3,1},{4,2},{5,3},{6,4},{7,5},{8,6},{9,7},{10,... | collective-permute-start | bytes 1572872 | tf_op jit(solution)/shard_map/ppermute | solution.py:112
  106.3 0.3 fusion.17
  106.7 10.5 %collective-permute-done.4 = bf16[1024,256]{1,0:T(8,128)(2,1)S(1)} collective-permute-done((bf16[1024,256]{1,0:T(8,128)(2,1)S(1)}, bf16[1024,256]{1,0:T(8,128)(2,1)S(1)}, u32[]{:S(2)}, u32[]{:S(2)}) %collective-permute-start.4) | collective-permute-done | bytes 524320 | tf_op jit(solution)/shard_map/ppermute | solution.py:111
  117.2 0.1 add_convert_fusion.7
  117.4 0.1 add_convert_fusion.1
  117.5 2.7 %collective-permute-start.12 = (bf16[1024,256]{1,0:T(8,128)(2,1)S(1)}, bf16[1024,256]{1,0:T(8,128)(2,1)S(1)}, u32[]{:S(2)}, u32[]{:S(2)}) collective-permute-start(bf16[1024,256]{1,0:T(8,128)(2,1)S(1)} %add_convert_fusion.1), channel_id=1, source_target_pairs={{0,14},{1,15},{2,0},{3,1},{4,2},{5,3},{6,4},{7,5},{8,6},{9,7},{10,... | collective-permute-start | bytes 1572872 | tf_op jit(solution)/shard_map/ppermute | solution.py:112
  120.3 0.3 fusion.15
  120.6 10.1 %collective-permute-done.5 = bf16[1024,256]{1,0:T(8,128)(2,1)S(1)} collective-permute-done((bf16[1024,256]{1,0:T(8,128)(2,1)S(1)}, bf16[1024,256]{1,0:T(8,128)(2,1)S(1)}, u32[]{:S(2)}, u32[]{:S(2)}) %collective-permute-start.5) | collective-permute-done | bytes 524320 | tf_op jit(solution)/shard_map/ppermute | solution.py:111
  130.7 0.1 add_convert_fusion.6
  130.9 0.1 add_convert_fusion
  131.0 2.7 %collective-permute-start.13 = (bf16[1024,256]{1,0:T(8,128)(2,1)S(1)}, bf16[1024,256]{1,0:T(8,128)(2,1)S(1)}, u32[]{:S(2)}, u32[]{:S(2)}) collective-permute-start(bf16[1024,256]{1,0:T(8,128)(2,1)S(1)} %add_convert_fusion), channel_id=1, source_target_pairs={{0,14},{1,15},{2,0},{3,1},{4,2},{5,3},{6,4},{7,5},{8,6},{9,7},{10,... | collective-permute-start | bytes 1572872 | tf_op jit(solution)/shard_map/ppermute | solution.py:112
  133.7 0.3 fusion.13
  134.1 21.6 %collective-permute-done.6 = bf16[1024,256]{1,0:T(8,128)(2,1)S(1)} collective-permute-done((bf16[1024,256]{1,0:T(8,128)(2,1)S(1)}, bf16[1024,256]{1,0:T(8,128)(2,1)S(1)}, u32[]{:S(2)}, u32[]{:S(2)}) %collective-permute-start.6) | collective-permute-done | bytes 524320 | tf_op jit(solution)/shard_map/ppermute | solution.py:111
  155.9 0.3 pad_maximum_fusion
  156.3 16.7 %all-gather.2.cloned.1.call-done.gathered_ref = bf16[16,512,512]{2,1,0:T(8,128)(2,1)} async-done(((bf16[1,512,512]{2,1,0:T(8,128)(2,1)}), bf16[16,512,512]{2,1,0:T(8,128)(2,1)}) %all-gather.2.cloned.1.call-update) | async-done | bytes 8388624 | tf_op jit(solution)/shard_map/all_gather | solution.py:149
  173.0 2.2 collective-permute-start.14
  175.2 0.6 convert_reduce_fusion
  175.8 0.8 divide_convert_fusion.scaled_ref
  176.6 2.2 copy-done.1
  178.8 10.5 %shard_map.119 = bf16[256,8192]{1,0:T(8,128)(2,1)} custom-call(bf16[256,512]{1,0:T(8,128)(2,1)S(1)} %divide_convert_fusion.scaled_ref, bf16[16,512,512]{2,1,0:T(8,128)(2,1)} %all-gather.2.cloned.1.call-done.gathered_ref, bf16[256,8192]{1,0:T(8,128)(2,1)S(1)} %copy-done.1, f32[256,1]{1,0:T(8,128)S(1)} %copy.20.inv_ref), custom_call_target="tpu_custom_call" | custom-call | flops 2147483648 | bytes 17039360 | tf_op jit(solution)/shard_map/pallas_call | solution.py:73
  189.3 0.2 convert_add_fusion
  189.5 2.6 %fusion.11 = (bf16[1,512,512]{2,1,0:T(8,128)(2,1)}, bf16[512,512]{1,0:T(8,128)(2,1)S(1)}, bf16[1,512,512]{2,1,0:T(8,128)(2,1)}) fusion(bf16[1,512,512]{2,1,0:T(8,128)(2,1)S(1)} %copy-done.12, f32[]{:T(128)} %convert_reduce_fusion, f32[512,512]{1,0:T(8,128)S(1)} %convert_add_fusion, f32[512,512]{1,0:T(8,128)S(1)} %copy-done.7, ...), kind=kLoop, calls=%fused_computation.40 | loop fusion | flops 5505024 | bytes 5767172 | tf_op jit(solution)/shard_map/broadcast_in_dim | solution.py:178
  192.2 15.5 %all_to_all.16 = bf16[16,32,512]{2,1,0:T(8,128)(2,1)S(1)} all-to-all(bf16[16,32,512]{2,1,0:T(8,128)(2,1)S(1)} %bitcast.44), channel_id=1, replica_groups=mesh['replica'=16,'fsdp'=16] {'replica'}, dimensions={0} | all-to-all | bytes 1048576 | tf_op jit(solution)/shard_map/all_to_all | solution.py:43
  207.8 13.5 %all_to_all.17 = bf16[16,32,512]{2,1,0:T(8,128)(2,1)S(1)} all-to-all(bf16[16,32,512]{2,1,0:T(8,128)(2,1)S(1)} %broadcast_in_dim.9), channel_id=1, replica_groups=mesh['replica'=16,'fsdp'=16] {'replica'}, dimensions={0} | all-to-all | bytes 1048576 | tf_op jit(solution)/shard_map/all_to_all | solution.py:36
  221.2 0.1 convert_multiply_fusion.2
  221.4 1.7 fusion.4
  (56 shorter events, 1.0 us)
Async XLA Ops:
  7.2 5.5 %copy-start.17 = (s32[256]{0:T(256)S(1)}, s32[256]{0:T(256)}, u32[]{:S(2)}) copy-start(s32[256]{0:T(256)} %param.10) | copy-start | bytes 3076
  7.2 6.2 %copy-start.10 = (bf16[256,512]{1,0:T(8,128)(2,1)S(1)}, bf16[256,512]{1,0:T(8,128)(2,1)}, u32[]{:S(2)}) copy-start(bf16[256,512]{1,0:T(8,128)(2,1)} %param.9) | copy-start | bytes 786436
  7.2 165.8 %all-gather.2.cloned.1.call-start = ((), (), s32[]{:S(2)}) async-start(), calls=%async_computation.3 | async-start | bytes 8912896 | tf_op jit(solution)/shard_map/all_gather | solution.py:149
  9.4 4.0 %copy-start = (bf16[256,8192]{1,0:T(8,128)(2,1)S(1)}, bf16[256,8192]{1,0:T(8,128)(2,1)}, u32[]{:S(2)}) copy-start(bf16[256,8192]{1,0:T(8,128)(2,1)} %act_ref.1) | copy-start | bytes 12582916
  12.7 1.9 copy-start.16
  12.7 0.6 copy-start.14
  14.6 2.0 copy-start.2
  17.8 26.5 %collective-permute-start = (bf16[1024,256]{1,0:T(8,128)(2,1)}, bf16[1024,256]{1,0:T(8,128)(2,1)}, u32[]{:S(2)}, u32[]{:S(2)}) collective-permute-start(bf16[1024,256]{1,0:T(8,128)(2,1)} %convolution_convert_fusion.1), channel_id=1, source_target_pairs={{0,2},{1,3},{2,4},{3,5},{4,6},{5,7},{6,8},{7,9},{8,10},{9,11},{10,... | collective-permute-start | bytes 1572872 | tf_op jit(solution)/shard_map/ppermute | solution.py:111
  22.4 28.7 %collective-permute-start.7 = (bf16[1024,256]{1,0:T(8,128)(2,1)}, bf16[1024,256]{1,0:T(8,128)(2,1)}, u32[]{:S(2)}, u32[]{:S(2)}) collective-permute-start(bf16[1024,256]{1,0:T(8,128)(2,1)} %convolution_convert_fusion), channel_id=1, source_target_pairs={{0,14},{1,15},{2,0},{3,1},{4,2},{5,3},{6,4},{7,5},{8,6},{9,7},{10,... | collective-permute-start | bytes 1572872 | tf_op jit(solution)/shard_map/ppermute | solution.py:112
  27.0 129.3 %all-to-all-start = ((s32[16,1,256]{2,1,0:T(1,128)}), s32[16,1,256]{2,1,0:T(1,128)S(1)}, u32[]{:S(2)}, u32[]{:S(2)}) async-start(s32[16,1,256]{2,1,0:T(1,128)} %broadcast_in_dim.8), calls=%async_computation | async-start | bytes 32768 | tf_op jit(solution)/shard_map/all_to_all | solution.py:36
  46.6 23.6 %collective-permute-start.1 = (bf16[1024,256]{1,0:T(8,128)(2,1)}, bf16[1024,256]{1,0:T(8,128)(2,1)}, u32[]{:S(2)}, u32[]{:S(2)}) collective-permute-start(bf16[1024,256]{1,0:T(8,128)(2,1)} %add_convert_fusion.11), channel_id=1, source_target_pairs={{0,2},{1,3},{2,4},{3,5},{4,6},{5,7},{6,8},{7,9},{8,10},{9,11},{10,... | collective-permute-start | bytes 1572872 | tf_op jit(solution)/shard_map/ppermute | solution.py:111
  51.1 23.2 %copy-start.3 = (bf16[256,8192]{1,0:T(8,128)(2,1)S(1)}, bf16[256,8192]{1,0:T(8,128)(2,1)}, u32[]{:S(2)}) copy-start(bf16[256,8192]{1,0:T(8,128)(2,1)} %copy-done.2) | copy-start | bytes 12582916
  52.8 18.6 %collective-permute-start.8 = (bf16[1024,256]{1,0:T(8,128)(2,1)S(1)}, bf16[1024,256]{1,0:T(8,128)(2,1)S(1)}, u32[]{:S(2)}, u32[]{:S(2)}) collective-permute-start(bf16[1024,256]{1,0:T(8,128)(2,1)S(1)} %add_convert_fusion.5), channel_id=1, source_target_pairs={{0,14},{1,15},{2,0},{3,1},{4,2},{5,3},{6,4},{7,5},{8,6},{9,7},{10,... | collective-permute-start | bytes 1572872 | tf_op jit(solution)/shard_map/ppermute | solution.py:112
  71.3 15.7 %collective-permute-start.2 = (bf16[1024,256]{1,0:T(8,128)(2,1)S(1)}, bf16[1024,256]{1,0:T(8,128)(2,1)S(1)}, u32[]{:S(2)}, u32[]{:S(2)}) collective-permute-start(bf16[1024,256]{1,0:T(8,128)(2,1)S(1)} %add_convert_fusion.10), channel_id=1, source_target_pairs={{0,2},{1,3},{2,4},{3,5},{4,6},{5,7},{6,8},{7,9},{8,10},{9,11},{10,... | collective-permute-start | bytes 1572872 | tf_op jit(solution)/shard_map/ppermute | solution.py:111
  71.6 17.4 %collective-permute-start.9 = (bf16[1024,256]{1,0:T(8,128)(2,1)S(1)}, bf16[1024,256]{1,0:T(8,128)(2,1)S(1)}, u32[]{:S(2)}, u32[]{:S(2)}) collective-permute-start(bf16[1024,256]{1,0:T(8,128)(2,1)S(1)} %add_convert_fusion.4), channel_id=1, source_target_pairs={{0,14},{1,15},{2,0},{3,1},{4,2},{5,3},{6,4},{7,5},{8,6},{9,7},{10,... | collective-permute-start | bytes 1572872 | tf_op jit(solution)/shard_map/ppermute | solution.py:112
  87.1 16.1 %collective-permute-start.3 = (bf16[1024,256]{1,0:T(8,128)(2,1)S(1)}, bf16[1024,256]{1,0:T(8,128)(2,1)S(1)}, u32[]{:S(2)}, u32[]{:S(2)}) collective-permute-start(bf16[1024,256]{1,0:T(8,128)(2,1)S(1)} %add_convert_fusion.9), channel_id=1, source_target_pairs={{0,2},{1,3},{2,4},{3,5},{4,6},{5,7},{6,8},{7,9},{8,10},{9,11},{10,... | collective-permute-start | bytes 1572872 | tf_op jit(solution)/shard_map/ppermute | solution.py:111
  89.1 28.1 %copy-start.5 = (f32[1024,256]{1,0:T(8,128)S(1)}, f32[1024,256]{1,0:T(8,128)}, u32[]{:S(2)}) copy-start(f32[1024,256]{1,0:T(8,128)} %fusion.34) | copy-start | bytes 3145732
  89.1 14.3 %collective-permute-start.10 = (bf16[1024,256]{1,0:T(8,128)(2,1)S(1)}, bf16[1024,256]{1,0:T(8,128)(2,1)S(1)}, u32[]{:S(2)}, u32[]{:S(2)}) collective-permute-start(bf16[1024,256]{1,0:T(8,128)(2,1)S(1)} %add_convert_fusion.3), channel_id=1, source_target_pairs={{0,14},{1,15},{2,0},{3,1},{4,2},{5,3},{6,4},{7,5},{8,6},{9,7},{10,... | collective-permute-start | bytes 1572872 | tf_op jit(solution)/shard_map/ppermute | solution.py:112
  103.3 13.8 %collective-permute-start.4 = (bf16[1024,256]{1,0:T(8,128)(2,1)S(1)}, bf16[1024,256]{1,0:T(8,128)(2,1)S(1)}, u32[]{:S(2)}, u32[]{:S(2)}) collective-permute-start(bf16[1024,256]{1,0:T(8,128)(2,1)S(1)} %add_convert_fusion.8), channel_id=1, source_target_pairs={{0,2},{1,3},{2,4},{3,5},{4,6},{5,7},{6,8},{7,9},{8,10},{9,11},{10,... | collective-permute-start | bytes 1572872 | tf_op jit(solution)/shard_map/ppermute | solution.py:111
  103.6 27.1 %copy-start.4 = (f32[1024,256]{1,0:T(8,128)S(1)}, f32[1024,256]{1,0:T(8,128)}, u32[]{:S(2)}) copy-start(f32[1024,256]{1,0:T(8,128)} %fusion.32) | copy-start | bytes 3145732
  103.6 13.8 %collective-permute-start.11 = (bf16[1024,256]{1,0:T(8,128)(2,1)S(1)}, bf16[1024,256]{1,0:T(8,128)(2,1)S(1)}, u32[]{:S(2)}, u32[]{:S(2)}) collective-permute-start(bf16[1024,256]{1,0:T(8,128)(2,1)S(1)} %add_convert_fusion.2), channel_id=1, source_target_pairs={{0,14},{1,15},{2,0},{3,1},{4,2},{5,3},{6,4},{7,5},{8,6},{9,7},{10,... | collective-permute-start | bytes 1572872 | tf_op jit(solution)/shard_map/ppermute | solution.py:112
  117.3 13.4 %collective-permute-start.5 = (bf16[1024,256]{1,0:T(8,128)(2,1)S(1)}, bf16[1024,256]{1,0:T(8,128)(2,1)S(1)}, u32[]{:S(2)}, u32[]{:S(2)}) collective-permute-start(bf16[1024,256]{1,0:T(8,128)(2,1)S(1)} %add_convert_fusion.7), channel_id=1, source_target_pairs={{0,2},{1,3},{2,4},{3,5},{4,6},{5,7},{6,8},{7,9},{8,10},{9,11},{10,... | collective-permute-start | bytes 1572872 | tf_op jit(solution)/shard_map/ppermute | solution.py:111
  117.5 38.2 %copy-start.6 = (f32[1024,256]{1,0:T(8,128)S(1)}, f32[1024,256]{1,0:T(8,128)}, u32[]{:S(2)}) copy-start(f32[1024,256]{1,0:T(8,128)} %fusion.30) | copy-start | bytes 3145732
  117.5 13.4 %collective-permute-start.12 = (bf16[1024,256]{1,0:T(8,128)(2,1)S(1)}, bf16[1024,256]{1,0:T(8,128)(2,1)S(1)}, u32[]{:S(2)}, u32[]{:S(2)}) collective-permute-start(bf16[1024,256]{1,0:T(8,128)(2,1)S(1)} %add_convert_fusion.1), channel_id=1, source_target_pairs={{0,14},{1,15},{2,0},{3,1},{4,2},{5,3},{6,4},{7,5},{8,6},{9,7},{10,... | collective-permute-start | bytes 1572872 | tf_op jit(solution)/shard_map/ppermute | solution.py:112
  130.8 24.9 %collective-permute-start.6 = (bf16[1024,256]{1,0:T(8,128)(2,1)S(1)}, bf16[1024,256]{1,0:T(8,128)(2,1)S(1)}, u32[]{:S(2)}, u32[]{:S(2)}) collective-permute-start(bf16[1024,256]{1,0:T(8,128)(2,1)S(1)} %add_convert_fusion.6), channel_id=1, source_target_pairs={{0,2},{1,3},{2,4},{3,5},{4,6},{5,7},{6,8},{7,9},{8,10},{9,11},{10,... | collective-permute-start | bytes 1572872 | tf_op jit(solution)/shard_map/ppermute | solution.py:111
  131.0 24.8 %collective-permute-start.13 = (bf16[1024,256]{1,0:T(8,128)(2,1)S(1)}, bf16[1024,256]{1,0:T(8,128)(2,1)S(1)}, u32[]{:S(2)}, u32[]{:S(2)}) collective-permute-start(bf16[1024,256]{1,0:T(8,128)(2,1)S(1)} %add_convert_fusion), channel_id=1, source_target_pairs={{0,14},{1,15},{2,0},{3,1},{4,2},{5,3},{6,4},{7,5},{8,6},{9,7},{10,... | collective-permute-start | bytes 1572872 | tf_op jit(solution)/shard_map/ppermute | solution.py:112
  155.8 20.0 %copy-start.11 = (bf16[256,512]{1,0:T(8,128)(2,1)S(1)}, bf16[256,512]{1,0:T(8,128)(2,1)}, u32[]{:S(2)}) copy-start(bf16[256,512]{1,0:T(8,128)(2,1)} %param.9) | copy-start | bytes 786436
  155.8 20.0 %copy-start.15 = (f32[256]{0:T(256)S(1)}, f32[256]{0:T(256)}, u32[]{:S(2)}) copy-start(f32[256]{0:T(256)} %copy-done.14) | copy-start | bytes 3076
  173.0 16.3 %collective-permute-start.14 = (bf16[512,512]{1,0:T(8,128)(2,1)S(1)}, bf16[512,512]{1,0:T(8,128)(2,1)S(1)}, u32[]{:S(2)}, u32[]{:S(2)}) collective-permute-start(bf16[512,512]{1,0:T(8,128)(2,1)S(1)} %dynamic-slice_convert_fusion), channel_id=1, source_target_pairs={{0,1},{1,0},{2,3},{3,2},{4,5},{5,4},{6,7},{7,6},{8,9},{9,8},{10,11... | collective-permute-start | bytes 1572872 | tf_op jit(solution)/shard_map/ppermute | solution.py:125
  176.6 2.2 copy-start.1
  178.8 10.7 %copy-start.7 = (f32[512,512]{1,0:T(8,128)S(1)}, f32[512,512]{1,0:T(8,128)}, u32[]{:S(2)}) copy-start(f32[512,512]{1,0:T(8,128)} %param.14) | copy-start | bytes 3145732
  178.8 10.7 %copy-start.8 = (f32[1,512,512]{2,1,0:T(8,128)S(1)}, f32[1,512,512]{2,1,0:T(8,128)}, u32[]{:S(2)}) copy-start(f32[1,512,512]{2,1,0:T(8,128)} %param.11) | copy-start | bytes 3145732
  178.8 10.7 %copy-start.12 = (bf16[1,512,512]{2,1,0:T(8,128)(2,1)S(1)}, bf16[1,512,512]{2,1,0:T(8,128)(2,1)}, u32[]{:S(2)}) copy-start(bf16[1,512,512]{2,1,0:T(8,128)(2,1)} %param.13) | copy-start | bytes 1572868
  178.8 10.7 %copy-start.13 = (bf16[1,512,512]{2,1,0:T(8,128)(2,1)S(1)}, bf16[1,512,512]{2,1,0:T(8,128)(2,1)}, u32[]{:S(2)}) copy-start(bf16[1,512,512]{2,1,0:T(8,128)(2,1)} %param.12) | copy-start | bytes 1572868
  189.5 31.8 %copy-start.9 = (f32[512,512]{1,0:T(8,128)S(1)}, f32[512,512]{1,0:T(8,128)}, u32[]{:S(2)}) copy-start(f32[512,512]{1,0:T(8,128)} %param.15) | copy-start | bytes 3145732
Sparse Core Ops, SparseCore 0:
  11.2 161.7 all-gather.1
